TPU v7x, 32 devices: a whole 2x2x4 slice. The times are simulated.
32 devices in a mesh: grp: 2 (over y), tm: 4 (over z), freq: 4 (over x, core).
Axes of the slice: x: 2, y: 2, z: 4, core: 2. Of those that a mesh axis runs over, the one named last changes fastest.
Arguments:
- visibilities: bfloat16 [2, 132, 64, 1536], P(None, 'grp', 'tm', 'freq'), parts along dimension 1, may hold values from -6 to 6
- class_ids: int32 [132], P('grp'), parts along dimension 0, may hold values from 0 to 3, as said below
- class_counts: int32 [8], P('grp'), parts along dimension 0, may hold values from 1 to 32, as said below
- tap_windows: int32 [8], P('grp'), parts along dimension 0, may hold values from 1 to 4, as said below
- fringe_taps: float32 [2, 8, 9], P(None, 'grp'), parts along dimension 1, may hold values from -2.4 to 2.4
- flag_mask: int32 [64, 1536], P('freq'), may hold values 0 or 1
- filter_panels: bfloat16 [8, 1536, 1536], P(('grp', 'tm'), 'freq'), parts along dimension 0
Outputs:
- cleaned: bfloat16 [2, 8, 32, 64, 1536], P(None, ('grp', 'tm'), None, 'freq'), parts along dimension 1
There are 2 independent parts, one for each index of `grp`. A program takes and returns all parts, laid end to end along the dimension named above; an argument that names none is the same for every part. Nothing has to cross between parts.
Inputs may be any that keep to these rules, and one draw needn't show every extreme that they name: Baselines are listed grouped by class in increasing order of class; class_ids[b] is the class of baseline b. class_counts[c] is the number of baselines whose class is c; some class has exactly 32 baselines. `tap_windows`: some class has a window of exactly 4.
All inputs are finite; a program needn't handle non-finite values. No bound on the sum of `flag_mask` on one device may be relied on, other than what follows from the above.
Results may differ from a plain program's by a relative error of at most 0.0049.
Values may be sent and summed in bfloat16 or wider, within the bound.
No kernel may reach another device: no remote copies, remote signals or barrier semaphores. Data moves between devices by JAX's collectives and lax.ppermute only.
A program may use at most 128 MiB of HBM per device.

v0:
```python
import jax
import jax.numpy as jnp
from jax import lax
from jax.sharding import PartitionSpec as P

SLOTS = 32
REACH = 4


def extended(cells, sides, width):
    for axis, dim in sides:
        count = lax.axis_size(axis)
        ends = count - 1
        head = lax.slice_in_dim(cells, 0, width, axis=dim)
        tail = lax.slice_in_dim(cells, cells.shape[dim] - width, cells.shape[dim], axis=dim)
        cells = jnp.concatenate(
            [
                lax.ppermute(tail, axis, [(i, (i + 1) % count) for i in range(ends)]),
                cells,
                lax.ppermute(head, axis, [((i + 1) % count, i) for i in range(ends)]),
            ],
            axis=dim,
        )
    return cells


def masked_taps(fringe_taps, tap_windows):
    offsets = jnp.abs(jnp.arange(2 * REACH + 1, dtype=jnp.int32) - REACH)
    keep = (offsets[None, :] <= tap_windows[:, None]).astype(jnp.float32)
    return fringe_taps * keep[None, :, :]


def convolve(padded, row_taps, length):
    real_part = jnp.zeros(padded.shape[1:2] + (length,) + padded.shape[3:], jnp.float32)
    imag_part = jnp.zeros_like(real_part)
    for offset in range(2 * REACH + 1):
        shifted = lax.slice_in_dim(padded, 2 * REACH - offset, 2 * REACH - offset + length, axis=2)
        tap_real = row_taps[0, :, offset][:, None, None]
        tap_imag = row_taps[1, :, offset][:, None, None]
        real_part = real_part + tap_real * shifted[0] - tap_imag * shifted[1]
        imag_part = imag_part + tap_real * shifted[1] + tap_imag * shifted[0]
    return jnp.stack([real_part, imag_part]).astype(jnp.bfloat16)


def to_slots(per_baseline, class_counts):
    class_starts = jnp.cumsum(class_counts) - class_counts
    slot_positions = jnp.arange(SLOTS, dtype=jnp.int32)
    input_visibility = jnp.clip(
        class_starts[:, None] + slot_positions[None, :], 0, per_baseline.shape[1] - 1
    )
    live_slot = slot_positions[None, :] < class_counts[:, None]
    gathered = jnp.take(per_baseline, input_visibility.reshape(-1), axis=1)
    gathered = gathered.reshape(per_baseline.shape[:1] + live_slot.shape + per_baseline.shape[2:])
    return jnp.where(live_slot[None, :, :, None, None], gathered, jnp.zeros((), per_baseline.dtype))


def shards(
    visibilities, class_ids, class_counts, tap_windows, fringe_taps, flag_mask, filter_panels
):
    taps_kept = masked_taps(fringe_taps, tap_windows)
    padded = extended(visibilities, (("tm", 2),), REACH)
    class_iota = jnp.arange(taps_kept.shape[1], dtype=jnp.int32)
    one_hot = (class_ids[:, None] == class_iota[None, :]).astype(jnp.float32)
    row_taps = jnp.einsum("bc,rck->rbk", one_hot, taps_kept, precision=lax.Precision.HIGHEST)
    filtered = convolve(padded, row_taps, visibilities.shape[2])
    slotted = to_slots(filtered, class_counts)
    local_block = lax.all_to_all(
        lax.all_to_all(slotted, "tm", split_axis=1, concat_axis=3, tiled=True),
        "freq",
        split_axis=3,
        concat_axis=4,
        tiled=True,
    )
    flag_gate = flag_mask.astype(jnp.bfloat16)
    weighted = local_block * flag_gate
    dayenu_fit = jnp.einsum(
        "rcstj,cij->rcsti",
        weighted,
        lax.all_gather(filter_panels, "freq", axis=1, tiled=True),
        preferred_element_type=jnp.float32,
    )
    return (local_block.astype(jnp.float32) - dayenu_fit).astype(jnp.bfloat16)


def solution(mesh):
    return jax.shard_map(
        shards,
        mesh=mesh,
        in_specs=(
            P(None, "grp", "tm", "freq"),
            P("grp"),
            P("grp"),
            P("grp"),
            P(None, "grp", None),
            P("freq", None),
            P(("grp", "tm"), "freq", None),
        ),
        out_specs=P(None, ("grp", "tm"), None, "freq", None),
        check_vma=False,
    )
```

profile of v0, /device:TPU:0, one launch (start us, length us, event | category | flops | bytes accessed | tf_op | source)
XLA Modules:
  0.0 189.7 jit_solution(7154030668723489211)
XLA Ops:
  6.5 0.0 copy-start
  6.5 0.0 copy-start.4
  6.5 0.0 copy-start.5
  6.5 0.0 copy-start.2
  6.5 0.0 copy-start.3
  6.5 1.8 fusion.57
  8.4 1.3 collective-permute-start
  9.7 5.6 %collective-permute-start.1 = (bf16[2,66,4,384]{3,2,1,0:T(4,128)(2,1)S(1)}, bf16[2,66,4,384]{3,2,1,0:T(4,128)(2,1)S(1)}, u32[]{:S(2)}, u32[]{:S(2)}) collective-permute-start(bf16[2,66,4,384]{3,2,1,0:T(4,128)(2,1)S(1)} %get-tuple-element.7), channel_id=1, source_target_pairs={{0,4},{4,8},{8,12},{1,5},{5,9},{9,13},{2,6},{6,10},{10,14},{3,7},{... | collective-permute-start | bytes 1216520 | tf_op jit(solution)/shard_map/ppermute | solution.py:18
  15.3 0.0 copy-done.4
  15.3 0.2 reduce-window.9
  15.5 0.1 add_clamp_fusion
  15.6 0.1 iota_compare_fusion.1
  15.7 0.1 min.12
  15.7 0.0 copy-done.5
  15.7 0.1 compare_convert_fusion
  15.8 0.0 copy-done.2
  15.8 0.0 copy-done.3
  15.8 0.2 convolution_bitcast_fusion
  16.0 0.0 copy-done
  16.0 0.2 constant_dynamic-update-slice_fusion.1
  16.2 6.5 %collective-permute-done = bf16[2,66,4,384]{3,2,1,0:T(4,128)(2,1)S(1)} collective-permute-done((bf16[2,66,4,384]{3,2,1,0:T(4,128)(2,1)S(1)}, bf16[2,66,4,384]{3,2,1,0:T(4,128)(2,1)S(1)}, u32[]{:S(2)}, u32[]{:S(2)}) %collective-permute-start) | collective-permute-done | bytes 405536 | tf_op jit(solution)/shard_map/ppermute | solution.py:20
  22.7 0.3 constant_dynamic-update-slice_fusion
  23.0 0.9 collective-permute-done.1
  23.9 5.1 %fusion.43 = bf16[1,66,16,384]{3,2,1,0:T(8,128)(2,1)S(1)} fusion(f32[66]{0:T(128)S(1)} %get-tuple-element.10, f32[66]{0:T(128)S(1)} %get-tuple-element.11, f32[66]{0:T(128)S(1)} %get-tuple-element.12, f32[66]{0:T(128)S(1)} %get-tuple-element.13, f32[66]{0:T(128)S(1)} %get-tuple-element.14, f32[66]{0:T(128)S(1)} %get-tuple-element.15, ...), kind=kLoop, calls=%fused_computation.94 | loop fusion | flops 31629312 | bytes 10957824 | tf_op jit(solution)/shard_map/convert.1
  29.0 5.2 %fusion.42 = bf16[1,66,16,384]{3,2,1,0:T(8,128)(2,1)S(1)} fusion(f32[66]{0:T(128)S(1)} %get-tuple-element.10, f32[66]{0:T(128)S(1)} %get-tuple-element.11, f32[66]{0:T(128)S(1)} %get-tuple-element.12, f32[66]{0:T(128)S(1)} %get-tuple-element.13, f32[66]{0:T(128)S(1)} %get-tuple-element.14, f32[66]{0:T(128)S(1)} %get-tuple-element.15, ...), kind=kLoop, calls=%fused_computation.93 | loop fusion | flops 31629312 | bytes 10957824 | tf_op jit(solution)/shard_map/convert.2
  34.3 0.2 pad_maximum_fusion
  34.5 2.7 %gather_fusion = bf16[128,2,16,384]{3,2,1,0:T(8,128)(2,1)} fusion(bf16[2,66,16,384]{3,2,1,0:T(8,128)(2,1)S(1)} %pad_maximum_fusion, s32[1024]{0:T(1024)S(1)} %pad_clamp_fusion), kind=kCustom, calls=%fused_computation | custom fusion | bytes 6291968 | tf_op jit(solution)/shard_map/jit(_take)/gather | solution.py:52
  37.1 2.2 %copy.24 = bf16[2,128,16,384]{3,2,1,0:T(8,128)(2,1)S(1)} copy(bf16[2,128,16,384]{3,2,0,1:T(8,128)(2,1)} %bitcast.89) | data formatting | bytes 6291456 | tf_op jit(solution)/shard_map/jit(_take)/gather | solution.py:52
  39.3 0.7 select_select_fusion
  40.1 2.0 %copy.25 = bf16[2,4,32,16,384]{4,3,2,0,1:T(8,128)(2,1)} copy(bf16[2,4,32,16,384]{4,3,2,1,0:T(8,128)(2,1)S(1)} %select_select_fusion) | data formatting | bytes 6291456 | tf_op jit(solution)/shard_map/jit(_where)/select_n | solution.py:54
  42.0 6.0 %all-to-all-start = ((bf16[2,4,32,16,384]{4,3,2,0,1:T(8,128)(2,1)}), bf16[2,4,32,16,384]{4,3,2,0,1:T(8,128)(2,1)S(1)}, u32[]{:S(2)}, u32[]{:S(2)}) async-start(bf16[2,4,32,16,384]{4,3,2,0,1:T(8,128)(2,1)} %copy.25), calls=%async_computation | async-start | bytes 6291456 | tf_op jit(solution)/shard_map/all_to_all | solution.py:68
  48.0 0.0 all-gather.2.cloned.1.call-start
  48.0 0.7 all-gather.2.cloned.1.call-update
  48.7 68.8 %all-to-all-done = bf16[2,4,32,16,384]{4,3,2,0,1:T(8,128)(2,1)S(1)} async-done(((bf16[2,4,32,16,384]{4,3,2,0,1:T(8,128)(2,1)}), bf16[2,4,32,16,384]{4,3,2,0,1:T(8,128)(2,1)S(1)}, u32[]{:S(2)}, u32[]{:S(2)}) %all-to-all-start) | async-done | bytes 3145760 | tf_op jit(solution)/shard_map/all_to_all | solution.py:68
  117.5 0.6 copy.26
  118.1 3.5 %copy.27 = bf16[2,1,32,64,384]{4,2,0,1,3:T(8,128)(2,1)} copy(bf16[2,1,32,64,384]{4,3,2,0,1:T(8,128)(2,1)S(1)} %bitcast.90) | data formatting | bytes 6291456 | tf_op jit(solution)/shard_map/all_to_all | solution.py:68
  121.6 0.0 copy-start.1
  121.6 4.0 %all-to-all-start.1 = ((bf16[2,1,32,64,384]{4,2,0,1,3:T(8,128)(2,1)}), bf16[2,1,32,64,384]{4,2,0,1,3:T(8,128)(2,1)S(1)}, u32[]{:S(2)}, u32[]{:S(2)}) async-start(bf16[2,1,32,64,384]{4,2,0,1,3:T(8,128)(2,1)} %copy.27), calls=%async_computation.1 | async-start | bytes 6291456 | tf_op jit(solution)/shard_map/all_to_all | solution.py:67
  125.7 0.0 copy-done.1
  125.7 36.6 %all-to-all-done.1 = bf16[2,1,32,64,384]{4,2,0,1,3:T(8,128)(2,1)S(1)} async-done(((bf16[2,1,32,64,384]{4,2,0,1,3:T(8,128)(2,1)}), bf16[2,1,32,64,384]{4,2,0,1,3:T(8,128)(2,1)S(1)}, u32[]{:S(2)}, u32[]{:S(2)}) %all-to-all-start.1) | async-done | bytes 3145760 | tf_op jit(solution)/shard_map/all_to_all | solution.py:67
  162.3 1.8 copy.28
  164.2 0.7 broadcast_multiply_fusion
  164.9 3.5 %copy.35 = f32[1,2,32,4,2,8,384]{6,5,3,4,2,1,0:T(8,128)} copy(f32[1,2,32,4,2,8,384]{6,5,4,3,2,1,0:T(8,128)S(1)} %get-tuple-element.6) | data formatting | bytes 12582912 | tf_op jit(solution)/shard_map/convert_element_type | solution.py:82
  168.3 1.6 copy.31
  170.0 2.7 %mul.425 = bf16[2,32,16,1536]{3,2,1,0:T(8,128)(2,1)} reshape(bf16[2,1,32,16,4,384]{5,4,3,2,0,1:T(4,128)(2,1)S(1)} %copy.31) | data formatting | bytes 6291456 | tf_op jit(solution)/shard_map/mul | solution.py:75
  172.7 0.0 all-gather.2.cloned.1.call-done
  172.7 10.2 %fusion.5 = bf16[2,1,32,16,1536]{4,3,2,1,0:T(8,128)(2,1)} fusion(f32[2,1,32,16,1536]{4,3,2,0,1:T(8,128)} %bitcast.93, bf16[2,32,16,1536]{3,2,1,0:T(8,128)(2,1)} %mul.425, bf16[1,1536,1536]{2,1,0:T(8,128)(2,1)} %all-gather.2.cloned.1.call-done), kind=kOutput, calls=%fused_computation.13 | convolution fusion | flops 4834983936 | bytes 17301504 | tf_op jit(solution)/shard_map/rcstj,cij->rcsti/dot_general | solution.py:76
  (7 shorter events, 0.1 us)
Async XLA Ops:
  6.5 9.5 %copy-start = (bf16[2,66,16,384]{3,2,1,0:T(8,128)(2,1)S(1)}, bf16[2,66,16,384]{3,2,1,0:T(8,128)(2,1)}, u32[]{:S(2)}) copy-start(bf16[2,66,16,384]{3,2,1,0:T(8,128)(2,1)} %param.7) | copy-start | bytes 4866052
  6.5 8.8 %copy-start.4 = (s32[4]{0:T(128)S(1)}, s32[4]{0:T(128)}, u32[]{:S(2)}) copy-start(s32[4]{0:T(128)} %param.9) | copy-start | bytes 52
  6.5 9.2 %copy-start.5 = (s32[4]{0:T(128)S(1)}, s32[4]{0:T(128)}, u32[]{:S(2)}) copy-start(s32[4]{0:T(128)} %param.10) | copy-start | bytes 52
  6.5 9.3 %copy-start.2 = (f32[2,4,9]{2,1,0:T(4,128)S(1)}, f32[2,4,9]{2,1,0:T(4,128)}, u32[]{:S(2)}) copy-start(f32[2,4,9]{2,1,0:T(4,128)} %param.11) | copy-start | bytes 868
  6.5 9.3 %copy-start.3 = (s32[66]{0:T(128)S(1)}, s32[66]{0:T(128)}, u32[]{:S(2)}) copy-start(s32[66]{0:T(128)} %param.8) | copy-start | bytes 796
  8.4 14.3 %collective-permute-start = (bf16[2,66,4,384]{3,2,1,0:T(4,128)(2,1)S(1)}, bf16[2,66,4,384]{3,2,1,0:T(4,128)(2,1)S(1)}, u32[]{:S(2)}, u32[]{:S(2)}) collective-permute-start(bf16[2,66,4,384]{3,2,1,0:T(4,128)(2,1)S(1)} %get-tuple-element.8), channel_id=1, source_target_pairs={{4,0},{8,4},{12,8},{5,1},{9,5},{13,9},{6,2},{10,6},{14,10},{7,3},{... | collective-permute-start | bytes 1216520 | tf_op jit(solution)/shard_map/ppermute | solution.py:20
  9.7 14.2 %collective-permute-start.1 = (bf16[2,66,4,384]{3,2,1,0:T(4,128)(2,1)S(1)}, bf16[2,66,4,384]{3,2,1,0:T(4,128)(2,1)S(1)}, u32[]{:S(2)}, u32[]{:S(2)}) collective-permute-start(bf16[2,66,4,384]{3,2,1,0:T(4,128)(2,1)S(1)} %get-tuple-element.7), channel_id=1, source_target_pairs={{0,4},{4,8},{8,12},{1,5},{5,9},{9,13},{2,6},{6,10},{10,14},{3,7},{... | collective-permute-start | bytes 1216520 | tf_op jit(solution)/shard_map/ppermute | solution.py:18
  42.0 75.5 %all-to-all-start = ((bf16[2,4,32,16,384]{4,3,2,0,1:T(8,128)(2,1)}), bf16[2,4,32,16,384]{4,3,2,0,1:T(8,128)(2,1)S(1)}, u32[]{:S(2)}, u32[]{:S(2)}) async-start(bf16[2,4,32,16,384]{4,3,2,0,1:T(8,128)(2,1)} %copy.25), calls=%async_computation | async-start | bytes 6291456 | tf_op jit(solution)/shard_map/all_to_all | solution.py:68
  48.0 124.7 %all-gather.2.cloned.1.call-start = ((), (), s32[]{:S(2)}) async-start(), calls=%async_computation.2 | async-start | bytes 5898240 | tf_op jit(solution)/shard_map/all_gather | solution.py:79
  121.6 4.0 %copy-start.1 = (s32[16,1536]{1,0:T(8,128)S(1)}, s32[16,1536]{1,0:T(8,128)}, u32[]{:S(2)}) copy-start(s32[16,1536]{1,0:T(8,128)} %param.12) | copy-start | bytes 294916
  121.6 40.7 %all-to-all-start.1 = ((bf16[2,1,32,64,384]{4,2,0,1,3:T(8,128)(2,1)}), bf16[2,1,32,64,384]{4,2,0,1,3:T(8,128)(2,1)S(1)}, u32[]{:S(2)}, u32[]{:S(2)}) async-start(bf16[2,1,32,64,384]{4,2,0,1,3:T(8,128)(2,1)} %copy.27), calls=%async_computation.1 | async-start | bytes 6291456 | tf_op jit(solution)/shard_map/all_to_all | solution.py:67
Sparse Core Ops, SparseCore 0:
  50.4 38.8 all-gather.1
where the time goes:
time: 190 us
  waiting for transfers between devices  114 us (60%)
  local copies, waits for them, and re-layouts  23 us (12%)
  starting transfers between devices  16.9 us (9%)
  between operations  13.6 us (7%)
  other arithmetic  12.4 us (7%)
  matrix products  10.4 us (5%)
    all_to_all x1, waiting for transfers between devices, shards(): lax.all_to_all(slotted, 'tm', split_axis=1, concat_axis=3, tiled=True)  68.8 us
    all_to_all x1, waiting for transfers between devices, shards(): lax.all_to_all(lax.all_to_all(slotted, 'tm', split_axis=1, concat_axis=3,...  36.6 us
    another operation x3, other arithmetic  10.5 us
    dot_general x1, matrix products, shards(): jnp.einsum('rcstj,cij->rcsti', weighted, lax.all_gather(filter_panels, 'f...  10.2 us
    ppermute x1, waiting for transfers between devices, extended(): lax.ppermute(head, axis, [((i + 1) % count, i) for i in range(ends)])  6.46 us
    all_to_all x1, starting transfers between devices, shards(): lax.all_to_all(slotted, 'tm', split_axis=1, concat_axis=3, tiled=True)  5.95 us
    ppermute x1, starting transfers between devices, extended(): lax.ppermute(tail, axis, [(i, (i + 1) % count) for i in range(ends)])  5.61 us
    gather x2, local copies, waits for them, and re-layouts, to_slots(): gathered = jnp.take(per_baseline, input_visibility.reshape(-1), axis=1)  4.87 us
  transfers between devices with their start and end apart: 5, of which 4 were waited for; matrix products, arithmetic and copies ran while one was open for 8% of the time, Pallas kernels for 0%

commit v1 on v0

--- a/solution.py
+++ b/solution.py
@@ -30,13 +30,14 @@
     return fringe_taps * keep[None, :, :]
 
 
-def convolve(padded, row_taps, length):
-    real_part = jnp.zeros(padded.shape[1:2] + (length,) + padded.shape[3:], jnp.float32)
+def convolve(rows, slot_taps, length):
+    real_part = jnp.zeros(rows.shape[1:2] + (length,) + rows.shape[3:], jnp.float32)
     imag_part = jnp.zeros_like(real_part)
     for offset in range(2 * REACH + 1):
-        shifted = lax.slice_in_dim(padded, 2 * REACH - offset, 2 * REACH - offset + length, axis=2)
-        tap_real = row_taps[0, :, offset][:, None, None]
-        tap_imag = row_taps[1, :, offset][:, None, None]
+        shifted = lax.slice_in_dim(rows, 2 * REACH - offset, 2 * REACH - offset + length, axis=2)
+        shifted = shifted.astype(jnp.float32)
+        tap_real = slot_taps[0, :, offset][:, None, None]
+        tap_imag = slot_taps[1, :, offset][:, None, None]
         real_part = real_part + tap_real * shifted[0] - tap_imag * shifted[1]
         imag_part = imag_part + tap_real * shifted[1] + tap_imag * shifted[0]
     return jnp.stack([real_part, imag_part]).astype(jnp.bfloat16)
@@ -54,14 +55,12 @@
     return jnp.where(live_slot[None, :, :, None, None], gathered, jnp.zeros((), per_baseline.dtype))
 
 
-def shards(
+def two_stage(
     visibilities, class_ids, class_counts, tap_windows, fringe_taps, flag_mask, filter_panels
 ):
     taps_kept = masked_taps(fringe_taps, tap_windows)
     padded = extended(visibilities, (("tm", 2),), REACH)
-    class_iota = jnp.arange(taps_kept.shape[1], dtype=jnp.int32)
-    one_hot = (class_ids[:, None] == class_iota[None, :]).astype(jnp.float32)
-    row_taps = jnp.einsum("bc,rck->rbk", one_hot, taps_kept, precision=lax.Precision.HIGHEST)
+    row_taps = taps_kept[:, class_ids, :]
     filtered = convolve(padded, row_taps, visibilities.shape[2])
     slotted = to_slots(filtered, class_counts)
     local_block = lax.all_to_all(
@@ -71,8 +70,7 @@
         concat_axis=4,
         tiled=True,
     )
-    flag_gate = flag_mask.astype(jnp.bfloat16)
-    weighted = local_block * flag_gate
+    weighted = local_block * flag_mask.astype(jnp.bfloat16)
     dayenu_fit = jnp.einsum(
         "rcstj,cij->rcsti",
         weighted,
@@ -80,6 +78,72 @@
         preferred_element_type=jnp.float32,
     )
     return (local_block.astype(jnp.float32) - dayenu_fit).astype(jnp.bfloat16)
+
+
+def shards(
+    visibilities, class_ids, class_counts, tap_windows, fringe_taps, flag_mask, filter_panels
+):
+    nt = lax.axis_size("tm")
+    nf = lax.axis_size("freq")
+    if nt != nf:
+        return two_stage(
+            visibilities, class_ids, class_counts, tap_windows, fringe_taps, flag_mask,
+            filter_panels,
+        )
+    q = nt // nf
+    a = lax.axis_index("tm")
+    b = lax.axis_index("freq")
+    baselines = visibilities.shape[1]
+    t_in = visibilities.shape[2]
+    f_blk = visibilities.shape[3]
+    t_out = flag_mask.shape[0]
+    channels = flag_mask.shape[1]
+
+    taps_kept = masked_taps(fringe_taps, tap_windows)
+    class_starts = jnp.cumsum(class_counts) - class_counts
+    slot_positions = jnp.arange(SLOTS, dtype=jnp.int32)
+
+    padded = extended(visibilities, (("tm", 2),), REACH)
+    padded = jnp.pad(padded, ((0, 0), (0, SLOTS), (0, 0), (0, 0)))
+
+    panel = lax.all_gather(filter_panels[0], "freq", axis=0, tiled=True)
+    panel = panel.reshape(channels, nf, f_blk)
+
+    c_own = a
+    u_src = (a % q) * nf + b
+    fit = jnp.zeros((2, SLOTS, t_out, channels), jnp.float32)
+    slotted = jnp.zeros((2, SLOTS, t_out, channels), jnp.bfloat16)
+    for r in range(nt):
+        c_send = (u_src + r) % nt
+        start = class_starts[c_send]
+        rows = lax.dynamic_slice_in_dim(padded, start, SLOTS, axis=1)
+        row_ids = jnp.clip(start + slot_positions, 0, baselines - 1)
+        slot_taps = taps_kept[:, class_ids[row_ids], :]
+        chunk = convolve(rows, slot_taps, t_in)
+        live = slot_positions < class_counts[c_send]
+        chunk = jnp.where(live[None, :, None, None], chunk, jnp.zeros((), chunk.dtype))
+        perm = []
+        for sa in range(nt):
+            for sb in range(nf):
+                u = (sa % q) * nf + sb
+                dc = (u + r) % nt
+                perm.append((sa * nf + sb, dc * nf + sa // q))
+        got = lax.ppermute(chunk, ("tm", "freq"), perm)
+        u_dst = (c_own - r) % nt
+        t_sub = u_dst // nf
+        b_src = u_dst % nf
+        gate = lax.dynamic_slice(flag_mask, (t_sub * t_in, b_src * f_blk), (t_in, f_blk))
+        weighted = got * gate.astype(jnp.bfloat16)
+        cols = lax.dynamic_index_in_dim(panel, b_src, axis=1, keepdims=False)
+        part = jnp.einsum("rstj,ij->rsti", weighted, cols, preferred_element_type=jnp.float32)
+        if q == 1:
+            fit = fit + part
+        else:
+            prev = lax.dynamic_slice_in_dim(fit, t_sub * t_in, t_in, axis=2)
+            fit = lax.dynamic_update_slice_in_dim(fit, prev + part, t_sub * t_in, axis=2)
+        slotted = lax.dynamic_update_slice(slotted, got, (0, 0, t_sub * t_in, b_src * f_blk))
+    cleaned = (slotted.astype(jnp.float32) - fit).astype(jnp.bfloat16)
+    return cleaned[:, None]
 
 
 def solution(mesh):

time: 190 us -> 203 us (1.068)
  the two profiles are of different devices: /device:TPU:0 before, /device:TPU:14 now
where the time goes in v1:
time: 203 us; the launch traced here: 202 us
  local copies, waits for them, and re-layouts  57.6 us (28%)
  waiting for transfers between devices  50.8 us (25%)
  other arithmetic  46 us (23%)
  between operations  22.1 us (11%)
  matrix products  13.7 us (7%)
  starting transfers between devices  12.3 us (6%)
    ppermute x4, waiting for transfers between devices, shards(): got = lax.ppermute(chunk, ('tm', 'freq'), perm)  50.8 us
    convert_element_type x1, other arithmetic, convolve(): shifted = shifted.astype(jnp.float32)  17.1 us
    dynamic_slice x1, local copies, waits for them, and re-layouts, shards(): cols = lax.dynamic_index_in_dim(panel, b_src, axis=1, keepdims=False)  16.5 us
    another operation x9, other arithmetic  15.6 us
    dot_general x4, matrix products, shards(): jnp.einsum('rstj,ij->rsti', weighted, cols, preferred_element_type=jnp.fl...  13.7 us
    reshape x1, local copies, waits for them, and re-layouts, shards(): panel = panel.reshape(channels, nf, f_blk)  9.1 us
    slice x4, local copies, waits for them, and re-layouts, convolve(): tap_real = slot_taps[0, :, offset][:, None, None]  8.99 us
    unnamed x122, local copies, waits for them, and re-layouts  7.64 us
  transfers between devices with their start and end apart: 7, of which 4 were waited for; matrix products, arithmetic and copies ran while one was open for 34% of the time, Pallas kernels for 0%

profile of v1, /device:TPU:14, one launch (start us, length us, event | category | flops | bytes accessed | tf_op | source)
XLA Modules:
  0.0 202.4 jit_solution(16854114499550037249)
XLA Ops:
  6.6 1.7 fusion.26
  8.3 3.5 %collective-permute-start = (bf16[2,66,4,384]{3,2,1,0:T(4,128)(2,1)S(1)}, bf16[2,66,4,384]{3,2,1,0:T(4,128)(2,1)S(1)}, u32[]{:S(2)}, u32[]{:S(2)}) collective-permute-start(bf16[2,66,4,384]{3,2,1,0:T(4,128)(2,1)S(1)} %get-tuple-element.117), channel_id=1, source_target_pairs={{0,4},{4,8},{8,12},{1,5},{5,9},{9,13},{2,6},{6,10},{10,14},{3,7},{... | collective-permute-start | bytes 1216520 | tf_op jit(solution)/shard_map/ppermute | solution.py:18
  11.8 2.4 %collective-permute-start.1 = (bf16[2,66,4,384]{3,2,1,0:T(4,128)(2,1)S(1)}, bf16[2,66,4,384]{3,2,1,0:T(4,128)(2,1)S(1)}, u32[]{:S(2)}, u32[]{:S(2)}) collective-permute-start(bf16[2,66,4,384]{3,2,1,0:T(4,128)(2,1)S(1)} %get-tuple-element.118), channel_id=1, source_target_pairs={{4,0},{8,4},{12,8},{5,1},{9,5},{13,9},{6,2},{10,6},{14,10},{7,3},{... | collective-permute-start | bytes 1216520 | tf_op jit(solution)/shard_map/ppermute | solution.py:20
  20.3 1.3 fusion.22
  22.2 1.3 fusion.18
  23.5 0.7 gather_fusion.6
  24.9 2.1 %slice_reduce_fusion.17 = (f32[32]{0:T(128)S(1)}, f32[32]{0:T(128)S(1)}, f32[32]{0:T(128)S(1)}, f32[32]{0:T(128)S(1)}, f32[32]{0:T(128)S(1)}, /*index=5*/f32[32]...) fusion(f32[2,32,9]{2,0,1:T(2,128)S(1)} %bitcast.75), kind=kLoop, calls=%fused_computation.101 | loop fusion | bytes 4608 | tf_op jit(solution)/shard_map/slice | solution.py:39
  27.0 1.0 iota_compare_fusion.1
  28.1 0.7 gather_fusion
  29.4 2.1 %slice_reduce_fusion.71 = (f32[32]{0:T(128)S(1)}, f32[32]{0:T(128)S(1)}, f32[32]{0:T(128)S(1)}, f32[32]{0:T(128)S(1)}, f32[32]{0:T(128)S(1)}, /*index=5*/f32[32]...) fusion(f32[2,32,9]{2,0,1:T(2,128)S(1)} %bitcast.76), kind=kLoop, calls=%fused_computation.155 | loop fusion | bytes 4608 | tf_op jit(solution)/shard_map/slice | solution.py:39
  31.5 1.1 iota_compare_fusion.4
  34.0 1.1 iota_compare_fusion.3
  39.0 1.1 iota_compare_fusion.2
  40.1 2.7 %slice_reduce_fusion.53 = (f32[32]{0:T(128)S(1)}, f32[32]{0:T(128)S(1)}, f32[32]{0:T(128)S(1)}, f32[32]{0:T(128)S(1)}, f32[32]{0:T(128)S(1)}, /*index=5*/f32[32]...) fusion(f32[2,32,9]{2,0,1:T(2,128)S(1)} %bitcast.74), kind=kLoop, calls=%fused_computation.137 | loop fusion | bytes 4608 | tf_op jit(solution)/shard_map/slice | solution.py:39
  42.8 2.1 %slice_reduce_fusion.35 = (f32[32]{0:T(128)S(1)}, f32[32]{0:T(128)S(1)}, f32[32]{0:T(128)S(1)}, f32[32]{0:T(128)S(1)}, f32[32]{0:T(128)S(1)}, /*index=5*/f32[32]...) fusion(f32[2,32,9]{2,0,1:T(2,128)S(1)} %bitcast.73), kind=kLoop, calls=%fused_computation.119 | loop fusion | bytes 4608 | tf_op jit(solution)/shard_map/slice | solution.py:39
  44.9 1.8 fusion.4
  46.8 17.1 %dynamic-slice_convert_fusion.8 = (f32[2,32,16,384]{3,2,1,0:T(8,128)}, f32[2,32,16,384]{3,2,1,0:T(8,128)}, f32[2,32,16,384]{3,2,1,0:T(8,128)}, f32[2,32,16,384]{...) fusion(bf16[2,98,24,384]{3,2,1,0:T(8,128)(2,1)S(1)} %fusion.4, ...), kind=kLoop, calls=%fused_computation.32 | loop fusion | flops 14155776 | bytes 84934704 | tf_op jit(solution)/shard_map/convert_element_type | solution.py:38
  63.9 5.8 %subtract_convert_fusion.4 = bf16[1,32,16,384]{3,2,1,0:T(8,128)(2,1)S(1)} fusion(f32[2,32,16,384]{3,2,1,0:T(8,128)} %get-tuple-element.115, f32[2,32,16,384]{3,2,1,0:T(8,128)} %get-tuple-element.105, f32[2,32,16,384]{3,2,1,0:T(8,128)} %get-tuple-element.106, f32[2,32,16,384]{3,2,1,0:T(8,128)} %get-tuple-element.107, ...), kind=kLoop, calls=%fused_computation.75 | loop fusion | flops 7077888 | bytes 14551296 | tf_op jit(solution)/shard_map/convert.6
  73.1 1.4 add_convert_fusion.3
  74.6 1.1 maximum_select_fusion
  75.7 2.6 %collective-permute-start.2 = (bf16[2,32,16,384]{3,2,1,0:T(8,128)(2,1)}, bf16[2,32,16,384]{3,2,1,0:T(8,128)(2,1)S(1)}, u32[]{:S(2)}, u32[]{:S(2)}) collective-permute-start(bf16[2,32,16,384]{3,2,1,0:T(8,128)(2,1)} %maximum_select_fusion), channel_id=1, source_target_pairs={{0,0},{1,4},{2,8},{3,12},{4,1},{5,5},{6,9},{7,13},{8,2},{9,6},{10,... | collective-permute-start | bytes 2359304 | tf_op jit(solution)/shard_map/ppermute | solution.py:131
  78.7 1.4 subtract_convert_fusion.3
  80.2 1.4 add_convert_fusion.2
  81.6 1.1 maximum_select_fusion.1
  82.7 1.8 collective-permute-start.3
  85.7 1.3 subtract_convert_fusion.1
  87.1 1.4 add_convert_fusion
  91.2 1.3 subtract_convert_fusion.2
  92.6 1.4 add_convert_fusion.1
  94.0 1.1 maximum_select_fusion.2
  95.1 1.1 collective-permute-start.4
  96.2 1.1 maximum_select_fusion.3
  97.3 1.0 collective-permute-start.5
  98.3 34.1 %collective-permute-done.2 = bf16[2,32,16,384]{3,2,1,0:T(8,128)(2,1)S(1)} collective-permute-done((bf16[2,32,16,384]{3,2,1,0:T(8,128)(2,1)}, bf16[2,32,16,384]{3,2,1,0:T(8,128)(2,1)S(1)}, u32[]{:S(2)}, u32[]{:S(2)}) %collective-permute-start.2) | collective-permute-done | bytes 786464 | tf_op jit(solution)/shard_map/ppermute | solution.py:131
  132.4 2.0 %broadcast_in_dim.55 = bf16[2,32,16,1536]{3,2,1,0:T(8,128)(2,1)} broadcast(bf16[]{:T(256)} %constant.134.clone.1), dimensions={} | broadcast | bytes 3145730 | tf_op jit(solution)/shard_map/broadcast_in_dim | solution.py:115
  134.4 1.0 constant_dynamic-update-slice_fusion.3
  135.4 13.3 %collective-permute-done.3 = bf16[2,32,16,384]{3,2,1,0:T(8,128)(2,1)} collective-permute-done((bf16[2,32,16,384]{3,2,1,0:T(8,128)(2,1)}, bf16[2,32,16,384]{3,2,1,0:T(8,128)(2,1)}, u32[]{:S(2)}, u32[]{:S(2)}) %collective-permute-start.3) | collective-permute-done | bytes 786464 | tf_op jit(solution)/shard_map/ppermute | solution.py:131
  148.6 2.1 %constant_dynamic-update-slice_fusion.2 = bf16[2,32,16,1536]{3,2,1,0:T(8,128)(2,1)} fusion(bf16[2,32,16,1536]{3,2,1,0:T(8,128)(2,1)} %constant_dynamic-update-slice_fusion.3, bf16[2,32,16,384]{3,2,1,0:T(8,128)(2,1)} %collective-permute-done.3, s32[]{:T(128)S(6)} %select_n.233), kind=kLoop, calls=%fused_computation.162 | loop fusion | bytes 1572868 | tf_op jit(solution)/shard_map/dynamic_update_slice | solution.py:144
  150.7 0.7 collective-permute-done.4
  151.5 1.0 constant_dynamic-update-slice_fusion.1
  152.5 2.7 %collective-permute-done.5 = bf16[2,32,16,384]{3,2,1,0:T(8,128)(2,1)S(1)} collective-permute-done((bf16[2,32,16,384]{3,2,1,0:T(8,128)(2,1)}, bf16[2,32,16,384]{3,2,1,0:T(8,128)(2,1)S(1)}, u32[]{:S(2)}, u32[]{:S(2)}) %collective-permute-start.5) | collective-permute-done | bytes 786464 | tf_op jit(solution)/shard_map/ppermute | solution.py:131
  155.2 1.0 constant_dynamic-update-slice_fusion
  156.2 9.1 %reshape.283 = bf16[1536,4,384]{2,1,0:T(4,128)(2,1)} reshape(bf16[1,1536,1536]{2,1,0:T(8,128)(2,1)} %all-gather.3.cloned.1.call-done) | data formatting | bytes 9437184 | tf_op jit(solution)/shard_map/reshape | solution.py:110
  165.3 16.5 %constant_dynamic-slice_fusion = (bf16[1536,1,384]{2,1,0:T(2,128)(2,1)}, bf16[1536,1,384]{2,1,0:T(2,128)(2,1)S(1)}, bf16[1536,1,384]{2,1,0:T(2,128)(2,1)S(1)}, bf16[1536,1,384]{2,1,0:T(2,128)(2,1)S(1)}) fusion(bf16[1536,4,384]{2,1,0:T(4,128)(2,1)} %reshape.283, s32[]{:T(128)S(6)} %select_n.255, s32[]{:T(128)S(6)} %select_n.254, s32[]{:T(128)S(6)} %select_n.253, ...), kind=kLoop, calls=%fused_computation.156 | loop fusion | bytes 9437200 | tf_op jit(solution)/shard_map/jit(dynamic_index_in_dim)/dynamic_slice | solution.py:137
  181.8 3.0 %fusion.8 = f32[2,32,16,1536]{3,2,1,0:T(8,128)S(1)} fusion(bf16[1536,1,384]{2,1,0:T(2,128)(2,1)S(1)} %get-tuple-element.79, bf16[2,32,16,384]{3,2,1,0:T(8,128)(2,1)} %collective-permute-done.3, bf16[16,384]{1,0:T(8,128)(2,1)S(1)} %get-tuple-element.120), kind=kOutput, calls=%fused_computation.21 | convolution fusion | flops 1208352768 | bytes 8269824 | tf_op jit(solution)/shard_map/rstj,ij->rsti/dot_general | solution.py:138
  184.8 1.8 fusion.9
  186.7 1.8 fusion.7
  188.5 7.0 %fusion.5 = bf16[2,1,32,16,1536]{4,3,2,1,0:T(8,128)(2,1)} fusion(f32[2,32,16,1536]{3,2,1,0:T(8,128)S(1)} %fusion.7, f32[2,32,16,1536]{3,2,1,0:T(8,128)S(1)} %fusion.9, f32[2,32,16,1536]{3,2,1,0:T(8,128)S(1)} %fusion.8, bf16[2,32,16,1536]{3,2,1,0:T(8,128)(2,1)} %constant_dynamic-update-slice_fusion, bf16[1536,1,384]{2,1,0:T(2,128)(2,1)} %get-tuple-element.77, ...), kind=kOutput, calls=%fused_computation.15 | convolution fusion | flops 1217789952 | bytes 27144192 | tf_op jit(solution)/shard_map/rstj,ij->rsti/dot_general | solution.py:138
  (153 shorter events, 13.1 us)
Async XLA Ops:
  6.5 17.0 %copy-start = (s32[66]{0:T(128)S(1)}, s32[66]{0:T(128)}, u32[]{:S(2)}) copy-start(s32[66]{0:T(128)} %param.8) | copy-start | bytes 796
  6.5 7.7 %copy-start.41 = (s32[4]{0:T(128)S(1)}, s32[4]{0:T(128)}, u32[]{:S(2)}) copy-start(s32[4]{0:T(128)} %param.9) | copy-start | bytes 52
  6.5 17.7 %copy-start.60 = (s32[4]{0:T(128)S(1)}, s32[4]{0:T(128)}, u32[]{:S(2)}) copy-start(s32[4]{0:T(128)} %param.10) | copy-start | bytes 52
  6.5 17.8 %copy-start.55 = (f32[2,4,9]{2,1,0:T(4,128)S(1)}, f32[2,4,9]{2,1,0:T(4,128)}, u32[]{:S(2)}) copy-start(f32[2,4,9]{2,1,0:T(4,128)} %param.11) | copy-start | bytes 868
  6.5 149.7 %all-gather.3.cloned.1.call-start = ((), (), s32[]{:S(2)}) async-start(), calls=%async_computation | async-start | bytes 5898240 | tf_op jit(solution)/shard_map/all_gather | solution.py:109
  8.3 36.6 %collective-permute-start = (bf16[2,66,4,384]{3,2,1,0:T(4,128)(2,1)S(1)}, bf16[2,66,4,384]{3,2,1,0:T(4,128)(2,1)S(1)}, u32[]{:S(2)}, u32[]{:S(2)}) collective-permute-start(bf16[2,66,4,384]{3,2,1,0:T(4,128)(2,1)S(1)} %get-tuple-element.117), channel_id=1, source_target_pairs={{0,4},{4,8},{8,12},{1,5},{5,9},{9,13},{2,6},{6,10},{10,14},{3,7},{... | collective-permute-start | bytes 1216520 | tf_op jit(solution)/shard_map/ppermute | solution.py:18
  11.8 33.1 %collective-permute-start.1 = (bf16[2,66,4,384]{3,2,1,0:T(4,128)(2,1)S(1)}, bf16[2,66,4,384]{3,2,1,0:T(4,128)(2,1)S(1)}, u32[]{:S(2)}, u32[]{:S(2)}) collective-permute-start(bf16[2,66,4,384]{3,2,1,0:T(4,128)(2,1)S(1)} %get-tuple-element.118), channel_id=1, source_target_pairs={{4,0},{8,4},{12,8},{5,1},{9,5},{13,9},{6,2},{10,6},{14,10},{7,3},{... | collective-permute-start | bytes 1216520 | tf_op jit(solution)/shard_map/ppermute | solution.py:20
  24.3 20.6 %copy-start.36 = (bf16[2,66,16,384]{3,2,1,0:T(8,128)(2,1)S(1)}, bf16[2,66,16,384]{3,2,1,0:T(8,128)(2,1)}, u32[]{:S(2)}) copy-start(bf16[2,66,16,384]{3,2,1,0:T(8,128)(2,1)} %param.7) | copy-start | bytes 4866052
  63.8 5.9 %copy-start.27 = (f32[2,32,16,384]{3,2,1,0:T(8,128)S(1)}, f32[2,32,16,384]{3,2,1,0:T(8,128)}, u32[]{:S(2)}) copy-start(f32[2,32,16,384]{3,2,1,0:T(8,128)} %get-tuple-element.105) | copy-start | bytes 4718596
  63.8 6.0 %copy-start.28 = (f32[2,32,16,384]{3,2,1,0:T(8,128)S(1)}, f32[2,32,16,384]{3,2,1,0:T(8,128)}, u32[]{:S(2)}) copy-start(f32[2,32,16,384]{3,2,1,0:T(8,128)} %get-tuple-element.106) | copy-start | bytes 4718596
  63.8 6.4 %copy-start.29 = (f32[2,32,16,384]{3,2,1,0:T(8,128)S(1)}, f32[2,32,16,384]{3,2,1,0:T(8,128)}, u32[]{:S(2)}) copy-start(f32[2,32,16,384]{3,2,1,0:T(8,128)} %get-tuple-element.107) | copy-start | bytes 4718596
  63.8 6.9 %copy-start.30 = (f32[2,32,16,384]{3,2,1,0:T(8,128)S(1)}, f32[2,32,16,384]{3,2,1,0:T(8,128)}, u32[]{:S(2)}) copy-start(f32[2,32,16,384]{3,2,1,0:T(8,128)} %get-tuple-element.108) | copy-start | bytes 4718596
  63.9 7.4 %copy-start.31 = (f32[2,32,16,384]{3,2,1,0:T(8,128)S(1)}, f32[2,32,16,384]{3,2,1,0:T(8,128)}, u32[]{:S(2)}) copy-start(f32[2,32,16,384]{3,2,1,0:T(8,128)} %get-tuple-element.109) | copy-start | bytes 4718596
  63.9 7.8 %copy-start.32 = (f32[2,32,16,384]{3,2,1,0:T(8,128)S(1)}, f32[2,32,16,384]{3,2,1,0:T(8,128)}, u32[]{:S(2)}) copy-start(f32[2,32,16,384]{3,2,1,0:T(8,128)} %get-tuple-element.110) | copy-start | bytes 4718596
  63.9 8.2 %copy-start.33 = (f32[2,32,16,384]{3,2,1,0:T(8,128)S(1)}, f32[2,32,16,384]{3,2,1,0:T(8,128)}, u32[]{:S(2)}) copy-start(f32[2,32,16,384]{3,2,1,0:T(8,128)} %get-tuple-element.111) | copy-start | bytes 4718596
  63.9 8.7 %copy-start.34 = (f32[2,32,16,384]{3,2,1,0:T(8,128)S(1)}, f32[2,32,16,384]{3,2,1,0:T(8,128)}, u32[]{:S(2)}) copy-start(f32[2,32,16,384]{3,2,1,0:T(8,128)} %get-tuple-element.112) | copy-start | bytes 4718596
  63.9 9.1 %copy-start.35 = (f32[2,32,16,384]{3,2,1,0:T(8,128)S(1)}, f32[2,32,16,384]{3,2,1,0:T(8,128)}, u32[]{:S(2)}) copy-start(f32[2,32,16,384]{3,2,1,0:T(8,128)} %get-tuple-element.115) | copy-start | bytes 4718596
  73.0 5.2 %copy-start.19 = (f32[2,32,16,384]{3,2,1,0:T(8,128)S(1)}, f32[2,32,16,384]{3,2,1,0:T(8,128)}, u32[]{:S(2)}) copy-start(f32[2,32,16,384]{3,2,1,0:T(8,128)} %get-tuple-element.98) | copy-start | bytes 4718596
  73.0 5.3 %copy-start.20 = (f32[2,32,16,384]{3,2,1,0:T(8,128)S(1)}, f32[2,32,16,384]{3,2,1,0:T(8,128)}, u32[]{:S(2)}) copy-start(f32[2,32,16,384]{3,2,1,0:T(8,128)} %get-tuple-element.99) | copy-start | bytes 4718596
  73.0 5.3 %copy-start.21 = (f32[2,32,16,384]{3,2,1,0:T(8,128)S(1)}, f32[2,32,16,384]{3,2,1,0:T(8,128)}, u32[]{:S(2)}) copy-start(f32[2,32,16,384]{3,2,1,0:T(8,128)} %get-tuple-element.100) | copy-start | bytes 4718596
  73.0 5.3 %copy-start.22 = (f32[2,32,16,384]{3,2,1,0:T(8,128)S(1)}, f32[2,32,16,384]{3,2,1,0:T(8,128)}, u32[]{:S(2)}) copy-start(f32[2,32,16,384]{3,2,1,0:T(8,128)} %get-tuple-element.101) | copy-start | bytes 4718596
  73.0 5.3 %copy-start.23 = (f32[2,32,16,384]{3,2,1,0:T(8,128)S(1)}, f32[2,32,16,384]{3,2,1,0:T(8,128)}, u32[]{:S(2)}) copy-start(f32[2,32,16,384]{3,2,1,0:T(8,128)} %get-tuple-element.102) | copy-start | bytes 4718596
  73.0 5.3 %copy-start.24 = (f32[2,32,16,384]{3,2,1,0:T(8,128)S(1)}, f32[2,32,16,384]{3,2,1,0:T(8,128)}, u32[]{:S(2)}) copy-start(f32[2,32,16,384]{3,2,1,0:T(8,128)} %get-tuple-element.103) | copy-start | bytes 4718596
  73.1 5.3 %copy-start.25 = (f32[2,32,16,384]{3,2,1,0:T(8,128)S(1)}, f32[2,32,16,384]{3,2,1,0:T(8,128)}, u32[]{:S(2)}) copy-start(f32[2,32,16,384]{3,2,1,0:T(8,128)} %get-tuple-element.104) | copy-start | bytes 4718596
  73.1 5.3 %copy-start.26 = (f32[2,32,16,384]{3,2,1,0:T(8,128)S(1)}, f32[2,32,16,384]{3,2,1,0:T(8,128)}, u32[]{:S(2)}) copy-start(f32[2,32,16,384]{3,2,1,0:T(8,128)} %get-tuple-element.114) | copy-start | bytes 4718596
  74.5 4.1 %copy-start.18 = (f32[2,32,16,384]{3,2,1,0:T(8,128)S(1)}, f32[2,32,16,384]{3,2,1,0:T(8,128)}, u32[]{:S(2)}) copy-start(f32[2,32,16,384]{3,2,1,0:T(8,128)} %get-tuple-element.97) | copy-start | bytes 4718596
  74.5 4.1 %copy-start.42 = (f32[32]{0:T(128)S(1)}, f32[32]{0:T(128)}, u32[]{:S(2)}) copy-start(f32[32]{0:T(128)} %get-tuple-element.28) | copy-start | bytes 388
  74.5 4.1 %copy-start.43 = (f32[32]{0:T(128)S(1)}, f32[32]{0:T(128)}, u32[]{:S(2)}) copy-start(f32[32]{0:T(128)} %get-tuple-element.29) | copy-start | bytes 388
  74.5 4.1 %copy-start.44 = (f32[32]{0:T(128)S(1)}, f32[32]{0:T(128)}, u32[]{:S(2)}) copy-start(f32[32]{0:T(128)} %get-tuple-element.30) | copy-start | bytes 388
  74.5 4.1 %copy-start.45 = (f32[32]{0:T(128)S(1)}, f32[32]{0:T(128)}, u32[]{:S(2)}) copy-start(f32[32]{0:T(128)} %get-tuple-element.31) | copy-start | bytes 388
  75.7 56.7 %collective-permute-start.2 = (bf16[2,32,16,384]{3,2,1,0:T(8,128)(2,1)}, bf16[2,32,16,384]{3,2,1,0:T(8,128)(2,1)S(1)}, u32[]{:S(2)}, u32[]{:S(2)}) collective-permute-start(bf16[2,32,16,384]{3,2,1,0:T(8,128)(2,1)} %maximum_select_fusion), channel_id=1, source_target_pairs={{0,0},{1,4},{2,8},{3,12},{4,1},{5,5},{6,9},{7,13},{8,2},{9,6},{10,... | collective-permute-start | bytes 2359304 | tf_op jit(solution)/shard_map/ppermute | solution.py:131
  80.1 4.4 %copy-start.10 = (f32[2,32,16,384]{3,2,1,0:T(8,128)S(1)}, f32[2,32,16,384]{3,2,1,0:T(8,128)}, u32[]{:S(2)}) copy-start(f32[2,32,16,384]{3,2,1,0:T(8,128)} %get-tuple-element.82) | copy-start | bytes 4718596
  80.1 4.4 %copy-start.11 = (f32[2,32,16,384]{3,2,1,0:T(8,128)S(1)}, f32[2,32,16,384]{3,2,1,0:T(8,128)}, u32[]{:S(2)}) copy-start(f32[2,32,16,384]{3,2,1,0:T(8,128)} %get-tuple-element.83) | copy-start | bytes 4718596
  80.1 4.3 %copy-start.12 = (f32[2,32,16,384]{3,2,1,0:T(8,128)S(1)}, f32[2,32,16,384]{3,2,1,0:T(8,128)}, u32[]{:S(2)}) copy-start(f32[2,32,16,384]{3,2,1,0:T(8,128)} %get-tuple-element.84) | copy-start | bytes 4718596
  80.1 4.3 %copy-start.13 = (f32[2,32,16,384]{3,2,1,0:T(8,128)S(1)}, f32[2,32,16,384]{3,2,1,0:T(8,128)}, u32[]{:S(2)}) copy-start(f32[2,32,16,384]{3,2,1,0:T(8,128)} %get-tuple-element.85) | copy-start | bytes 4718596
  80.1 4.3 %copy-start.14 = (f32[2,32,16,384]{3,2,1,0:T(8,128)S(1)}, f32[2,32,16,384]{3,2,1,0:T(8,128)}, u32[]{:S(2)}) copy-start(f32[2,32,16,384]{3,2,1,0:T(8,128)} %get-tuple-element.86) | copy-start | bytes 4718596
  80.1 4.3 %copy-start.15 = (f32[2,32,16,384]{3,2,1,0:T(8,128)S(1)}, f32[2,32,16,384]{3,2,1,0:T(8,128)}, u32[]{:S(2)}) copy-start(f32[2,32,16,384]{3,2,1,0:T(8,128)} %get-tuple-element.87) | copy-start | bytes 4718596
  80.2 4.4 %copy-start.16 = (f32[2,32,16,384]{3,2,1,0:T(8,128)S(1)}, f32[2,32,16,384]{3,2,1,0:T(8,128)}, u32[]{:S(2)}) copy-start(f32[2,32,16,384]{3,2,1,0:T(8,128)} %get-tuple-element.88) | copy-start | bytes 4718596
  80.2 4.9 %copy-start.17 = (f32[2,32,16,384]{3,2,1,0:T(8,128)S(1)}, f32[2,32,16,384]{3,2,1,0:T(8,128)}, u32[]{:S(2)}) copy-start(f32[2,32,16,384]{3,2,1,0:T(8,128)} %get-tuple-element.116) | copy-start | bytes 4718596
  81.6 4.1 %copy-start.9 = (f32[2,32,16,384]{3,2,1,0:T(8,128)S(1)}, f32[2,32,16,384]{3,2,1,0:T(8,128)}, u32[]{:S(2)}) copy-start(f32[2,32,16,384]{3,2,1,0:T(8,128)} %get-tuple-element.81) | copy-start | bytes 4718596
  82.7 66.0 %collective-permute-start.3 = (bf16[2,32,16,384]{3,2,1,0:T(8,128)(2,1)}, bf16[2,32,16,384]{3,2,1,0:T(8,128)(2,1)}, u32[]{:S(2)}, u32[]{:S(2)}) collective-permute-start(bf16[2,32,16,384]{3,2,1,0:T(8,128)(2,1)} %maximum_select_fusion.1), channel_id=1, source_target_pairs={{0,4},{1,8},{2,12},{3,0},{4,5},{5,9},{6,13},{7,1},{8,6},{9,10},{10... | collective-permute-start | bytes 2359304 | tf_op jit(solution)/shard_map/ppermute | solution.py:131
  87.1 4.1 %copy-start.8 = (f32[2,32,16,384]{3,2,1,0:T(8,128)S(1)}, f32[2,32,16,384]{3,2,1,0:T(8,128)}, u32[]{:S(2)}) copy-start(f32[2,32,16,384]{3,2,1,0:T(8,128)} %get-tuple-element.113) | copy-start | bytes 4718596
  94.0 4.3 %copy-start.40 = (s32[16,1536]{1,0:T(8,128)S(1)}, s32[16,1536]{1,0:T(8,128)}, u32[]{:S(2)}) copy-start(s32[16,1536]{1,0:T(8,128)} %param.12) | copy-start | bytes 294916
  95.1 56.3 %collective-permute-start.4 = (bf16[2,32,16,384]{3,2,1,0:T(8,128)(2,1)}, bf16[2,32,16,384]{3,2,1,0:T(8,128)(2,1)S(1)}, u32[]{:S(2)}, u32[]{:S(2)}) collective-permute-start(bf16[2,32,16,384]{3,2,1,0:T(8,128)(2,1)} %maximum_select_fusion.2), channel_id=1, source_target_pairs={{0,8},{1,12},{2,0},{3,4},{4,9},{5,13},{6,1},{7,5},{8,10},{9,14},{1... | collective-permute-start | bytes 2359304 | tf_op jit(solution)/shard_map/ppermute | solution.py:131
  97.3 57.9 %collective-permute-start.5 = (bf16[2,32,16,384]{3,2,1,0:T(8,128)(2,1)}, bf16[2,32,16,384]{3,2,1,0:T(8,128)(2,1)S(1)}, u32[]{:S(2)}, u32[]{:S(2)}) collective-permute-start(bf16[2,32,16,384]{3,2,1,0:T(8,128)(2,1)} %maximum_select_fusion.3), channel_id=1, source_target_pairs={{0,12},{1,0},{2,4},{3,8},{4,13},{5,1},{6,5},{7,9},{8,14},{9,2},{10... | collective-permute-start | bytes 2359304 | tf_op jit(solution)/shard_map/ppermute | solution.py:131
  151.5 4.7 %copy-start.38 = (bf16[2,32,16,384]{3,2,1,0:T(8,128)(2,1)}, bf16[2,32,16,384]{3,2,1,0:T(8,128)(2,1)S(1)}, u32[]{:S(2)}) copy-start(bf16[2,32,16,384]{3,2,1,0:T(8,128)(2,1)S(1)} %collective-permute-done.4) | copy-start | bytes 2359300
  155.2 10.1 %copy-start.37 = (bf16[2,32,16,384]{3,2,1,0:T(8,128)(2,1)}, bf16[2,32,16,384]{3,2,1,0:T(8,128)(2,1)S(1)}, u32[]{:S(2)}) copy-start(bf16[2,32,16,384]{3,2,1,0:T(8,128)(2,1)S(1)} %collective-permute-done.5) | copy-start | bytes 2359300
  188.5 7.1 %copy-start.1 = (s32[66]{0:T(128)S(1)}, s32[66]{0:T(128)}, u32[]{:S(2)}) copy-start(s32[66]{0:T(128)} %param.8) | copy-start | bytes 796
  (20 other events, 60.7 us)
Sparse Core Ops, SparseCore 0:
  14.3 37.6 all-gather.2

commit v2 on v1

--- a/solution.py
+++ b/solution.py
@@ -35,7 +35,6 @@
     imag_part = jnp.zeros_like(real_part)
     for offset in range(2 * REACH + 1):
         shifted = lax.slice_in_dim(rows, 2 * REACH - offset, 2 * REACH - offset + length, axis=2)
-        shifted = shifted.astype(jnp.float32)
         tap_real = slot_taps[0, :, offset][:, None, None]
         tap_imag = slot_taps[1, :, offset][:, None, None]
         real_part = real_part + tap_real * shifted[0] - tap_imag * shifted[1]
@@ -107,16 +106,18 @@
     padded = jnp.pad(padded, ((0, 0), (0, SLOTS), (0, 0), (0, 0)))
 
     panel = lax.all_gather(filter_panels[0], "freq", axis=0, tiled=True)
-    panel = panel.reshape(channels, nf, f_blk)
+    if q == 1:
+        shift = ((a + 1) % nf) * f_blk
+        panel = lax.dynamic_slice_in_dim(jnp.concatenate([panel, panel], axis=1), shift, channels, axis=1)
 
     c_own = a
     u_src = (a % q) * nf + b
-    fit = jnp.zeros((2, SLOTS, t_out, channels), jnp.float32)
-    slotted = jnp.zeros((2, SLOTS, t_out, channels), jnp.bfloat16)
+    fit = None
+    received = []
     for r in range(nt):
         c_send = (u_src + r) % nt
         start = class_starts[c_send]
-        rows = lax.dynamic_slice_in_dim(padded, start, SLOTS, axis=1)
+        rows = lax.optimization_barrier(lax.dynamic_slice_in_dim(padded, start, SLOTS, axis=1))
         row_ids = jnp.clip(start + slot_positions, 0, baselines - 1)
         slot_taps = taps_kept[:, class_ids[row_ids], :]
         chunk = convolve(rows, slot_taps, t_in)
@@ -132,16 +133,30 @@
         u_dst = (c_own - r) % nt
         t_sub = u_dst // nf
         b_src = u_dst % nf
-        gate = lax.dynamic_slice(flag_mask, (t_sub * t_in, b_src * f_blk), (t_in, f_blk))
+        if q == 1:
+            gate = lax.dynamic_slice_in_dim(flag_mask, b_src * f_blk, f_blk, axis=1)
+            cols = lax.slice_in_dim(panel, (nf - 1 - r) * f_blk, (nf - r) * f_blk, axis=1)
+        else:
+            gate = lax.dynamic_slice(flag_mask, (t_sub * t_in, b_src * f_blk), (t_in, f_blk))
+            cols = lax.dynamic_slice_in_dim(panel, b_src * f_blk, f_blk, axis=1)
         weighted = got * gate.astype(jnp.bfloat16)
-        cols = lax.dynamic_index_in_dim(panel, b_src, axis=1, keepdims=False)
         part = jnp.einsum("rstj,ij->rsti", weighted, cols, preferred_element_type=jnp.float32)
         if q == 1:
-            fit = fit + part
+            fit = part if fit is None else fit + part
+            received.append(got)
         else:
+            if fit is None:
+                fit = jnp.zeros((2, SLOTS, t_out, channels), jnp.float32)
+                slotted = jnp.zeros((2, SLOTS, t_out, channels), jnp.bfloat16)
             prev = lax.dynamic_slice_in_dim(fit, t_sub * t_in, t_in, axis=2)
             fit = lax.dynamic_update_slice_in_dim(fit, prev + part, t_sub * t_in, axis=2)
-        slotted = lax.dynamic_update_slice(slotted, got, (0, 0, t_sub * t_in, b_src * f_blk))
+            slotted = lax.dynamic_update_slice(slotted, got, (0, 0, t_sub * t_in, b_src * f_blk))
+    if q == 1:
+        stacked = jnp.stack(received)
+        slotted = jnp.concatenate(
+            [lax.dynamic_index_in_dim(stacked, (a - k) % nf, 0, keepdims=False) for k in range(nf)],
+            axis=3,
+        )
     cleaned = (slotted.astype(jnp.float32) - fit).astype(jnp.bfloat16)
     return cleaned[:, None]
 

time: 203 us -> 166 us (0.82)
  local copies, waits for them, and re-layouts: 57.6 us -> 20.1 us
  other arithmetic: 46 us -> 35.2 us
  waiting for transfers between devices: 50.8 us -> 58.1 us
  matrix products: 13.7 us -> 16.6 us
    convert_element_type x1 -> x0, other arithmetic: 17.1 us -> none  [convolve(): shifted = shifted.astype(jnp.float32)]
    dynamic_slice x1, local copies, waits for them, and re-layouts: 16.5 us -> 0.71 us  [shards(): lax.dynamic_slice_in_dim(padded, start, SLOTS, axis=1)]
    reshape x1 -> x0, local copies, waits for them, and re-layouts: 9.1 us -> none  [shards(): panel = panel.reshape(channels, nf, f_blk)]
    unnamed x122 -> x62, local copies, waits for them, and re-layouts: 7.64 us -> 0.24 us
    ppermute x4, waiting for transfers between devices: 50.8 us -> 57.4 us  [shards(): got = lax.ppermute(chunk, ('tm', 'freq'), perm)]
    dynamic_update_slice x4 -> x0, local copies, waits for them, and re-layouts: 5.12 us -> none  [shards(): lax.dynamic_update_slice(slotted, got, (0, 0, t_sub * t_in, b_src * f_blk))]
    concatenate x0 -> x1, other arithmetic: none -> 4.15 us  [shards(): jnp.concatenate([panel, panel], axis=1)]
    dot_general x4, matrix products: 13.7 us -> 16.6 us  [shards(): jnp.einsum('rstj,ij->rsti', weighted, cols, preferred_element_type=jnp.fl...]
  transfers between devices with their start and end apart: 7 -> 7, of which waited for: 4 -> 3; matrix products, arithmetic and copies ran while one was open for 34% -> 31% of each run, Pallas kernels for 0% -> 0%
where the time goes in v2:
time: 166 us; the launch traced here: 164 us
  waiting for transfers between devices  58.1 us (35%)
  other arithmetic  35.2 us (21%)
  between operations  21.6 us (13%)
  local copies, waits for them, and re-layouts  20.1 us (12%)
  matrix products  16.6 us (10%)
  starting transfers between devices  12.1 us (7%)
    ppermute x4, waiting for transfers between devices, shards(): got = lax.ppermute(chunk, ('tm', 'freq'), perm)  57.4 us
    another operation x9, other arithmetic  16.8 us
    dot_general x4, matrix products, shards(): jnp.einsum('rstj,ij->rsti', weighted, cols, preferred_element_type=jnp.fl...  16.6 us
    slice x4, local copies, waits for them, and re-layouts, convolve(): tap_real = slot_taps[0, :, offset][:, None, None]  9.02 us
    ppermute x4, starting transfers between devices, shards(): got = lax.ppermute(chunk, ('tm', 'freq'), perm)  6.1 us
    gather x8, local copies, waits for them, and re-layouts, shards(): slot_taps = taps_kept[:, class_ids[row_ids], :]  5.23 us
    select_n x4, other arithmetic, shards(): jnp.where(live[None, :, None, None], chunk, jnp.zeros((), chunk.dtype))  4.27 us
    concatenate x1, other arithmetic, shards(): jnp.concatenate([panel, panel], axis=1)  4.15 us
  transfers between devices with their start and end apart: 7, of which 3 were waited for; matrix products, arithmetic and copies ran while one was open for 31% of the time, Pallas kernels for 0%

profile of v2, /device:TPU:14, one launch (start us, length us, event | category | flops | bytes accessed | tf_op | source)
XLA Modules:
  0.0 163.7 jit_solution(3784602580162282167)
XLA Ops:
  6.6 0.7 all-gather.3.cloned.1.call-update
  7.3 1.7 %fusion.171 = (bf16[2,66,4,384]{3,2,1,0:T(4,128)(2,1)S(1)}, bf16[2,66,4,384]{3,2,1,0:T(4,128)(2,1)S(1)}) fusion(bf16[2,66,16,384]{3,2,1,0:T(8,128)(2,1)} %param.7), kind=kLoop, calls=%fused_computation.444 | loop fusion | bytes 1622016 | tf_op jit(solution)/shard_map/slice | solution.py:15
  9.1 2.5 %collective-permute-start.1 = (bf16[2,66,4,384]{3,1,2,0:T(8,128)(2,1)S(1)}, bf16[2,66,4,384]{3,1,2,0:T(8,128)(2,1)S(1)}, u32[]{:S(2)}, u32[]{:S(2)}) collective-permute-start(bf16[2,66,4,384]{3,1,2,0:T(8,128)(2,1)S(1)} %copy.22), channel_id=1, source_target_pairs={{4,0},{8,4},{12,8},{5,1},{9,5},{13,9},{6,2},{10,6},{14,10},{7,3},{... | collective-permute-start | bytes 1216520 | tf_op jit(solution)/shard_map/ppermute | solution.py:20
  11.6 3.5 %collective-permute-start = (bf16[2,66,4,384]{3,1,2,0:T(8,128)(2,1)S(1)}, bf16[2,66,4,384]{3,1,2,0:T(8,128)(2,1)S(1)}, u32[]{:S(2)}, u32[]{:S(2)}) collective-permute-start(bf16[2,66,4,384]{3,1,2,0:T(8,128)(2,1)S(1)} %copy.21), channel_id=1, source_target_pairs={{0,4},{4,8},{8,12},{1,5},{5,9},{9,13},{2,6},{6,10},{10,14},{3,7},{... | collective-permute-start | bytes 1216520 | tf_op jit(solution)/shard_map/ppermute | solution.py:18
  15.4 0.7 fusion.173
  21.0 0.7 fusion.172
  21.7 1.2 fusion.167
  22.9 1.3 fusion.163
  24.2 1.1 iota_compare_fusion.1
  25.3 1.2 iota_compare_fusion.3
  26.5 1.2 iota_compare_fusion.4
  27.7 0.7 gather_fusion
  28.5 0.7 gather_fusion.4
  29.2 0.7 gather_fusion.2
  29.9 0.7 gather_fusion.6
  31.4 2.1 %slice_reduce_fusion.17 = (f32[32]{0:T(128)S(1)}, f32[32]{0:T(128)S(1)}, f32[32]{0:T(128)S(1)}, f32[32]{0:T(128)S(1)}, f32[32]{0:T(128)S(1)}, /*index=5*/f32[32]...) fusion(f32[2,32,9]{2,0,1:T(2,128)S(1)} %bitcast.81), kind=kLoop, calls=%fused_computation.353 | loop fusion | bytes 4608 | tf_op jit(solution)/shard_map/slice | solution.py:38
  33.5 0.6 gather_fusion.3
  34.1 2.7 %slice_reduce_fusion.53 = (f32[32]{0:T(128)S(1)}, f32[32]{0:T(128)S(1)}, f32[32]{0:T(128)}, f32[32]{0:T(128)}, f32[32]{0:T(128)}, /*index=5*/f32[32]{0:T(128)}, ...) fusion(f32[2,32,9]{2,0,1:T(2,128)S(1)} %bitcast.82), kind=kLoop, calls=%fused_computation.389 | loop fusion | bytes 4608 | tf_op jit(solution)/shard_map/slice | solution.py:38
  36.8 0.6 gather_fusion.5
  41.1 2.1 %slice_reduce_fusion.35 = (f32[32]{0:T(128)S(1)}, f32[32]{0:T(128)S(1)}, f32[32]{0:T(128)S(1)}, f32[32]{0:T(128)S(1)}, f32[32]{0:T(128)S(1)}, /*index=5*/f32[32]...) fusion(f32[2,32,9]{2,0,1:T(2,128)S(1)} %bitcast.80), kind=kLoop, calls=%fused_computation.371 | loop fusion | bytes 4608 | tf_op jit(solution)/shard_map/slice | solution.py:38
  43.2 2.1 %slice_reduce_fusion.71 = (f32[32]{0:T(128)S(1)}, f32[32]{0:T(128)S(1)}, f32[32]{0:T(128)S(1)}, f32[32]{0:T(128)S(1)}, f32[32]{0:T(128)S(1)}, /*index=5*/f32[32]...) fusion(f32[2,32,9]{2,0,1:T(2,128)S(1)} %bitcast.79), kind=kLoop, calls=%fused_computation.407 | loop fusion | bytes 4608 | tf_op jit(solution)/shard_map/slice | solution.py:38
  45.7 1.7 %fusion.5 = bf16[2,98,24,384]{3,2,1,0:T(8,128)(2,1)S(1)} fusion(bf16[2,66,4,384]{3,2,1,0:T(4,128)(2,1)S(1)} %copy.15, bf16[2,66,16,384]{3,2,1,0:T(8,128)(2,1)S(1)} %copy-done.2, bf16[2,66,4,384]{3,2,1,0:T(4,128)(2,1)S(1)} %copy.14), kind=kLoop, calls=%fused_computation.17 | loop fusion | flops 18063360 | bytes 6045696 | tf_op jit(solution)/shard_map/concatenate | solution.py:16
  47.3 0.7 constant_dynamic-slice_fusion
  48.1 2.1 %fusion.158 = bf16[1,32,16,384]{3,2,1,0:T(8,128)(2,1)S(1)} fusion(f32[32]{0:T(128)S(1)} %get-tuple-element.58, f32[32]{0:T(128)S(1)} %get-tuple-element.42, f32[32]{0:T(128)S(1)} %get-tuple-element.43, f32[32]{0:T(128)S(1)} %get-tuple-element.44, f32[32]{0:T(128)S(1)} %get-tuple-element.45, f32[32]{0:T(128)S(1)} %get-tuple-element.46, ...), kind=kLoop, calls=%fused_computation.327 | loop fusion | flops 10616832 | bytes 7473408 | tf_op jit(solution)/shard_map/convert.6
  50.3 2.1 %fusion.157 = bf16[1,32,16,384]{3,2,1,0:T(8,128)(2,1)S(1)} fusion(f32[32]{0:T(128)S(1)} %get-tuple-element.58, f32[32]{0:T(128)S(1)} %get-tuple-element.42, f32[32]{0:T(128)S(1)} %get-tuple-element.43, f32[32]{0:T(128)S(1)} %get-tuple-element.44, f32[32]{0:T(128)S(1)} %get-tuple-element.45, f32[32]{0:T(128)S(1)} %get-tuple-element.46, ...), kind=kLoop, calls=%fused_computation.326 | loop fusion | flops 10616832 | bytes 7473408 | tf_op jit(solution)/shard_map/convert.7
  52.4 1.1 maximum_select_fusion
  53.5 2.5 %collective-permute-start.2 = (bf16[2,32,16,384]{3,2,1,0:T(8,128)(2,1)}, bf16[2,32,16,384]{3,2,1,0:T(8,128)(2,1)S(1)}, u32[]{:S(2)}, u32[]{:S(2)}) collective-permute-start(bf16[2,32,16,384]{3,2,1,0:T(8,128)(2,1)} %maximum_select_fusion), channel_id=1, source_target_pairs={{0,0},{1,4},{2,8},{3,12},{4,1},{5,5},{6,9},{7,13},{8,2},{9,6},{10,... | collective-permute-start | bytes 2359304 | tf_op jit(solution)/shard_map/ppermute | solution.py:132
  56.2 2.1 %fusion.156 = bf16[1,32,16,384]{3,2,1,0:T(8,128)(2,1)S(1)} fusion(f32[32]{0:T(128)S(1)} %copy-done.24, f32[32]{0:T(128)S(1)} %get-tuple-element.24, f32[32]{0:T(128)S(1)} %copy-done.9, f32[32]{0:T(128)S(1)} %copy-done.10, f32[32]{0:T(128)S(1)} %copy-done.11, f32[32]{0:T(128)S(1)} %copy-done.12, f32[32]{0:T(128)S(1)} %copy-done.13, f32[32]{0:T(128)S(1)} %copy-done.14, ...), kind=kLoop, calls=%fused_computation.325 | loop fusion | flops 10616832 | bytes 7473408 | tf_op jit(solution)/shard_map/convert.4
  58.3 2.1 %fusion.155 = bf16[1,32,16,384]{3,2,1,0:T(8,128)(2,1)S(1)} fusion(f32[32]{0:T(128)S(1)} %copy-done.24, f32[32]{0:T(128)S(1)} %get-tuple-element.24, f32[32]{0:T(128)S(1)} %copy-done.9, f32[32]{0:T(128)S(1)} %copy-done.10, f32[32]{0:T(128)S(1)} %copy-done.11, f32[32]{0:T(128)S(1)} %copy-done.12, f32[32]{0:T(128)S(1)} %copy-done.13, f32[32]{0:T(128)S(1)} %copy-done.14, ...), kind=kLoop, calls=%fused_computation.324 | loop fusion | flops 10616832 | bytes 7473408 | tf_op jit(solution)/shard_map/convert.5
  60.4 1.1 maximum_select_fusion.1
  61.5 2.0 %collective-permute-start.3 = (bf16[2,32,16,384]{3,2,1,0:T(8,128)(2,1)}, bf16[2,32,16,384]{3,2,1,0:T(8,128)(2,1)S(1)}, u32[]{:S(2)}, u32[]{:S(2)}) collective-permute-start(bf16[2,32,16,384]{3,2,1,0:T(8,128)(2,1)} %maximum_select_fusion.1), channel_id=1, source_target_pairs={{0,4},{1,8},{2,12},{3,0},{4,5},{5,9},{6,13},{7,1},{8,6},{9,10},{10... | collective-permute-start | bytes 2359304 | tf_op jit(solution)/shard_map/ppermute | solution.py:132
  63.5 2.0 %fusion.152 = bf16[1,32,16,384]{3,2,1,0:T(8,128)(2,1)S(1)} fusion(f32[32]{0:T(128)S(1)} %get-tuple-element.22, f32[32]{0:T(128)S(1)} %get-tuple-element.6, f32[32]{0:T(128)S(1)} %get-tuple-element.7, f32[32]{0:T(128)S(1)} %get-tuple-element.8, f32[32]{0:T(128)S(1)} %get-tuple-element.9, f32[32]{0:T(128)S(1)} %get-tuple-element.10, ...), kind=kLoop, calls=%fused_computation.321 | loop fusion | flops 10616832 | bytes 7473408 | tf_op jit(solution)/shard_map/convert
  65.6 2.1 %fusion.151 = bf16[1,32,16,384]{3,2,1,0:T(8,128)(2,1)S(1)} fusion(f32[32]{0:T(128)S(1)} %get-tuple-element.22, f32[32]{0:T(128)S(1)} %get-tuple-element.6, f32[32]{0:T(128)S(1)} %get-tuple-element.7, f32[32]{0:T(128)S(1)} %get-tuple-element.8, f32[32]{0:T(128)S(1)} %get-tuple-element.9, f32[32]{0:T(128)S(1)} %get-tuple-element.10, ...), kind=kLoop, calls=%fused_computation.320 | loop fusion | flops 10616832 | bytes 7473408 | tf_op jit(solution)/shard_map/convert.1
  67.7 1.1 maximum_select_fusion.3
  69.2 2.0 %fusion.154 = bf16[1,32,16,384]{3,2,1,0:T(8,128)(2,1)S(1)} fusion(f32[32]{0:T(128)S(1)} %get-tuple-element.76, f32[32]{0:T(128)S(1)} %get-tuple-element.60, f32[32]{0:T(128)S(1)} %get-tuple-element.61, f32[32]{0:T(128)S(1)} %get-tuple-element.62, f32[32]{0:T(128)S(1)} %get-tuple-element.63, f32[32]{0:T(128)S(1)} %get-tuple-element.64, ...), kind=kLoop, calls=%fused_computation.323 | loop fusion | flops 10616832 | bytes 7473408 | tf_op jit(solution)/shard_map/convert.2
  71.3 2.1 %fusion.153 = bf16[1,32,16,384]{3,2,1,0:T(8,128)(2,1)S(1)} fusion(f32[32]{0:T(128)S(1)} %get-tuple-element.76, f32[32]{0:T(128)S(1)} %get-tuple-element.60, f32[32]{0:T(128)S(1)} %get-tuple-element.61, f32[32]{0:T(128)S(1)} %get-tuple-element.62, f32[32]{0:T(128)S(1)} %get-tuple-element.63, f32[32]{0:T(128)S(1)} %get-tuple-element.64, ...), kind=kLoop, calls=%fused_computation.322 | loop fusion | flops 10616832 | bytes 7473408 | tf_op jit(solution)/shard_map/convert.3
  73.4 1.1 maximum_select_fusion.2
  74.5 1.1 collective-permute-start.4
  75.6 34.2 %collective-permute-done.2 = bf16[2,32,16,384]{3,2,1,0:T(8,128)(2,1)S(1)} collective-permute-done((bf16[2,32,16,384]{3,2,1,0:T(8,128)(2,1)}, bf16[2,32,16,384]{3,2,1,0:T(8,128)(2,1)S(1)}, u32[]{:S(2)}, u32[]{:S(2)}) %collective-permute-start.2) | collective-permute-done | bytes 786464 | tf_op jit(solution)/shard_map/ppermute | solution.py:132
  109.8 16.9 %collective-permute-done.3 = bf16[2,32,16,384]{3,2,1,0:T(8,128)(2,1)S(1)} collective-permute-done((bf16[2,32,16,384]{3,2,1,0:T(8,128)(2,1)}, bf16[2,32,16,384]{3,2,1,0:T(8,128)(2,1)S(1)}, u32[]{:S(2)}, u32[]{:S(2)}) %collective-permute-start.3) | collective-permute-done | bytes 786464 | tf_op jit(solution)/shard_map/ppermute | solution.py:132
  126.7 6.3 %collective-permute-done.4 = bf16[2,32,16,384]{3,2,1,0:T(8,128)(2,1)} collective-permute-done((bf16[2,32,16,384]{3,2,1,0:T(8,128)(2,1)}, bf16[2,32,16,384]{3,2,1,0:T(8,128)(2,1)}, u32[]{:S(2)}, u32[]{:S(2)}) %collective-permute-start.4) | collective-permute-done | bytes 786464 | tf_op jit(solution)/shard_map/ppermute | solution.py:132
  133.0 1.5 pad_maximum_fusion
  134.5 1.5 dynamic-slice_bitcast_fusion.3
  136.0 4.1 %fusion.3 = bf16[1536,1536]{1,0:T(8,128)(2,1)S(1)} fusion(s32[]{:T(128)S(6)} %select_n.249, bf16[1536,1536]{1,0:T(8,128)(2,1)} %bitcast.78), kind=kLoop, calls=%fused_computation.15 | loop fusion | flops 9437184 | bytes 9437188 | tf_op jit(solution)/shard_map/concatenate | solution.py:111
  140.2 3.6 %fusion.8 = f32[2,32,16,1536]{3,2,1,0:T(8,128)S(1)} fusion(bf16[1536,1536]{1,0:T(8,128)(2,1)S(1)} %fusion.3, bf16[2,32,16,384]{3,2,1,0:T(8,128)(2,1)} %collective-permute-done.4, bf16[16,384]{1,0:T(8,128)(2,1)S(1)} %get-tuple-element.90), kind=kOutput, calls=%fused_computation.23 | convolution fusion | flops 1208352768 | bytes 8269824 | tf_op jit(solution)/shard_map/rstj,ij->rsti/dot_general | solution.py:143
  143.8 1.8 %fusion.9 = f32[2,32,16,1536]{3,2,1,0:T(8,128)S(1)} fusion(bf16[1536,1536]{1,0:T(8,128)(2,1)S(1)} %fusion.3, bf16[2,32,16,384]{3,2,1,0:T(8,128)(2,1)S(1)} %copy-done.6, bf16[16,384]{1,0:T(8,128)(2,1)S(1)} %get-tuple-element.88), kind=kOutput, calls=%fused_computation.25 | convolution fusion | flops 1208352768 | bytes 8269824 | tf_op jit(solution)/shard_map/rstj,ij->rsti/dot_general | solution.py:143
  145.7 4.5 %fusion.10 = f32[2,32,16,1536]{3,2,1,0:T(8,128)} fusion(bf16[1536,1536]{1,0:T(8,128)(2,1)S(1)} %fusion.3, bf16[2,32,16,384]{3,2,1,0:T(8,128)(2,1)S(1)} %copy-done.4, bf16[16,384]{1,0:T(8,128)(2,1)S(1)} %get-tuple-element.89), kind=kOutput, calls=%fused_computation.27 | convolution fusion | flops 1208352768 | bytes 8269824 | tf_op jit(solution)/shard_map/rstj,ij->rsti/dot_general | solution.py:143
  150.2 6.7 %fusion.6 = bf16[2,1,32,16,1536]{4,3,2,1,0:T(8,128)(2,1)} fusion(f32[2,32,16,1536]{3,2,1,0:T(8,128)S(1)} %fusion.8, f32[2,32,16,1536]{3,2,1,0:T(8,128)} %fusion.10, f32[2,32,16,1536]{3,2,1,0:T(8,128)S(1)} %fusion.9, bf16[2,32,16,384]{3,2,1,0:T(8,128)(2,1)} %get-tuple-element.82, bf16[2,32,16,384]{3,2,1,0:T(8,128)(2,1)} %get-tuple-element.83, ...), kind=kOutput, calls=%fused_computation.18 | convolution fusion | flops 1228800000 | bytes 27144192 | tf_op jit(solution)/shard_map/rstj,ij->rsti/dot_general | solution.py:143
  (91 shorter events, 3.2 us)
Async XLA Ops:
  6.5 21.2 %copy-start = (s32[66]{0:T(128)S(1)}, s32[66]{0:T(128)}, u32[]{:S(2)}) copy-start(s32[66]{0:T(128)} %param.8) | copy-start | bytes 796
  6.5 8.6 %copy-start.8 = (s32[4]{0:T(128)S(1)}, s32[4]{0:T(128)}, u32[]{:S(2)}) copy-start(s32[4]{0:T(128)} %param.9) | copy-start | bytes 52
  6.5 24.1 %copy-start.29 = (s32[4]{0:T(128)S(1)}, s32[4]{0:T(128)}, u32[]{:S(2)}) copy-start(s32[4]{0:T(128)} %param.10) | copy-start | bytes 52
  6.5 24.2 %copy-start.25 = (f32[2,4,9]{2,1,0:T(4,128)S(1)}, f32[2,4,9]{2,1,0:T(4,128)}, u32[]{:S(2)}) copy-start(f32[2,4,9]{2,1,0:T(4,128)} %param.11) | copy-start | bytes 868
  6.5 129.5 %all-gather.3.cloned.1.call-start = ((), (), s32[]{:S(2)}) async-start(), calls=%async_computation | async-start | bytes 5898240 | tf_op jit(solution)/shard_map/all_gather | solution.py:108
  9.0 36.7 %copy-start.2 = (bf16[2,66,16,384]{3,2,1,0:T(8,128)(2,1)S(1)}, bf16[2,66,16,384]{3,2,1,0:T(8,128)(2,1)}, u32[]{:S(2)}) copy-start(bf16[2,66,16,384]{3,2,1,0:T(8,128)(2,1)} %param.7) | copy-start | bytes 4866052
  9.1 36.2 %collective-permute-start.1 = (bf16[2,66,4,384]{3,1,2,0:T(8,128)(2,1)S(1)}, bf16[2,66,4,384]{3,1,2,0:T(8,128)(2,1)S(1)}, u32[]{:S(2)}, u32[]{:S(2)}) collective-permute-start(bf16[2,66,4,384]{3,1,2,0:T(8,128)(2,1)S(1)} %copy.22), channel_id=1, source_target_pairs={{4,0},{8,4},{12,8},{5,1},{9,5},{13,9},{6,2},{10,6},{14,10},{7,3},{... | collective-permute-start | bytes 1216520 | tf_op jit(solution)/shard_map/ppermute | solution.py:20
  11.6 33.9 %collective-permute-start = (bf16[2,66,4,384]{3,1,2,0:T(8,128)(2,1)S(1)}, bf16[2,66,4,384]{3,1,2,0:T(8,128)(2,1)S(1)}, u32[]{:S(2)}, u32[]{:S(2)}) collective-permute-start(bf16[2,66,4,384]{3,1,2,0:T(8,128)(2,1)S(1)} %copy.21), channel_id=1, source_target_pairs={{0,4},{4,8},{8,12},{1,5},{5,9},{9,13},{2,6},{6,10},{10,14},{3,7},{... | collective-permute-start | bytes 1216520 | tf_op jit(solution)/shard_map/ppermute | solution.py:18
  50.2 2.3 %copy-start.28 = (pred[32]{0:T(512)(128)(4,1)S(1)}, pred[32]{0:T(512)(128)(4,1)}, u32[]{:S(2)}) copy-start(pred[32]{0:T(512)(128)(4,1)} %iota_compare_fusion.4) | copy-start | bytes 100
  50.2 5.9 %copy-start.9 = (f32[32]{0:T(128)S(1)}, f32[32]{0:T(128)}, u32[]{:S(2)}) copy-start(f32[32]{0:T(128)} %get-tuple-element.25) | copy-start | bytes 388
  50.2 5.9 %copy-start.10 = (f32[32]{0:T(128)S(1)}, f32[32]{0:T(128)}, u32[]{:S(2)}) copy-start(f32[32]{0:T(128)} %get-tuple-element.26) | copy-start | bytes 388
  50.2 5.9 %copy-start.11 = (f32[32]{0:T(128)S(1)}, f32[32]{0:T(128)}, u32[]{:S(2)}) copy-start(f32[32]{0:T(128)} %get-tuple-element.27) | copy-start | bytes 388
  50.2 5.9 %copy-start.12 = (f32[32]{0:T(128)S(1)}, f32[32]{0:T(128)}, u32[]{:S(2)}) copy-start(f32[32]{0:T(128)} %get-tuple-element.28) | copy-start | bytes 388
  50.2 5.9 %copy-start.13 = (f32[32]{0:T(128)S(1)}, f32[32]{0:T(128)}, u32[]{:S(2)}) copy-start(f32[32]{0:T(128)} %get-tuple-element.29) | copy-start | bytes 388
  50.2 5.9 %copy-start.14 = (f32[32]{0:T(128)S(1)}, f32[32]{0:T(128)}, u32[]{:S(2)}) copy-start(f32[32]{0:T(128)} %get-tuple-element.30) | copy-start | bytes 388
  50.2 5.9 %copy-start.15 = (f32[32]{0:T(128)S(1)}, f32[32]{0:T(128)}, u32[]{:S(2)}) copy-start(f32[32]{0:T(128)} %get-tuple-element.31) | copy-start | bytes 388
  50.2 5.9 %copy-start.16 = (f32[32]{0:T(128)S(1)}, f32[32]{0:T(128)}, u32[]{:S(2)}) copy-start(f32[32]{0:T(128)} %get-tuple-element.32) | copy-start | bytes 388
  50.2 5.9 %copy-start.17 = (f32[32]{0:T(128)S(1)}, f32[32]{0:T(128)}, u32[]{:S(2)}) copy-start(f32[32]{0:T(128)} %get-tuple-element.33) | copy-start | bytes 388
  50.3 5.9 %copy-start.18 = (f32[32]{0:T(128)S(1)}, f32[32]{0:T(128)}, u32[]{:S(2)}) copy-start(f32[32]{0:T(128)} %get-tuple-element.34) | copy-start | bytes 388
  50.3 5.9 %copy-start.19 = (f32[32]{0:T(128)S(1)}, f32[32]{0:T(128)}, u32[]{:S(2)}) copy-start(f32[32]{0:T(128)} %get-tuple-element.35) | copy-start | bytes 388
  50.3 5.9 %copy-start.20 = (f32[32]{0:T(128)S(1)}, f32[32]{0:T(128)}, u32[]{:S(2)}) copy-start(f32[32]{0:T(128)} %get-tuple-element.36) | copy-start | bytes 388
  50.3 5.9 %copy-start.21 = (f32[32]{0:T(128)S(1)}, f32[32]{0:T(128)}, u32[]{:S(2)}) copy-start(f32[32]{0:T(128)} %get-tuple-element.37) | copy-start | bytes 388
  50.3 5.9 %copy-start.22 = (f32[32]{0:T(128)S(1)}, f32[32]{0:T(128)}, u32[]{:S(2)}) copy-start(f32[32]{0:T(128)} %get-tuple-element.38) | copy-start | bytes 388
  50.3 5.9 %copy-start.23 = (f32[32]{0:T(128)S(1)}, f32[32]{0:T(128)}, u32[]{:S(2)}) copy-start(f32[32]{0:T(128)} %get-tuple-element.39) | copy-start | bytes 388
  50.3 5.9 %copy-start.24 = (f32[32]{0:T(128)S(1)}, f32[32]{0:T(128)}, u32[]{:S(2)}) copy-start(f32[32]{0:T(128)} %get-tuple-element.40) | copy-start | bytes 388
  53.5 56.3 %collective-permute-start.2 = (bf16[2,32,16,384]{3,2,1,0:T(8,128)(2,1)}, bf16[2,32,16,384]{3,2,1,0:T(8,128)(2,1)S(1)}, u32[]{:S(2)}, u32[]{:S(2)}) collective-permute-start(bf16[2,32,16,384]{3,2,1,0:T(8,128)(2,1)} %maximum_select_fusion), channel_id=1, source_target_pairs={{0,0},{1,4},{2,8},{3,12},{4,1},{5,5},{6,9},{7,13},{8,2},{9,6},{10,... | collective-permute-start | bytes 2359304 | tf_op jit(solution)/shard_map/ppermute | solution.py:132
  58.3 2.1 %copy-start.27 = (pred[32]{0:T(512)(128)(4,1)S(1)}, pred[32]{0:T(512)(128)(4,1)}, u32[]{:S(2)}) copy-start(pred[32]{0:T(512)(128)(4,1)} %iota_compare_fusion.3) | copy-start | bytes 100
  61.5 65.2 %collective-permute-start.3 = (bf16[2,32,16,384]{3,2,1,0:T(8,128)(2,1)}, bf16[2,32,16,384]{3,2,1,0:T(8,128)(2,1)S(1)}, u32[]{:S(2)}, u32[]{:S(2)}) collective-permute-start(bf16[2,32,16,384]{3,2,1,0:T(8,128)(2,1)} %maximum_select_fusion.1), channel_id=1, source_target_pairs={{0,4},{1,8},{2,12},{3,0},{4,5},{5,9},{6,13},{7,1},{8,6},{9,10},{10... | collective-permute-start | bytes 2359304 | tf_op jit(solution)/shard_map/ppermute | solution.py:132
  65.5 2.1 %copy-start.26 = (pred[32]{0:T(512)(128)(4,1)S(1)}, pred[32]{0:T(512)(128)(4,1)}, u32[]{:S(2)}) copy-start(pred[32]{0:T(512)(128)(4,1)} %iota_compare_fusion.1) | copy-start | bytes 100
  68.7 58.0 %collective-permute-start.5 = (bf16[2,32,16,384]{3,2,1,0:T(8,128)(2,1)}, bf16[2,32,16,384]{3,2,1,0:T(8,128)(2,1)S(1)}, u32[]{:S(2)}, u32[]{:S(2)}) collective-permute-start(bf16[2,32,16,384]{3,2,1,0:T(8,128)(2,1)} %maximum_select_fusion.3), channel_id=1, source_target_pairs={{0,12},{1,0},{2,4},{3,8},{4,13},{5,1},{6,5},{7,9},{8,14},{9,2},{10... | collective-permute-start | bytes 2359304 | tf_op jit(solution)/shard_map/ppermute | solution.py:132
  71.3 4.3 %copy-start.7 = (s32[16,1536]{1,0:T(8,128)S(1)}, s32[16,1536]{1,0:T(8,128)}, u32[]{:S(2)}) copy-start(s32[16,1536]{1,0:T(8,128)} %param.12) | copy-start | bytes 294916
  74.5 58.5 %collective-permute-start.4 = (bf16[2,32,16,384]{3,2,1,0:T(8,128)(2,1)}, bf16[2,32,16,384]{3,2,1,0:T(8,128)(2,1)}, u32[]{:S(2)}, u32[]{:S(2)}) collective-permute-start(bf16[2,32,16,384]{3,2,1,0:T(8,128)(2,1)} %maximum_select_fusion.2), channel_id=1, source_target_pairs={{0,8},{1,12},{2,0},{3,4},{4,9},{5,13},{6,1},{7,5},{8,10},{9,14},{1... | collective-permute-start | bytes 2359304 | tf_op jit(solution)/shard_map/ppermute | solution.py:132
  109.8 26.2 %copy-start.3 = (bf16[2,32,16,384]{3,2,1,0:T(8,128)(2,1)}, bf16[2,32,16,384]{3,2,1,0:T(8,128)(2,1)S(1)}, u32[]{:S(2)}) copy-start(bf16[2,32,16,384]{3,2,1,0:T(8,128)(2,1)S(1)} %collective-permute-done.2) | copy-start | bytes 2359300
  126.7 6.3 %copy-start.5 = (bf16[2,32,16,384]{3,2,1,0:T(8,128)(2,1)}, bf16[2,32,16,384]{3,2,1,0:T(8,128)(2,1)S(1)}, u32[]{:S(2)}) copy-start(bf16[2,32,16,384]{3,2,1,0:T(8,128)(2,1)S(1)} %collective-permute-done.3) | copy-start | bytes 2359300
  140.2 5.5 %copy-start.1 = (bf16[1536,1536]{1,0:T(8,128)(2,1)}, bf16[1536,1536]{1,0:T(8,128)(2,1)S(1)}, u32[]{:S(2)}) copy-start(bf16[1536,1536]{1,0:T(8,128)(2,1)S(1)} %fusion.3) | copy-start | bytes 14155780
  140.2 3.6 %copy-start.6 = (bf16[2,32,16,384]{3,2,1,0:T(8,128)(2,1)S(1)}, bf16[2,32,16,384]{3,2,1,0:T(8,128)(2,1)}, u32[]{:S(2)}) copy-start(bf16[2,32,16,384]{3,2,1,0:T(8,128)(2,1)} %copy-done.5) | copy-start | bytes 2359300
  143.8 1.9 %copy-start.4 = (bf16[2,32,16,384]{3,2,1,0:T(8,128)(2,1)S(1)}, bf16[2,32,16,384]{3,2,1,0:T(8,128)(2,1)}, u32[]{:S(2)}) copy-start(bf16[2,32,16,384]{3,2,1,0:T(8,128)(2,1)} %copy-done.3) | copy-start | bytes 2359300
Sparse Core Ops, SparseCore 0:
  8.9 37.5 all-gather.2

commit v3 on v2

--- a/solution.py
+++ b/solution.py
@@ -2,6 +2,7 @@
 import jax.numpy as jnp
 from jax import lax
 from jax.sharding import PartitionSpec as P
+
 
 SLOTS = 32
 REACH = 4
@@ -40,6 +41,18 @@
         real_part = real_part + tap_real * shifted[0] - tap_imag * shifted[1]
         imag_part = imag_part + tap_real * shifted[1] + tap_imag * shifted[0]
     return jnp.stack([real_part, imag_part]).astype(jnp.bfloat16)
+
+
+def convolve_class(rows, taps, count, length):
+    real_part = jnp.zeros(rows.shape[1:2] + (length,) + rows.shape[3:], jnp.float32)
+    imag_part = jnp.zeros_like(real_part)
+    for offset in range(2 * REACH + 1):
+        shifted = lax.slice_in_dim(rows, 2 * REACH - offset, 2 * REACH - offset + length, axis=2)
+        real_part = real_part + taps[0, offset] * shifted[0] - taps[1, offset] * shifted[1]
+        imag_part = imag_part + taps[0, offset] * shifted[1] + taps[1, offset] * shifted[0]
+    out = jnp.stack([real_part, imag_part])
+    live = lax.broadcasted_iota(jnp.int32, out.shape, 1) < count
+    return jnp.where(live, out, 0.0).astype(jnp.bfloat16)
 
 
 def to_slots(per_baseline, class_counts):
@@ -92,7 +105,6 @@
     q = nt // nf
     a = lax.axis_index("tm")
     b = lax.axis_index("freq")
-    baselines = visibilities.shape[1]
     t_in = visibilities.shape[2]
     f_blk = visibilities.shape[3]
     t_out = flag_mask.shape[0]
@@ -100,7 +112,6 @@
 
     taps_kept = masked_taps(fringe_taps, tap_windows)
     class_starts = jnp.cumsum(class_counts) - class_counts
-    slot_positions = jnp.arange(SLOTS, dtype=jnp.int32)
 
     padded = extended(visibilities, (("tm", 2),), REACH)
     padded = jnp.pad(padded, ((0, 0), (0, SLOTS), (0, 0), (0, 0)))
@@ -113,16 +124,12 @@
     c_own = a
     u_src = (a % q) * nf + b
     fit = None
-    received = []
     for r in range(nt):
         c_send = (u_src + r) % nt
         start = class_starts[c_send]
         rows = lax.optimization_barrier(lax.dynamic_slice_in_dim(padded, start, SLOTS, axis=1))
-        row_ids = jnp.clip(start + slot_positions, 0, baselines - 1)
-        slot_taps = taps_kept[:, class_ids[row_ids], :]
-        chunk = convolve(rows, slot_taps, t_in)
-        live = slot_positions < class_counts[c_send]
-        chunk = jnp.where(live[None, :, None, None], chunk, jnp.zeros((), chunk.dtype))
+        taps = lax.dynamic_index_in_dim(taps_kept, c_send, axis=1, keepdims=False)
+        chunk = convolve_class(rows, taps, class_counts[c_send], t_in)
         perm = []
         for sa in range(nt):
             for sb in range(nf):
@@ -141,22 +148,17 @@
             cols = lax.dynamic_slice_in_dim(panel, b_src * f_blk, f_blk, axis=1)
         weighted = got * gate.astype(jnp.bfloat16)
         part = jnp.einsum("rstj,ij->rsti", weighted, cols, preferred_element_type=jnp.float32)
+        if fit is None:
+            slotted = jnp.zeros((2, SLOTS, t_out, channels), jnp.bfloat16)
         if q == 1:
             fit = part if fit is None else fit + part
-            received.append(got)
+            slotted = lax.dynamic_update_slice_in_dim(slotted, got, b_src * f_blk, axis=3)
         else:
             if fit is None:
                 fit = jnp.zeros((2, SLOTS, t_out, channels), jnp.float32)
-                slotted = jnp.zeros((2, SLOTS, t_out, channels), jnp.bfloat16)
             prev = lax.dynamic_slice_in_dim(fit, t_sub * t_in, t_in, axis=2)
             fit = lax.dynamic_update_slice_in_dim(fit, prev + part, t_sub * t_in, axis=2)
             slotted = lax.dynamic_update_slice(slotted, got, (0, 0, t_sub * t_in, b_src * f_blk))
-    if q == 1:
-        stacked = jnp.stack(received)
-        slotted = jnp.concatenate(
-            [lax.dynamic_index_in_dim(stacked, (a - k) % nf, 0, keepdims=False) for k in range(nf)],
-            axis=3,
-        )
     cleaned = (slotted.astype(jnp.float32) - fit).astype(jnp.bfloat16)
     return cleaned[:, None]
 

time: 166 us -> 228 us (1.37)
  other arithmetic: 35.2 us -> 120 us
  waiting for transfers between devices: 58.1 us -> 45.6 us
  local copies, waits for them, and re-layouts: 20.1 us -> 12.9 us
  matrix products: 16.6 us -> 13.4 us
    add x0 -> x4, other arithmetic: none -> 52.2 us  [convolve_class(): imag_part + taps[0, offset] * shifted[1] + taps[1, offset] * shifted[0]]
    sub x0 -> x4, other arithmetic: none -> 52.2 us  [convolve_class(): real_part + taps[0, offset] * shifted[0] - taps[1, offset] * shifted[1]]
    another operation x10 -> x1, other arithmetic: 18.4 us -> 0.83 us
    ppermute x4, waiting for transfers between devices: 57.4 us -> 44.9 us  [shards(): got = lax.ppermute(chunk, ('tm', 'freq'), perm)]
    select_n x10 -> x0, other arithmetic: 6.8 us -> none  [the longest x4 4.27 us: shards(): jnp.where(live[None, :, None, None], chunk, jnp.zeros((), chunk.dtype))]
    slice x4, local copies, waits for them, and re-layouts: 9.02 us -> 2.88 us  [convolve_class(): taps[0, offset] * shifted[0]]
    gather x8 -> x0, local copies, waits for them, and re-layouts: 5.23 us -> none  [shards(): slot_taps = taps_kept[:, class_ids[row_ids], :]]
    convert_element_type x0 -> x4, other arithmetic: none -> 4.42 us  [convolve_class(): return jnp.where(live, out, 0.0).astype(jnp.bfloat16)]
  transfers between devices with their start and end apart: 7 -> 7, of which waited for: 3 -> 2; matrix products, arithmetic and copies ran while one was open for 31% -> 57% of each run, Pallas kernels for 0% -> 0%
where the time goes in v3:
time: 228 us; the launch traced here: 226 us
  other arithmetic  120 us (53%)
  waiting for transfers between devices  45.6 us (20%)
  between operations  21.4 us (9%)
  matrix products  13.4 us (6%)
  starting transfers between devices  13 us (6%)
  local copies, waits for them, and re-layouts  12.9 us (6%)
    add x4, other arithmetic, convolve_class(): imag_part + taps[0, offset] * shifted[1] + taps[1, offset] * shifted[0]  52.2 us
    sub x4, other arithmetic, convolve_class(): real_part + taps[0, offset] * shifted[0] - taps[1, offset] * shifted[1]  52.2 us
    ppermute x4, waiting for transfers between devices, shards(): got = lax.ppermute(chunk, ('tm', 'freq'), perm)  44.9 us
    dot_general x4, matrix products, shards(): jnp.einsum('rstj,ij->rsti', weighted, cols, preferred_element_type=jnp.fl...  13.4 us
    ppermute x4, starting transfers between devices, shards(): got = lax.ppermute(chunk, ('tm', 'freq'), perm)  7.13 us
  transfers between devices with their start and end apart: 7, of which 2 were waited for; matrix products, arithmetic and copies ran while one was open for 57% of the time, Pallas kernels for 0%

profile of v3, /device:TPU:14, one launch (start us, length us, event | category | flops | bytes accessed | tf_op | source)
XLA Modules:
  0.0 226.4 jit_solution(4030177534224634228)
XLA Ops:
  6.5 0.7 all-gather.3.cloned.1.call-update
  7.3 1.7 fusion.159
  9.0 3.5 %collective-permute-start = (bf16[2,66,4,384]{3,2,1,0:T(4,128)(2,1)S(1)}, bf16[2,66,4,384]{3,2,1,0:T(4,128)(2,1)S(1)}, u32[]{:S(2)}, u32[]{:S(2)}) collective-permute-start(bf16[2,66,4,384]{3,2,1,0:T(4,128)(2,1)S(1)} %get-tuple-element.9), channel_id=1, source_target_pairs={{0,4},{4,8},{8,12},{1,5},{5,9},{9,13},{2,6},{6,10},{10,14},{3,7},{... | collective-permute-start | bytes 1216520 | tf_op jit(solution)/shard_map/ppermute | solution.py:19
  12.5 2.4 %collective-permute-start.1 = (bf16[2,66,4,384]{3,2,1,0:T(4,128)(2,1)S(1)}, bf16[2,66,4,384]{3,2,1,0:T(4,128)(2,1)S(1)}, u32[]{:S(2)}, u32[]{:S(2)}) collective-permute-start(bf16[2,66,4,384]{3,2,1,0:T(4,128)(2,1)S(1)} %get-tuple-element.10), channel_id=1, source_target_pairs={{4,0},{8,4},{12,8},{5,1},{9,5},{13,9},{6,2},{10,6},{14,10},{7,3},{... | collective-permute-start | bytes 1216520 | tf_op jit(solution)/shard_map/ppermute | solution.py:21
  14.9 0.8 reduce-window.9
  15.7 0.7 bitcast_subtract_fusion
  16.4 1.5 fusion.164
  23.0 0.7 compare_convert_fusion
  23.8 0.7 broadcast_multiply_fusion
  24.5 0.7 iota_compare_fusion.1
  25.1 0.6 iota_compare_fusion.3
  25.8 0.6 iota_compare_fusion.4
  26.4 0.7 fusion.163
  29.7 0.6 iota_compare_fusion.2
  30.4 0.7 fusion.160
  31.1 0.7 fusion.161
  31.8 0.7 fusion.162
  32.5 1.7 fusion.5
  34.2 0.7 constant_dynamic-slice_fusion
  34.9 13.1 %fusion.31 = bf16[1,32,16,384]{3,2,1,0:T(8,128)(2,1)S(1)} fusion(f32[]{:T(128)} %bitcast.22, f32[]{:T(128)} %bitcast.21, f32[]{:T(128)} %bitcast.20, f32[]{:T(128)} %bitcast.19, f32[]{:T(128)} %bitcast.18, f32[]{:T(128)} %bitcast.17, f32[]{:T(128)} %bitcast.16, f32[]{:T(128)} %bitcast.15, f32[]{:T(128)} %bitcast.14, f32[]{:T(128)} %bitcast.13, f32[]{:T(128)} %bitcast.12, ...), kind=kLoop, calls=%fused_computation.187 | loop fusion | flops 10616832 | bytes 7471176 | tf_op jit(solution)/shard_map/sub | solution.py:51
  48.1 13.1 %fusion.48 = bf16[1,32,16,384]{3,2,1,0:T(8,128)(2,1)S(1)} fusion(f32[]{:T(128)} %bitcast.22, f32[]{:T(128)} %bitcast.21, f32[]{:T(128)} %bitcast.20, f32[]{:T(128)} %bitcast.19, f32[]{:T(128)} %bitcast.18, f32[]{:T(128)} %bitcast.17, f32[]{:T(128)} %bitcast.16, f32[]{:T(128)} %bitcast.15, f32[]{:T(128)} %bitcast.14, f32[]{:T(128)} %bitcast.13, f32[]{:T(128)} %bitcast.12, ...), kind=kLoop, calls=%fused_computation.204 | loop fusion | flops 10616832 | bytes 7471176 | tf_op jit(solution)/shard_map/add | solution.py:52
  61.2 1.1 fusion.7
  62.3 2.3 %collective-permute-start.2 = (bf16[2,32,16,384]{3,2,1,0:T(8,128)(2,1)}, bf16[2,32,16,384]{3,2,1,0:T(8,128)(2,1)S(1)}, u32[]{:S(2)}, u32[]{:S(2)}) collective-permute-start(bf16[2,32,16,384]{3,2,1,0:T(8,128)(2,1)} %fusion.7), channel_id=1, source_target_pairs={{0,0},{1,4},{2,8},{3,12},{4,1},{5,5},{6,9},{7,13},{8,2},{9,6},{10,... | collective-permute-start | bytes 2359304 | tf_op jit(solution)/shard_map/ppermute | solution.py:139
  64.6 13.1 %fusion.65 = bf16[1,32,16,384]{3,2,1,0:T(8,128)(2,1)S(1)} fusion(f32[]{:T(128)} %bitcast.43, f32[]{:T(128)} %bitcast.42, f32[]{:T(128)} %bitcast.41, f32[]{:T(128)} %bitcast.40, f32[]{:T(128)} %bitcast.39, f32[]{:T(128)} %bitcast.38, f32[]{:T(128)} %bitcast.37, f32[]{:T(128)} %bitcast.36, f32[]{:T(128)} %bitcast.35, f32[]{:T(128)} %bitcast.34, f32[]{:T(128)} %bitcast.33, ...), kind=kLoop, calls=%fused_computation.221 | loop fusion | flops 10616832 | bytes 7471176 | tf_op jit(solution)/shard_map/sub | solution.py:51
  77.8 13.1 %fusion.82 = bf16[1,32,16,384]{3,2,1,0:T(8,128)(2,1)S(1)} fusion(f32[]{:T(128)} %bitcast.43, f32[]{:T(128)} %bitcast.42, f32[]{:T(128)} %bitcast.41, f32[]{:T(128)} %bitcast.40, f32[]{:T(128)} %bitcast.39, f32[]{:T(128)} %bitcast.38, f32[]{:T(128)} %bitcast.37, f32[]{:T(128)} %bitcast.36, f32[]{:T(128)} %bitcast.35, f32[]{:T(128)} %bitcast.34, f32[]{:T(128)} %bitcast.33, ...), kind=kLoop, calls=%fused_computation.238 | loop fusion | flops 10616832 | bytes 7471176 | tf_op jit(solution)/shard_map/add | solution.py:52
  90.9 1.1 fusion.8
  92.0 2.0 collective-permute-start.3
  94.1 13.0 %fusion.99 = bf16[1,32,16,384]{3,2,1,0:T(8,128)(2,1)S(1)} fusion(f32[]{:T(128)} %bitcast.64, f32[]{:T(128)} %bitcast.63, f32[]{:T(128)} %bitcast.62, f32[]{:T(128)} %bitcast.61, f32[]{:T(128)} %bitcast.60, f32[]{:T(128)} %bitcast.59, f32[]{:T(128)} %bitcast.58, f32[]{:T(128)} %bitcast.57, f32[]{:T(128)} %bitcast.56, f32[]{:T(128)} %bitcast.55, f32[]{:T(128)} %bitcast.54, ...), kind=kLoop, calls=%fused_computation.255 | loop fusion | flops 10616832 | bytes 7471176 | tf_op jit(solution)/shard_map/sub | solution.py:51
  107.1 13.0 %fusion.116 = bf16[1,32,16,384]{3,2,1,0:T(8,128)(2,1)S(1)} fusion(f32[]{:T(128)} %bitcast.64, f32[]{:T(128)} %bitcast.63, f32[]{:T(128)} %bitcast.62, f32[]{:T(128)} %bitcast.61, f32[]{:T(128)} %bitcast.60, f32[]{:T(128)} %bitcast.59, f32[]{:T(128)} %bitcast.58, f32[]{:T(128)} %bitcast.57, f32[]{:T(128)} %bitcast.56, f32[]{:T(128)} %bitcast.55, ...), kind=kLoop, calls=%fused_computation.272 | loop fusion | flops 10616832 | bytes 7471176 | tf_op jit(solution)/shard_map/add | solution.py:52
  120.2 12.9 %fusion.133 = bf16[1,32,16,384]{3,2,1,0:T(8,128)(2,1)S(1)} fusion(f32[]{:T(128)} %bitcast.85, f32[]{:T(128)} %bitcast.84, f32[]{:T(128)} %bitcast.83, f32[]{:T(128)} %bitcast.82, f32[]{:T(128)} %bitcast.81, f32[]{:T(128)} %bitcast.80, f32[]{:T(128)} %bitcast.79, f32[]{:T(128)} %bitcast.78, f32[]{:T(128)} %bitcast.77, f32[]{:T(128)} %bitcast.76, ...), kind=kLoop, calls=%fused_computation.289 | loop fusion | flops 10616832 | bytes 7471176 | tf_op jit(solution)/shard_map/sub | solution.py:51
  133.0 12.9 %fusion.150 = bf16[1,32,16,384]{3,2,1,0:T(8,128)(2,1)S(1)} fusion(f32[]{:T(128)} %bitcast.85, f32[]{:T(128)} %bitcast.84, f32[]{:T(128)} %bitcast.83, f32[]{:T(128)} %bitcast.82, f32[]{:T(128)} %bitcast.81, f32[]{:T(128)} %bitcast.80, f32[]{:T(128)} %bitcast.79, f32[]{:T(128)} %bitcast.78, f32[]{:T(128)} %bitcast.77, f32[]{:T(128)} %bitcast.76, ...), kind=kLoop, calls=%fused_computation.306 | loop fusion | flops 10616832 | bytes 7471176 | tf_op jit(solution)/shard_map/add | solution.py:52
  145.9 1.1 fusion.9
  147.1 0.5 collective-permute-start.4
  147.6 1.1 fusion.10
  148.7 2.3 %collective-permute-start.5 = (bf16[2,32,16,384]{3,2,1,0:T(8,128)(2,1)}, bf16[2,32,16,384]{3,2,1,0:T(8,128)(2,1)S(1)}, u32[]{:S(2)}, u32[]{:S(2)}) collective-permute-start(bf16[2,32,16,384]{3,2,1,0:T(8,128)(2,1)} %fusion.10), channel_id=1, source_target_pairs={{0,12},{1,0},{2,4},{3,8},{4,13},{5,1},{6,5},{7,9},{8,14},{9,2},{10... | collective-permute-start | bytes 2359304 | tf_op jit(solution)/shard_map/ppermute | solution.py:139
  151.0 2.0 broadcast_in_dim.20
  153.0 1.0 constant_dynamic-update-slice_fusion.3
  154.0 1.0 constant_dynamic-update-slice_fusion.2
  155.0 35.8 %collective-permute-done.4 = bf16[2,32,16,384]{3,2,1,0:T(8,128)(2,1)S(1)} collective-permute-done((bf16[2,32,16,384]{3,2,1,0:T(8,128)(2,1)}, bf16[2,32,16,384]{3,2,1,0:T(8,128)(2,1)S(1)}, u32[]{:S(2)}, u32[]{:S(2)}) %collective-permute-start.4) | collective-permute-done | bytes 786464 | tf_op jit(solution)/shard_map/ppermute | solution.py:139
  190.8 1.0 constant_dynamic-update-slice_fusion.1
  191.7 9.1 %collective-permute-done.5 = bf16[2,32,16,384]{3,2,1,0:T(8,128)(2,1)S(1)} collective-permute-done((bf16[2,32,16,384]{3,2,1,0:T(8,128)(2,1)}, bf16[2,32,16,384]{3,2,1,0:T(8,128)(2,1)S(1)}, u32[]{:S(2)}, u32[]{:S(2)}) %collective-permute-start.5) | collective-permute-done | bytes 786464 | tf_op jit(solution)/shard_map/ppermute | solution.py:139
  200.8 1.0 constant_dynamic-update-slice_fusion
  201.9 0.1 copy-done.2
  202.0 4.1 %fusion.3 = bf16[1536,1536]{1,0:T(8,128)(2,1)S(1)} fusion(s32[]{:T(128)S(6)} %select_n.151, bf16[1536,1536]{1,0:T(8,128)(2,1)} %bitcast.117), kind=kLoop, calls=%fused_computation.7 | loop fusion | flops 9437184 | bytes 9437188 | tf_op jit(solution)/shard_map/concatenate | solution.py:122
  206.1 1.8 fusion.12
  208.0 1.8 fusion.13
  209.8 3.1 %fusion.14 = f32[2,32,16,1536]{3,2,1,0:T(8,128)S(1)} fusion(bf16[1536,1536]{1,0:T(8,128)(2,1)} %copy-done, bf16[2,32,16,384]{3,2,1,0:T(8,128)(2,1)S(1)} %copy-done.4, bf16[16,384]{1,0:T(8,128)(2,1)S(1)} %get-tuple-element.13), kind=kOutput, calls=%fused_computation.26 | convolution fusion | flops 1208352768 | bytes 8269824 | tf_op jit(solution)/shard_map/rstj,ij->rsti/dot_general | solution.py:150
  212.9 6.7 %fusion.6 = bf16[2,1,32,16,1536]{4,3,2,1,0:T(8,128)(2,1)} fusion(f32[2,32,16,1536]{3,2,1,0:T(8,128)S(1)} %fusion.12, f32[2,32,16,1536]{3,2,1,0:T(8,128)S(1)} %fusion.14, f32[2,32,16,1536]{3,2,1,0:T(8,128)S(1)} %fusion.13, bf16[2,32,16,1536]{3,2,1,0:T(8,128)(2,1)} %constant_dynamic-update-slice_fusion, bf16[1536,1536]{1,0:T(8,128)(2,1)} %copy-done, ...), kind=kOutput, calls=%fused_computation.10 | convolution fusion | flops 1217789952 | bytes 27144192 | tf_op jit(solution)/shard_map/rstj,ij->rsti/dot_general | solution.py:150
  (21 shorter events, 0.1 us)
Async XLA Ops:
  6.5 26.0 %copy-start.1 = (bf16[2,66,16,384]{3,2,1,0:T(8,128)(2,1)S(1)}, bf16[2,66,16,384]{3,2,1,0:T(8,128)(2,1)}, u32[]{:S(2)}) copy-start(bf16[2,66,16,384]{3,2,1,0:T(8,128)(2,1)} %param.7) | copy-start | bytes 4866052
  6.5 195.3 %all-gather.3.cloned.1.call-start = ((), (), s32[]{:S(2)}) async-start(), calls=%async_computation | async-start | bytes 5898240 | tf_op jit(solution)/shard_map/all_gather | solution.py:119
  9.0 23.5 %collective-permute-start = (bf16[2,66,4,384]{3,2,1,0:T(4,128)(2,1)S(1)}, bf16[2,66,4,384]{3,2,1,0:T(4,128)(2,1)S(1)}, u32[]{:S(2)}, u32[]{:S(2)}) collective-permute-start(bf16[2,66,4,384]{3,2,1,0:T(4,128)(2,1)S(1)} %get-tuple-element.9), channel_id=1, source_target_pairs={{0,4},{4,8},{8,12},{1,5},{5,9},{9,13},{2,6},{6,10},{10,14},{3,7},{... | collective-permute-start | bytes 1216520 | tf_op jit(solution)/shard_map/ppermute | solution.py:19
  12.5 20.1 %collective-permute-start.1 = (bf16[2,66,4,384]{3,2,1,0:T(4,128)(2,1)S(1)}, bf16[2,66,4,384]{3,2,1,0:T(4,128)(2,1)S(1)}, u32[]{:S(2)}, u32[]{:S(2)}) collective-permute-start(bf16[2,66,4,384]{3,2,1,0:T(4,128)(2,1)S(1)} %get-tuple-element.10), channel_id=1, source_target_pairs={{4,0},{8,4},{12,8},{5,1},{9,5},{13,9},{6,2},{10,6},{14,10},{7,3},{... | collective-permute-start | bytes 1216520 | tf_op jit(solution)/shard_map/ppermute | solution.py:21
  62.3 88.7 %collective-permute-start.2 = (bf16[2,32,16,384]{3,2,1,0:T(8,128)(2,1)}, bf16[2,32,16,384]{3,2,1,0:T(8,128)(2,1)S(1)}, u32[]{:S(2)}, u32[]{:S(2)}) collective-permute-start(bf16[2,32,16,384]{3,2,1,0:T(8,128)(2,1)} %fusion.7), channel_id=1, source_target_pairs={{0,0},{1,4},{2,8},{3,12},{4,1},{5,5},{6,9},{7,13},{8,2},{9,6},{10,... | collective-permute-start | bytes 2359304 | tf_op jit(solution)/shard_map/ppermute | solution.py:139
  92.0 62.0 %collective-permute-start.3 = (bf16[2,32,16,384]{3,2,1,0:T(8,128)(2,1)}, bf16[2,32,16,384]{3,2,1,0:T(8,128)(2,1)S(1)}, u32[]{:S(2)}, u32[]{:S(2)}) collective-permute-start(bf16[2,32,16,384]{3,2,1,0:T(8,128)(2,1)} %fusion.8), channel_id=1, source_target_pairs={{0,4},{1,8},{2,12},{3,0},{4,5},{5,9},{6,13},{7,1},{8,6},{9,10},{10... | collective-permute-start | bytes 2359304 | tf_op jit(solution)/shard_map/ppermute | solution.py:139
  145.9 5.0 %copy-start.5 = (s32[16,1536]{1,0:T(8,128)S(1)}, s32[16,1536]{1,0:T(8,128)}, u32[]{:S(2)}) copy-start(s32[16,1536]{1,0:T(8,128)} %param.11) | copy-start | bytes 294916
  147.1 43.7 %collective-permute-start.4 = (bf16[2,32,16,384]{3,2,1,0:T(8,128)(2,1)}, bf16[2,32,16,384]{3,2,1,0:T(8,128)(2,1)S(1)}, u32[]{:S(2)}, u32[]{:S(2)}) collective-permute-start(bf16[2,32,16,384]{3,2,1,0:T(8,128)(2,1)} %fusion.9), channel_id=1, source_target_pairs={{0,8},{1,12},{2,0},{3,4},{4,9},{5,13},{6,1},{7,5},{8,10},{9,14},{1... | collective-permute-start | bytes 2359304 | tf_op jit(solution)/shard_map/ppermute | solution.py:139
  148.7 52.2 %collective-permute-start.5 = (bf16[2,32,16,384]{3,2,1,0:T(8,128)(2,1)}, bf16[2,32,16,384]{3,2,1,0:T(8,128)(2,1)S(1)}, u32[]{:S(2)}, u32[]{:S(2)}) collective-permute-start(bf16[2,32,16,384]{3,2,1,0:T(8,128)(2,1)} %fusion.10), channel_id=1, source_target_pairs={{0,12},{1,0},{2,4},{3,8},{4,13},{5,1},{6,5},{7,9},{8,14},{9,2},{10... | collective-permute-start | bytes 2359304 | tf_op jit(solution)/shard_map/ppermute | solution.py:139
  151.0 4.0 %copy-start.3 = (bf16[2,32,16,384]{3,2,1,0:T(8,128)(2,1)}, bf16[2,32,16,384]{3,2,1,0:T(8,128)(2,1)S(1)}, u32[]{:S(2)}) copy-start(bf16[2,32,16,384]{3,2,1,0:T(8,128)(2,1)S(1)} %collective-permute-done.2) | copy-start | bytes 2359300
  200.8 1.2 copy-start.2
  206.1 3.7 %copy-start = (bf16[1536,1536]{1,0:T(8,128)(2,1)}, bf16[1536,1536]{1,0:T(8,128)(2,1)S(1)}, u32[]{:S(2)}) copy-start(bf16[1536,1536]{1,0:T(8,128)(2,1)S(1)} %fusion.3) | copy-start | bytes 14155780
  208.0 1.9 copy-start.4
Sparse Core Ops, SparseCore 0:
  8.9 37.5 all-gather.2

commit v4 on v3

--- a/solution.py
+++ b/solution.py
@@ -44,15 +44,8 @@
 
 
 def convolve_class(rows, taps, count, length):
-    real_part = jnp.zeros(rows.shape[1:2] + (length,) + rows.shape[3:], jnp.float32)
-    imag_part = jnp.zeros_like(real_part)
-    for offset in range(2 * REACH + 1):
-        shifted = lax.slice_in_dim(rows, 2 * REACH - offset, 2 * REACH - offset + length, axis=2)
-        real_part = real_part + taps[0, offset] * shifted[0] - taps[1, offset] * shifted[1]
-        imag_part = imag_part + taps[0, offset] * shifted[1] + taps[1, offset] * shifted[0]
-    out = jnp.stack([real_part, imag_part])
-    live = lax.broadcasted_iota(jnp.int32, out.shape, 1) < count
-    return jnp.where(live, out, 0.0).astype(jnp.bfloat16)
+    live = (jnp.arange(rows.shape[1], dtype=jnp.int32) < count).astype(jnp.float32)
+    return convolve(rows, taps[:, None, :] * live[None, :, None], length)
 
 
 def to_slots(per_baseline, class_counts):
@@ -119,7 +112,8 @@
     panel = lax.all_gather(filter_panels[0], "freq", axis=0, tiled=True)
     if q == 1:
         shift = ((a + 1) % nf) * f_blk
-        panel = lax.dynamic_slice_in_dim(jnp.concatenate([panel, panel], axis=1), shift, channels, axis=1)
+        panel = jnp.concatenate([panel, panel], axis=1)
+        panel = lax.dynamic_slice_in_dim(panel, shift, channels, axis=1)
 
     c_own = a
     u_src = (a % q) * nf + b

time: 228 us -> 152 us (0.67)
  other arithmetic: 120 us -> 32.3 us
  waiting for transfers between devices: 45.6 us -> 61.7 us
  local copies, waits for them, and re-layouts: 12.9 us -> 10.3 us
    add x4 -> x0, other arithmetic: 52.2 us -> none  [convolve_class(): imag_part + taps[0, offset] * shifted[1] + taps[1, offset] * shifted[0]]
    sub x4 -> x0, other arithmetic: 52.2 us -> none  [convolve_class(): real_part + taps[0, offset] * shifted[0] - taps[1, offset] * shifted[1]]
    another operation x1 -> x13, other arithmetic: 0.83 us -> 21.5 us
    ppermute x4, waiting for transfers between devices: 44.9 us -> 60.9 us  [shards(): got = lax.ppermute(chunk, ('tm', 'freq'), perm)]
    slice x4 -> x0, local copies, waits for them, and re-layouts: 2.88 us -> none  [convolve_class(): taps[0, offset] * shifted[0]]
    lt x4 -> x0, other arithmetic: 2.53 us -> none  [convolve_class(): live = lax.broadcasted_iota(jnp.int32, out.shape, 1) < count]
  transfers between devices with their start and end apart: 7 -> 7, of which waited for: 2 -> 4; matrix products, arithmetic and copies ran while one was open for 57% -> 25% of each run, Pallas kernels for 0% -> 0%
where the time goes in v4:
time: 152 us
  waiting for transfers between devices  61.7 us (41%)
  other arithmetic  32.3 us (21%)
  between operations  21.3 us (14%)
  matrix products  13.4 us (9%)
  starting transfers between devices  13 us (9%)
  local copies, waits for them, and re-layouts  10.3 us (7%)
    ppermute x4, waiting for transfers between devices, shards(): got = lax.ppermute(chunk, ('tm', 'freq'), perm)  60.9 us
    another operation x9, other arithmetic  17.6 us
    dot_general x4, matrix products, shards(): jnp.einsum('rstj,ij->rsti', weighted, cols, preferred_element_type=jnp.fl...  13.4 us
    ppermute x4, starting transfers between devices, shards(): got = lax.ppermute(chunk, ('tm', 'freq'), perm)  7.13 us
    concatenate x1, other arithmetic, shards(): panel = jnp.concatenate([panel, panel], axis=1)  4.15 us
    another operation x4, other arithmetic, convolve(): return jnp.stack([real_part, imag_part]).astype(jnp.bfloat16)  3.93 us
    dynamic_update_slice x4, local copies, waits for them, and re-layouts, shards(): lax.dynamic_update_slice_in_dim(slotted, got, b_src * f_blk, axis=3)  3.91 us
    ppermute x1, starting transfers between devices, extended(): lax.ppermute(tail, axis, [(i, (i + 1) % count) for i in range(ends)])  3.48 us
  transfers between devices with their start and end apart: 7, of which 4 were waited for; matrix products, arithmetic and copies ran while one was open for 25% of the time, Pallas kernels for 0%

profile of v4, /device:TPU:14, one launch (start us, length us, event | category | flops | bytes accessed | tf_op | source)
XLA Modules:
  0.0 152.0 jit_solution(951673988614990349)
XLA Ops:
  6.5 0.7 all-gather.3.cloned.1.call-update
  7.3 1.7 %fusion.163 = (bf16[2,66,4,384]{3,2,1,0:T(4,128)(2,1)S(1)}, bf16[2,66,4,384]{3,2,1,0:T(4,128)(2,1)S(1)}) fusion(bf16[2,66,16,384]{3,2,1,0:T(8,128)(2,1)} %param.7), kind=kLoop, calls=%fused_computation.419 | loop fusion | bytes 1622016 | tf_op jit(solution)/shard_map/slice | solution.py:16
  9.0 3.5 %collective-permute-start = (bf16[2,66,4,384]{3,2,1,0:T(4,128)(2,1)S(1)}, bf16[2,66,4,384]{3,2,1,0:T(4,128)(2,1)S(1)}, u32[]{:S(2)}, u32[]{:S(2)}) collective-permute-start(bf16[2,66,4,384]{3,2,1,0:T(4,128)(2,1)S(1)} %get-tuple-element.9), channel_id=1, source_target_pairs={{0,4},{4,8},{8,12},{1,5},{5,9},{9,13},{2,6},{6,10},{10,14},{3,7},{... | collective-permute-start | bytes 1216520 | tf_op jit(solution)/shard_map/ppermute | solution.py:19
  12.5 2.4 %collective-permute-start.1 = (bf16[2,66,4,384]{3,2,1,0:T(4,128)(2,1)S(1)}, bf16[2,66,4,384]{3,2,1,0:T(4,128)(2,1)S(1)}, u32[]{:S(2)}, u32[]{:S(2)}) collective-permute-start(bf16[2,66,4,384]{3,2,1,0:T(4,128)(2,1)S(1)} %get-tuple-element.10), channel_id=1, source_target_pairs={{4,0},{8,4},{12,8},{5,1},{9,5},{13,9},{6,2},{10,6},{14,10},{7,3},{... | collective-permute-start | bytes 1216520 | tf_op jit(solution)/shard_map/ppermute | solution.py:21
  14.9 0.8 reduce-window.9
  15.7 0.7 bitcast_subtract_fusion
  16.4 1.5 fusion.164
  23.0 0.7 compare_convert_fusion.4
  23.7 0.7 broadcast_multiply_fusion.4
  24.4 0.6 compare_convert_fusion.1
  25.1 0.7 compare_convert_fusion.3
  25.7 0.6 compare_convert_fusion.2
  26.4 0.6 compare_convert_fusion
  27.0 0.1 broadcast_multiply_fusion
  29.9 1.7 %fusion.5 = bf16[2,98,24,384]{3,2,1,0:T(8,128)(2,1)S(1)} fusion(bf16[2,66,4,384]{3,2,1,0:T(4,128)(2,1)S(1)} %collective-permute-done.1, bf16[2,66,16,384]{3,2,1,0:T(8,128)(2,1)S(1)} %copy-done.1, bf16[2,66,4,384]{3,2,1,0:T(4,128)(2,1)S(1)} %collective-permute-done), kind=kLoop, calls=%fused_computation.9 | loop fusion | flops 18063360 | bytes 6045696 | tf_op jit(solution)/shard_map/concatenate | solution.py:17
  31.6 0.7 constant_dynamic-slice_fusion
  32.3 2.1 %fusion.158 = bf16[1,32,16,384]{3,2,1,0:T(8,128)(2,1)S(1)} fusion(f32[32]{0:T(128)S(1)} %get-tuple-element.52, f32[32]{0:T(128)S(1)} %get-tuple-element.53, f32[32]{0:T(128)S(1)} %get-tuple-element.54, f32[32]{0:T(128)S(1)} %get-tuple-element.55, f32[32]{0:T(128)S(1)} %get-tuple-element.56, f32[32]{0:T(128)S(1)} %get-tuple-element.57, ...), kind=kLoop, calls=%fused_computation.314 | loop fusion | flops 10616832 | bytes 7473408 | tf_op jit(solution)/shard_map/convert.6
  34.4 2.1 %fusion.157 = bf16[1,32,16,384]{3,2,1,0:T(8,128)(2,1)S(1)} fusion(f32[32]{0:T(128)S(1)} %get-tuple-element.52, f32[32]{0:T(128)S(1)} %get-tuple-element.53, f32[32]{0:T(128)S(1)} %get-tuple-element.54, f32[32]{0:T(128)S(1)} %get-tuple-element.55, f32[32]{0:T(128)S(1)} %get-tuple-element.56, f32[32]{0:T(128)S(1)} %get-tuple-element.57, ...), kind=kLoop, calls=%fused_computation.313 | loop fusion | flops 10616832 | bytes 7473408 | tf_op jit(solution)/shard_map/convert.7
  36.5 1.0 pad_maximum_fusion
  37.5 2.3 %collective-permute-start.2 = (bf16[2,32,16,384]{3,2,1,0:T(8,128)(2,1)}, bf16[2,32,16,384]{3,2,1,0:T(8,128)(2,1)S(1)}, u32[]{:S(2)}, u32[]{:S(2)}) collective-permute-start(bf16[2,32,16,384]{3,2,1,0:T(8,128)(2,1)} %pad_maximum_fusion), channel_id=1, source_target_pairs={{0,0},{1,4},{2,8},{3,12},{4,1},{5,5},{6,9},{7,13},{8,2},{9,6},{10,... | collective-permute-start | bytes 2359304 | tf_op jit(solution)/shard_map/ppermute | solution.py:133
  39.8 2.1 %fusion.154 = bf16[1,32,16,384]{3,2,1,0:T(8,128)(2,1)S(1)} fusion(f32[32]{0:T(128)S(1)} %get-tuple-element.70, f32[32]{0:T(128)S(1)} %get-tuple-element.71, f32[32]{0:T(128)S(1)} %get-tuple-element.72, f32[32]{0:T(128)S(1)} %get-tuple-element.73, f32[32]{0:T(128)S(1)} %get-tuple-element.74, f32[32]{0:T(128)S(1)} %get-tuple-element.75, ...), kind=kLoop, calls=%fused_computation.310 | loop fusion | flops 10616832 | bytes 7473408 | tf_op jit(solution)/shard_map/convert.2
  41.9 2.1 %fusion.153 = bf16[1,32,16,384]{3,2,1,0:T(8,128)(2,1)S(1)} fusion(f32[32]{0:T(128)S(1)} %get-tuple-element.70, f32[32]{0:T(128)S(1)} %get-tuple-element.71, f32[32]{0:T(128)S(1)} %get-tuple-element.72, f32[32]{0:T(128)S(1)} %get-tuple-element.73, f32[32]{0:T(128)S(1)} %get-tuple-element.74, f32[32]{0:T(128)S(1)} %get-tuple-element.75, ...), kind=kLoop, calls=%fused_computation.309 | loop fusion | flops 10616832 | bytes 7473408 | tf_op jit(solution)/shard_map/convert.3
  44.0 2.1 %fusion.152 = bf16[1,32,16,384]{3,2,1,0:T(8,128)(2,1)S(1)} fusion(f32[32]{0:T(128)S(1)} %get-tuple-element.16, f32[32]{0:T(128)S(1)} %get-tuple-element.17, f32[32]{0:T(128)S(1)} %get-tuple-element.18, f32[32]{0:T(128)S(1)} %get-tuple-element.19, f32[32]{0:T(128)S(1)} %get-tuple-element.20, f32[32]{0:T(128)S(1)} %get-tuple-element.21, ...), kind=kLoop, calls=%fused_computation.308 | loop fusion | flops 10616832 | bytes 7473408 | tf_op jit(solution)/shard_map/convert
  46.1 2.1 %fusion.151 = bf16[1,32,16,384]{3,2,1,0:T(8,128)(2,1)S(1)} fusion(f32[32]{0:T(128)S(1)} %get-tuple-element.16, f32[32]{0:T(128)S(1)} %get-tuple-element.17, f32[32]{0:T(128)S(1)} %get-tuple-element.18, f32[32]{0:T(128)S(1)} %get-tuple-element.19, f32[32]{0:T(128)S(1)} %get-tuple-element.20, f32[32]{0:T(128)S(1)} %get-tuple-element.21, ...), kind=kLoop, calls=%fused_computation.307 | loop fusion | flops 10616832 | bytes 7473408 | tf_op jit(solution)/shard_map/convert.1
  48.2 2.1 %fusion.156 = bf16[1,32,16,384]{3,2,1,0:T(8,128)(2,1)S(1)} fusion(f32[32]{0:T(128)S(1)} %get-tuple-element.34, f32[32]{0:T(128)S(1)} %get-tuple-element.35, f32[32]{0:T(128)S(1)} %get-tuple-element.36, f32[32]{0:T(128)S(1)} %get-tuple-element.37, f32[32]{0:T(128)S(1)} %get-tuple-element.38, f32[32]{0:T(128)S(1)} %get-tuple-element.39, ...), kind=kLoop, calls=%fused_computation.312 | loop fusion | flops 10616832 | bytes 7473408 | tf_op jit(solution)/shard_map/convert.4
  50.3 2.1 %fusion.155 = bf16[1,32,16,384]{3,2,1,0:T(8,128)(2,1)S(1)} fusion(f32[32]{0:T(128)S(1)} %get-tuple-element.34, f32[32]{0:T(128)S(1)} %get-tuple-element.35, f32[32]{0:T(128)S(1)} %get-tuple-element.36, f32[32]{0:T(128)S(1)} %get-tuple-element.37, f32[32]{0:T(128)S(1)} %get-tuple-element.38, f32[32]{0:T(128)S(1)} %get-tuple-element.39, ...), kind=kLoop, calls=%fused_computation.311 | loop fusion | flops 10616832 | bytes 7473408 | tf_op jit(solution)/shard_map/convert.5
  52.4 1.0 pad_maximum_fusion.1
  53.4 2.0 %collective-permute-start.3 = (bf16[2,32,16,384]{3,2,1,0:T(8,128)(2,1)}, bf16[2,32,16,384]{3,2,1,0:T(8,128)(2,1)S(1)}, u32[]{:S(2)}, u32[]{:S(2)}) collective-permute-start(bf16[2,32,16,384]{3,2,1,0:T(8,128)(2,1)} %pad_maximum_fusion.1), channel_id=1, source_target_pairs={{0,4},{1,8},{2,12},{3,0},{4,5},{5,9},{6,13},{7,1},{8,6},{9,10},{10... | collective-permute-start | bytes 2359304 | tf_op jit(solution)/shard_map/ppermute | solution.py:133
  55.4 1.0 pad_maximum_fusion.2
  56.4 0.5 collective-permute-start.4
  56.9 1.0 pad_maximum_fusion.3
  57.9 2.3 %collective-permute-start.5 = (bf16[2,32,16,384]{3,2,1,0:T(8,128)(2,1)}, bf16[2,32,16,384]{3,2,1,0:T(8,128)(2,1)S(1)}, u32[]{:S(2)}, u32[]{:S(2)}) collective-permute-start(bf16[2,32,16,384]{3,2,1,0:T(8,128)(2,1)} %pad_maximum_fusion.3), channel_id=1, source_target_pairs={{0,12},{1,0},{2,4},{3,8},{4,13},{5,1},{6,5},{7,9},{8,14},{9,2},{10... | collective-permute-start | bytes 2359304 | tf_op jit(solution)/shard_map/ppermute | solution.py:133
  60.2 33.7 %collective-permute-done.2 = bf16[2,32,16,384]{3,2,1,0:T(8,128)(2,1)S(1)} collective-permute-done((bf16[2,32,16,384]{3,2,1,0:T(8,128)(2,1)}, bf16[2,32,16,384]{3,2,1,0:T(8,128)(2,1)S(1)}, u32[]{:S(2)}, u32[]{:S(2)}) %collective-permute-start.2) | collective-permute-done | bytes 786464 | tf_op jit(solution)/shard_map/ppermute | solution.py:133
  93.9 2.0 %broadcast_in_dim.4 = bf16[2,32,16,1536]{3,2,1,0:T(8,128)(2,1)} broadcast(bf16[]{:T(256)} %constant.99.clone.1), dimensions={} | broadcast | bytes 3145730 | tf_op jit(solution)/shard_map/broadcast_in_dim | solution.py:146
  95.9 1.0 constant_dynamic-update-slice_fusion.3
  96.9 12.9 %collective-permute-done.3 = bf16[2,32,16,384]{3,2,1,0:T(8,128)(2,1)S(1)} collective-permute-done((bf16[2,32,16,384]{3,2,1,0:T(8,128)(2,1)}, bf16[2,32,16,384]{3,2,1,0:T(8,128)(2,1)S(1)}, u32[]{:S(2)}, u32[]{:S(2)}) %collective-permute-start.3) | collective-permute-done | bytes 786464 | tf_op jit(solution)/shard_map/ppermute | solution.py:133
  109.8 1.0 constant_dynamic-update-slice_fusion.2
  110.7 13.7 %collective-permute-done.4 = bf16[2,32,16,384]{3,2,1,0:T(8,128)(2,1)S(1)} collective-permute-done((bf16[2,32,16,384]{3,2,1,0:T(8,128)(2,1)}, bf16[2,32,16,384]{3,2,1,0:T(8,128)(2,1)S(1)}, u32[]{:S(2)}, u32[]{:S(2)}) %collective-permute-start.4) | collective-permute-done | bytes 786464 | tf_op jit(solution)/shard_map/ppermute | solution.py:133
  124.4 1.0 constant_dynamic-update-slice_fusion.1
  125.3 0.8 collective-permute-done.5
  126.1 1.0 constant_dynamic-update-slice_fusion
  127.1 0.1 copy-done.2
  127.3 4.1 %fusion.3 = bf16[1536,1536]{1,0:T(8,128)(2,1)S(1)} fusion(s32[]{:T(128)S(6)} %select_n.134, bf16[1536,1536]{1,0:T(8,128)(2,1)} %bitcast.189), kind=kLoop, calls=%fused_computation.7 | loop fusion | flops 9437184 | bytes 9437188 | tf_op jit(solution)/shard_map/concatenate | solution.py:115
  131.4 1.8 %fusion.8 = f32[2,32,16,1536]{3,2,1,0:T(8,128)S(1)} fusion(bf16[1536,1536]{1,0:T(8,128)(2,1)S(1)} %fusion.3, bf16[2,32,16,384]{3,2,1,0:T(8,128)(2,1)S(1)} %collective-permute-done.4, bf16[16,384]{1,0:T(8,128)(2,1)S(1)} %get-tuple-element.14), kind=kOutput, calls=%fused_computation.14 | convolution fusion | flops 1208352768 | bytes 8269824 | tf_op jit(solution)/shard_map/rstj,ij->rsti/dot_general | solution.py:144
  133.3 0.3 copy-done
  133.5 1.8 %fusion.9 = f32[2,32,16,1536]{3,2,1,0:T(8,128)S(1)} fusion(bf16[1536,1536]{1,0:T(8,128)(2,1)S(1)} %fusion.3, bf16[2,32,16,384]{3,2,1,0:T(8,128)(2,1)S(1)} %collective-permute-done.3, bf16[16,384]{1,0:T(8,128)(2,1)S(1)} %get-tuple-element.12), kind=kOutput, calls=%fused_computation.16 | convolution fusion | flops 1208352768 | bytes 8269824 | tf_op jit(solution)/shard_map/rstj,ij->rsti/dot_general | solution.py:144
  135.4 3.1 %fusion.10 = f32[2,32,16,1536]{3,2,1,0:T(8,128)S(1)} fusion(bf16[1536,1536]{1,0:T(8,128)(2,1)} %copy-done, bf16[2,32,16,384]{3,2,1,0:T(8,128)(2,1)S(1)} %copy-done.4, bf16[16,384]{1,0:T(8,128)(2,1)S(1)} %get-tuple-element.13), kind=kOutput, calls=%fused_computation.18 | convolution fusion | flops 1208352768 | bytes 8269824 | tf_op jit(solution)/shard_map/rstj,ij->rsti/dot_general | solution.py:144
  138.5 6.7 %fusion.6 = bf16[2,1,32,16,1536]{4,3,2,1,0:T(8,128)(2,1)} fusion(f32[2,32,16,1536]{3,2,1,0:T(8,128)S(1)} %fusion.8, f32[2,32,16,1536]{3,2,1,0:T(8,128)S(1)} %fusion.10, f32[2,32,16,1536]{3,2,1,0:T(8,128)S(1)} %fusion.9, bf16[2,32,16,1536]{3,2,1,0:T(8,128)(2,1)} %constant_dynamic-update-slice_fusion, bf16[1536,1536]{1,0:T(8,128)(2,1)} %copy-done, ...), kind=kOutput, calls=%fused_computation.10 | convolution fusion | flops 1217789952 | bytes 27144192 | tf_op jit(solution)/shard_map/rstj,ij->rsti/dot_general | solution.py:144
  (25 shorter events, 0.3 us)
Async XLA Ops:
  6.5 23.4 %copy-start.1 = (bf16[2,66,16,384]{3,2,1,0:T(8,128)(2,1)S(1)}, bf16[2,66,16,384]{3,2,1,0:T(8,128)(2,1)}, u32[]{:S(2)}) copy-start(bf16[2,66,16,384]{3,2,1,0:T(8,128)(2,1)} %param.7) | copy-start | bytes 4866052
  6.5 120.6 %all-gather.3.cloned.1.call-start = ((), (), s32[]{:S(2)}) async-start(), calls=%async_computation | async-start | bytes 5898240 | tf_op jit(solution)/shard_map/all_gather | solution.py:112
  9.0 20.9 %collective-permute-start = (bf16[2,66,4,384]{3,2,1,0:T(4,128)(2,1)S(1)}, bf16[2,66,4,384]{3,2,1,0:T(4,128)(2,1)S(1)}, u32[]{:S(2)}, u32[]{:S(2)}) collective-permute-start(bf16[2,66,4,384]{3,2,1,0:T(4,128)(2,1)S(1)} %get-tuple-element.9), channel_id=1, source_target_pairs={{0,4},{4,8},{8,12},{1,5},{5,9},{9,13},{2,6},{6,10},{10,14},{3,7},{... | collective-permute-start | bytes 1216520 | tf_op jit(solution)/shard_map/ppermute | solution.py:19
  12.5 17.4 %collective-permute-start.1 = (bf16[2,66,4,384]{3,2,1,0:T(4,128)(2,1)S(1)}, bf16[2,66,4,384]{3,2,1,0:T(4,128)(2,1)S(1)}, u32[]{:S(2)}, u32[]{:S(2)}) collective-permute-start(bf16[2,66,4,384]{3,2,1,0:T(4,128)(2,1)S(1)} %get-tuple-element.10), channel_id=1, source_target_pairs={{4,0},{8,4},{12,8},{5,1},{9,5},{13,9},{6,2},{10,6},{14,10},{7,3},{... | collective-permute-start | bytes 1216520 | tf_op jit(solution)/shard_map/ppermute | solution.py:21
  37.5 56.4 %collective-permute-start.2 = (bf16[2,32,16,384]{3,2,1,0:T(8,128)(2,1)}, bf16[2,32,16,384]{3,2,1,0:T(8,128)(2,1)S(1)}, u32[]{:S(2)}, u32[]{:S(2)}) collective-permute-start(bf16[2,32,16,384]{3,2,1,0:T(8,128)(2,1)} %pad_maximum_fusion), channel_id=1, source_target_pairs={{0,0},{1,4},{2,8},{3,12},{4,1},{5,5},{6,9},{7,13},{8,2},{9,6},{10,... | collective-permute-start | bytes 2359304 | tf_op jit(solution)/shard_map/ppermute | solution.py:133
  52.4 7.8 %copy-start.5 = (s32[16,1536]{1,0:T(8,128)S(1)}, s32[16,1536]{1,0:T(8,128)}, u32[]{:S(2)}) copy-start(s32[16,1536]{1,0:T(8,128)} %param.11) | copy-start | bytes 294916
  53.4 56.3 %collective-permute-start.3 = (bf16[2,32,16,384]{3,2,1,0:T(8,128)(2,1)}, bf16[2,32,16,384]{3,2,1,0:T(8,128)(2,1)S(1)}, u32[]{:S(2)}, u32[]{:S(2)}) collective-permute-start(bf16[2,32,16,384]{3,2,1,0:T(8,128)(2,1)} %pad_maximum_fusion.1), channel_id=1, source_target_pairs={{0,4},{1,8},{2,12},{3,0},{4,5},{5,9},{6,13},{7,1},{8,6},{9,10},{10... | collective-permute-start | bytes 2359304 | tf_op jit(solution)/shard_map/ppermute | solution.py:133
  56.4 68.0 %collective-permute-start.4 = (bf16[2,32,16,384]{3,2,1,0:T(8,128)(2,1)}, bf16[2,32,16,384]{3,2,1,0:T(8,128)(2,1)S(1)}, u32[]{:S(2)}, u32[]{:S(2)}) collective-permute-start(bf16[2,32,16,384]{3,2,1,0:T(8,128)(2,1)} %pad_maximum_fusion.2), channel_id=1, source_target_pairs={{0,8},{1,12},{2,0},{3,4},{4,9},{5,13},{6,1},{7,5},{8,10},{9,14},{1... | collective-permute-start | bytes 2359304 | tf_op jit(solution)/shard_map/ppermute | solution.py:133
  57.9 68.2 %collective-permute-start.5 = (bf16[2,32,16,384]{3,2,1,0:T(8,128)(2,1)}, bf16[2,32,16,384]{3,2,1,0:T(8,128)(2,1)S(1)}, u32[]{:S(2)}, u32[]{:S(2)}) collective-permute-start(bf16[2,32,16,384]{3,2,1,0:T(8,128)(2,1)} %pad_maximum_fusion.3), channel_id=1, source_target_pairs={{0,12},{1,0},{2,4},{3,8},{4,13},{5,1},{6,5},{7,9},{8,14},{9,2},{10... | collective-permute-start | bytes 2359304 | tf_op jit(solution)/shard_map/ppermute | solution.py:133
  93.9 31.4 %copy-start.3 = (bf16[2,32,16,384]{3,2,1,0:T(8,128)(2,1)}, bf16[2,32,16,384]{3,2,1,0:T(8,128)(2,1)S(1)}, u32[]{:S(2)}) copy-start(bf16[2,32,16,384]{3,2,1,0:T(8,128)(2,1)S(1)} %collective-permute-done.2) | copy-start | bytes 2359300
  126.1 1.2 copy-start.2
  131.4 2.1 %copy-start = (bf16[1536,1536]{1,0:T(8,128)(2,1)}, bf16[1536,1536]{1,0:T(8,128)(2,1)S(1)}, u32[]{:S(2)}) copy-start(bf16[1536,1536]{1,0:T(8,128)(2,1)S(1)} %fusion.3) | copy-start | bytes 14155780
  133.5 1.8 %copy-start.4 = (bf16[2,32,16,384]{3,2,1,0:T(8,128)(2,1)S(1)}, bf16[2,32,16,384]{3,2,1,0:T(8,128)(2,1)}, u32[]{:S(2)}) copy-start(bf16[2,32,16,384]{3,2,1,0:T(8,128)(2,1)} %copy-done.3) | copy-start | bytes 2359300
Sparse Core Ops, SparseCore 0:
  8.9 39.5 all-gather.2

commit v5 on v4

--- a/solution.py
+++ b/solution.py
@@ -109,7 +109,28 @@
     padded = extended(visibilities, (("tm", 2),), REACH)
     padded = jnp.pad(padded, ((0, 0), (0, SLOTS), (0, 0), (0, 0)))
 
-    panel = lax.all_gather(filter_panels[0], "freq", axis=0, tiled=True)
+    if q == 1 and nf & (nf - 1) == 0:
+        blocks = filter_panels[0][None]
+        step = nf // 2
+        while step >= 1:
+            perm = [(f, f ^ step) for f in range(nf)]
+            blocks = jnp.concatenate([blocks, lax.ppermute(blocks, "freq", perm)], axis=0)
+            step //= 2
+        codes = [0]
+        step = nf // 2
+        while step >= 1:
+            codes = codes + [x ^ step for x in codes]
+            step //= 2
+        where = {code: m for m, code in enumerate(codes)}
+        rows = []
+        for k in range(nf):
+            pick = sum(
+                jnp.where((k ^ b) == code, m, 0) for code, m in where.items()
+            )
+            rows.append(lax.dynamic_index_in_dim(blocks, pick, 0, keepdims=False))
+        panel = jnp.concatenate(rows, axis=0)
+    else:
+        panel = lax.all_gather(filter_panels[0], "freq", axis=0, tiled=True)
     if q == 1:
         shift = ((a + 1) % nf) * f_blk
         panel = jnp.concatenate([panel, panel], axis=1)

time: 152 us -> 155 us (1.020)
  the two profiles are of different devices: /device:TPU:14 before, /device:TPU:17 now
where the time goes in v5:
time: 155 us
  waiting for transfers between devices  51.2 us (33%)
  other arithmetic  49.7 us (32%)
  local copies, waits for them, and re-layouts  16.1 us (10%)
  starting transfers between devices  15.7 us (10%)
  matrix products  13.9 us (9%)
  between operations  8.17 us (5%)
    ppermute x4, waiting for transfers between devices, shards(): got = lax.ppermute(chunk, ('tm', 'freq'), perm)  51.2 us
    concatenate x1, other arithmetic, shards(): panel = jnp.concatenate([panel, panel], axis=1)  18 us
    another operation x9, other arithmetic  17.5 us
    dot_general x4, matrix products, shards(): jnp.einsum('rstj,ij->rsti', weighted, cols, preferred_element_type=jnp.fl...  13.9 us
    ppermute x4, starting transfers between devices, shards(): got = lax.ppermute(chunk, ('tm', 'freq'), perm)  7.7 us
    dynamic_update_slice x4, local copies, waits for them, and re-layouts, shards(): lax.dynamic_update_slice_in_dim(slotted, got, b_src * f_blk, axis=3)  5.04 us
    another operation x4, other arithmetic, convolve(): return jnp.stack([real_part, imag_part]).astype(jnp.bfloat16)  3.95 us
    ppermute x1, starting transfers between devices, extended(): lax.ppermute(tail, axis, [(i, (i + 1) % count) for i in range(ends)])  3.2 us
  transfers between devices with their start and end apart: 8, of which 2 were waited for; matrix products, arithmetic and copies ran while one was open for 28% of the time, Pallas kernels for 0%

profile of v5, /device:TPU:17, one launch (start us, length us, event | category | flops | bytes accessed | tf_op | source)
XLA Modules:
  0.0 154.8 jit_solution(17722309726596058290)
XLA Ops:
  0.0 1.7 %fusion.169 = (bf16[2,66,4,384]{3,2,1,0:T(4,128)(2,1)S(1)}, bf16[2,66,4,384]{3,2,1,0:T(4,128)(2,1)S(1)}) fusion(bf16[2,66,16,384]{3,2,1,0:T(8,128)(2,1)} %param.7), kind=kLoop, calls=%fused_computation.439 | loop fusion | bytes 1622016 | tf_op jit(solution)/shard_map/slice | solution.py:16
  1.7 3.2 %collective-permute-start = (bf16[2,66,4,384]{3,2,1,0:T(4,128)(2,1)S(1)}, bf16[2,66,4,384]{3,2,1,0:T(4,128)(2,1)S(1)}, u32[]{:S(2)}, u32[]{:S(2)}) collective-permute-start(bf16[2,66,4,384]{3,2,1,0:T(4,128)(2,1)S(1)} %get-tuple-element.13), channel_id=1, source_target_pairs={{0,4},{4,8},{8,12},{1,5},{5,9},{9,13},{2,6},{6,10},{10,14},{3,7},{... | collective-permute-start | bytes 1216520 | tf_op jit(solution)/shard_map/ppermute | solution.py:19
  4.9 2.1 %collective-permute-start.1 = (bf16[2,66,4,384]{3,2,1,0:T(4,128)(2,1)S(1)}, bf16[2,66,4,384]{3,2,1,0:T(4,128)(2,1)S(1)}, u32[]{:S(2)}, u32[]{:S(2)}) collective-permute-start(bf16[2,66,4,384]{3,2,1,0:T(4,128)(2,1)S(1)} %get-tuple-element.14), channel_id=1, source_target_pairs={{4,0},{8,4},{12,8},{5,1},{9,5},{13,9},{6,2},{10,6},{14,10},{7,3},{... | collective-permute-start | bytes 1216520 | tf_op jit(solution)/shard_map/ppermute | solution.py:21
  7.0 1.3 collective-permute-start.6
  8.3 0.8 reduce-window.9
  9.1 0.7 bitcast_subtract_fusion
  9.8 1.5 fusion.170
  16.4 0.7 compare_convert_fusion.4
  17.1 0.7 broadcast_multiply_fusion.4
  18.4 0.6 compare_convert_fusion.3
  19.0 0.6 compare_convert_fusion.2
  19.6 0.6 compare_convert_fusion
  20.3 0.6 slice_bitcast_fusion.27
  23.8 2.9 %fusion.11 = bf16[2,98,24,384]{3,2,1,0:T(8,128)(2,1)S(1)} fusion(bf16[2,66,4,384]{3,2,1,0:T(4,128)(2,1)S(1)} %collective-permute-done.1, bf16[2,66,16,384]{3,2,1,0:T(8,128)(2,1)} %param.7, bf16[2,66,4,384]{3,2,1,0:T(4,128)(2,1)S(1)} %collective-permute-done), kind=kLoop, calls=%fused_computation.21 | loop fusion | flops 18063360 | bytes 6045696 | tf_op jit(solution)/shard_map/concatenate | solution.py:17
  26.7 0.7 constant_dynamic-slice_fusion
  27.4 2.1 %fusion.162 = bf16[1,32,16,384]{3,2,1,0:T(8,128)(2,1)S(1)} fusion(f32[32]{0:T(128)S(1)} %get-tuple-element.38, f32[32]{0:T(128)S(1)} %get-tuple-element.39, f32[32]{0:T(128)S(1)} %get-tuple-element.40, f32[32]{0:T(128)S(1)} %get-tuple-element.41, f32[32]{0:T(128)S(1)} %get-tuple-element.42, f32[32]{0:T(128)S(1)} %get-tuple-element.43, ...), kind=kLoop, calls=%fused_computation.329 | loop fusion | flops 10616832 | bytes 7473408 | tf_op jit(solution)/shard_map/convert.4
  29.5 2.1 %fusion.161 = bf16[1,32,16,384]{3,2,1,0:T(8,128)(2,1)S(1)} fusion(f32[32]{0:T(128)S(1)} %get-tuple-element.38, f32[32]{0:T(128)S(1)} %get-tuple-element.39, f32[32]{0:T(128)S(1)} %get-tuple-element.40, f32[32]{0:T(128)S(1)} %get-tuple-element.41, f32[32]{0:T(128)S(1)} %get-tuple-element.42, f32[32]{0:T(128)S(1)} %get-tuple-element.43, ...), kind=kLoop, calls=%fused_computation.328 | loop fusion | flops 10616832 | bytes 7473408 | tf_op jit(solution)/shard_map/convert.5
  31.6 2.1 %fusion.164 = bf16[1,32,16,384]{3,2,1,0:T(8,128)(2,1)S(1)} fusion(f32[32]{0:T(128)S(1)} %get-tuple-element.56, f32[32]{0:T(128)S(1)} %get-tuple-element.57, f32[32]{0:T(128)S(1)} %get-tuple-element.58, f32[32]{0:T(128)S(1)} %get-tuple-element.59, f32[32]{0:T(128)S(1)} %get-tuple-element.60, f32[32]{0:T(128)S(1)} %get-tuple-element.61, ...), kind=kLoop, calls=%fused_computation.331 | loop fusion | flops 10616832 | bytes 7473408 | tf_op jit(solution)/shard_map/convert.6
  33.7 2.1 %fusion.163 = bf16[1,32,16,384]{3,2,1,0:T(8,128)(2,1)S(1)} fusion(f32[32]{0:T(128)S(1)} %get-tuple-element.56, f32[32]{0:T(128)S(1)} %get-tuple-element.57, f32[32]{0:T(128)S(1)} %get-tuple-element.58, f32[32]{0:T(128)S(1)} %get-tuple-element.59, f32[32]{0:T(128)S(1)} %get-tuple-element.60, f32[32]{0:T(128)S(1)} %get-tuple-element.61, ...), kind=kLoop, calls=%fused_computation.330 | loop fusion | flops 10616832 | bytes 7473408 | tf_op jit(solution)/shard_map/convert.7
  35.8 1.0 pad_maximum_fusion.1
  36.8 3.5 %collective-permute-start.2 = (bf16[2,32,16,384]{3,2,1,0:T(8,128)(2,1)}, bf16[2,32,16,384]{3,2,1,0:T(8,128)(2,1)S(1)}, u32[]{:S(2)}, u32[]{:S(2)}) collective-permute-start(bf16[2,32,16,384]{3,2,1,0:T(8,128)(2,1)} %pad_maximum_fusion.1), channel_id=1, source_target_pairs={{0,0},{1,4},{2,8},{3,12},{4,1},{5,5},{6,9},{7,13},{8,2},{9,6},{10,... | collective-permute-start | bytes 2359304 | tf_op jit(solution)/shard_map/ppermute | solution.py:154
  40.3 1.0 pad_maximum_fusion.2
  41.3 2.1 %fusion.160 = bf16[1,32,16,384]{3,2,1,0:T(8,128)(2,1)S(1)} fusion(f32[32]{0:T(128)S(1)} %get-tuple-element.74, f32[32]{0:T(128)S(1)} %get-tuple-element.75, f32[32]{0:T(128)S(1)} %get-tuple-element.76, f32[32]{0:T(128)S(1)} %get-tuple-element.77, f32[32]{0:T(128)S(1)} %get-tuple-element.78, f32[32]{0:T(128)S(1)} %get-tuple-element.79, ...), kind=kLoop, calls=%fused_computation.327 | loop fusion | flops 10616832 | bytes 7473408 | tf_op jit(solution)/shard_map/convert.2
  43.3 2.1 %fusion.159 = bf16[1,32,16,384]{3,2,1,0:T(8,128)(2,1)S(1)} fusion(f32[32]{0:T(128)S(1)} %get-tuple-element.74, f32[32]{0:T(128)S(1)} %get-tuple-element.75, f32[32]{0:T(128)S(1)} %get-tuple-element.76, f32[32]{0:T(128)S(1)} %get-tuple-element.77, f32[32]{0:T(128)S(1)} %get-tuple-element.78, f32[32]{0:T(128)S(1)} %get-tuple-element.79, ...), kind=kLoop, calls=%fused_computation.326 | loop fusion | flops 10616832 | bytes 7473408 | tf_op jit(solution)/shard_map/convert.3
  45.6 1.7 %pad_maximum_fusion = bf16[2,384,1536]{2,1,0:T(8,128)(2,1)} fusion(bf16[1,384,1536]{2,1,0:T(8,128)(2,1)S(1)} %collective-permute-done.6, bf16[1,384,1536]{2,1,0:T(8,128)(2,1)S(1)} %copy-done.2), kind=kLoop, calls=%fused_computation.23 | loop fusion | flops 1179648 | bytes 4718592 | tf_op jit(solution)/shard_map/concatenate | solution.py:117
  47.3 1.5 collective-permute-start.7
  48.9 2.1 %fusion.158 = bf16[1,32,16,384]{3,2,1,0:T(8,128)(2,1)S(1)} fusion(f32[32]{0:T(128)S(1)} %get-tuple-element.20, f32[32]{0:T(128)S(1)} %get-tuple-element.21, f32[32]{0:T(128)S(1)} %get-tuple-element.22, f32[32]{0:T(128)S(1)} %copy-done.6, f32[32]{0:T(128)S(1)} %copy-done.7, f32[32]{0:T(128)S(1)} %copy-done.8, f32[32]{0:T(128)S(1)} %copy-done.9, ...), kind=kLoop, calls=%fused_computation.325 | loop fusion | flops 10616832 | bytes 7473408 | tf_op jit(solution)/shard_map/convert
  51.0 2.1 %fusion.157 = bf16[1,32,16,384]{3,2,1,0:T(8,128)(2,1)S(1)} fusion(f32[32]{0:T(128)S(1)} %get-tuple-element.20, f32[32]{0:T(128)S(1)} %get-tuple-element.21, f32[32]{0:T(128)S(1)} %get-tuple-element.22, f32[32]{0:T(128)S(1)} %copy-done.6, f32[32]{0:T(128)S(1)} %copy-done.7, f32[32]{0:T(128)S(1)} %copy-done.8, f32[32]{0:T(128)S(1)} %copy-done.9, ...), kind=kLoop, calls=%fused_computation.324 | loop fusion | flops 10616832 | bytes 7473408 | tf_op jit(solution)/shard_map/convert.1
  53.1 1.0 pad_maximum_fusion.4
  54.1 3.1 %collective-permute-start.5 = (bf16[2,32,16,384]{3,2,1,0:T(8,128)(2,1)}, bf16[2,32,16,384]{3,2,1,0:T(8,128)(2,1)S(1)}, u32[]{:S(2)}, u32[]{:S(2)}) collective-permute-start(bf16[2,32,16,384]{3,2,1,0:T(8,128)(2,1)} %pad_maximum_fusion.4), channel_id=1, source_target_pairs={{0,12},{1,0},{2,4},{3,8},{4,13},{5,1},{6,5},{7,9},{8,14},{9,2},{10... | collective-permute-start | bytes 2359304 | tf_op jit(solution)/shard_map/ppermute | solution.py:154
  57.1 1.0 pad_maximum_fusion.3
  58.1 1.2 collective-permute-start.4
  59.3 1.1 constant_dynamic-update-slice_fusion.2
  60.4 0.8 dynamic-slice_convert_fusion
  61.2 1.1 constant_dynamic-update-slice_fusion.1
  62.3 30.9 %collective-permute-done.2 = bf16[2,32,16,384]{3,2,1,0:T(8,128)(2,1)S(1)} collective-permute-done((bf16[2,32,16,384]{3,2,1,0:T(8,128)(2,1)}, bf16[2,32,16,384]{3,2,1,0:T(8,128)(2,1)S(1)}, u32[]{:S(2)}, u32[]{:S(2)}) %collective-permute-start.2) | collective-permute-done | bytes 786464 | tf_op jit(solution)/shard_map/ppermute | solution.py:154
  93.3 2.0 %broadcast_in_dim.4 = bf16[2,32,16,1536]{3,2,1,0:T(8,128)(2,1)} broadcast(bf16[]{:T(256)} %constant.109.clone.1), dimensions={} | broadcast | bytes 3145730 | tf_op jit(solution)/shard_map/broadcast_in_dim | solution.py:167
  95.3 1.0 constant_dynamic-update-slice_fusion.6
  96.3 1.0 constant_dynamic-update-slice_fusion.5
  97.3 20.3 %collective-permute-done.4 = bf16[2,32,16,384]{3,2,1,0:T(8,128)(2,1)} collective-permute-done((bf16[2,32,16,384]{3,2,1,0:T(8,128)(2,1)}, bf16[2,32,16,384]{3,2,1,0:T(8,128)(2,1)}, u32[]{:S(2)}, u32[]{:S(2)}) %collective-permute-start.4) | collective-permute-done | bytes 786464 | tf_op jit(solution)/shard_map/ppermute | solution.py:154
  117.5 2.1 %constant_dynamic-update-slice_fusion.4 = bf16[2,32,16,1536]{3,2,1,0:T(8,128)(2,1)} fusion(bf16[2,32,16,1536]{3,2,1,0:T(8,128)(2,1)} %constant_dynamic-update-slice_fusion.5, bf16[2,32,16,384]{3,2,1,0:T(8,128)(2,1)} %collective-permute-done.4, s32[]{:T(128)S(6)} %select_n.180), kind=kLoop, calls=%fused_computation.350 | loop fusion | bytes 1572868 | tf_op jit(solution)/shard_map/dynamic_update_slice | solution.py:170
  119.7 1.0 constant_dynamic-update-slice_fusion.3
  120.7 1.8 %constant_dynamic-update-slice_fusion = bf16[4,384,1536]{2,1,0:T(8,128)(2,1)S(1)} fusion(bf16[4,384,1536]{2,1,0:T(8,128)(2,1)S(1)} %copy-done.1, bf16[2,384,1536]{2,1,0:T(8,128)(2,1)} %collective-permute-done.7), kind=kLoop, calls=%fused_computation.340 | loop fusion | bytes 4718592 | tf_op jit(solution)/shard_map/concatenate | solution.py:117
  122.8 18.0 %fusion.6 = bf16[1536,1536]{1,0:T(8,128)(2,1)S(1)} fusion(s32[]{:T(128)S(6)} %select_n.204, bf16[384,1536]{1,0:T(8,128)(2,1)S(1)} %get-tuple-element.8, bf16[384,1536]{1,0:T(8,128)(2,1)S(1)} %get-tuple-element.7, bf16[384,1536]{1,0:T(8,128)(2,1)S(1)} %get-tuple-element.6, bf16[384,1536]{1,0:T(8,128)(2,1)S(1)} %get-tuple-element.5), kind=kLoop, calls=%fused_computation.16 | loop fusion | flops 37748736 | bytes 9437188 | tf_op jit(solution)/shard_map/concatenate | solution.py:136
  140.9 3.5 %fusion.14 = f32[2,32,16,1536]{3,2,1,0:T(8,128)S(1)} fusion(bf16[1536,1536]{1,0:T(8,128)(2,1)S(1)} %fusion.6, bf16[2,32,16,384]{3,2,1,0:T(8,128)(2,1)} %collective-permute-done.4, bf16[16,384]{1,0:T(8,128)(2,1)S(1)} %get-tuple-element.18), kind=kOutput, calls=%fused_computation.27 | convolution fusion | flops 1208352768 | bytes 8269824 | tf_op jit(solution)/shard_map/rstj,ij->rsti/dot_general | solution.py:165
  144.4 1.8 %fusion.15 = f32[2,32,16,1536]{3,2,1,0:T(8,128)S(1)} fusion(bf16[1536,1536]{1,0:T(8,128)(2,1)S(1)} %fusion.6, bf16[2,32,16,384]{3,2,1,0:T(8,128)(2,1)S(1)} %collective-permute-done.3, bf16[16,384]{1,0:T(8,128)(2,1)S(1)} %get-tuple-element.16), kind=kOutput, calls=%fused_computation.29 | convolution fusion | flops 1208352768 | bytes 8269824 | tf_op jit(solution)/shard_map/rstj,ij->rsti/dot_general | solution.py:165
  146.3 1.8 %fusion.16 = f32[2,32,16,1536]{3,2,1,0:T(8,128)S(1)} fusion(bf16[1536,1536]{1,0:T(8,128)(2,1)S(1)} %fusion.6, bf16[2,32,16,384]{3,2,1,0:T(8,128)(2,1)S(1)} %copy-done.5, bf16[16,384]{1,0:T(8,128)(2,1)S(1)} %get-tuple-element.17), kind=kOutput, calls=%fused_computation.31 | convolution fusion | flops 1208352768 | bytes 8269824 | tf_op jit(solution)/shard_map/rstj,ij->rsti/dot_general | solution.py:165
  148.1 6.7 %fusion.12 = bf16[2,1,32,16,1536]{4,3,2,1,0:T(8,128)(2,1)} fusion(f32[2,32,16,1536]{3,2,1,0:T(8,128)S(1)} %fusion.14, f32[2,32,16,1536]{3,2,1,0:T(8,128)S(1)} %fusion.16, f32[2,32,16,1536]{3,2,1,0:T(8,128)S(1)} %fusion.15, bf16[2,32,16,1536]{3,2,1,0:T(8,128)(2,1)} %constant_dynamic-update-slice_fusion.3, bf16[1536,1536]{1,0:T(8,128)(2,1)} %copy-done, ...), kind=kOutput, calls=%fused_computation.22 | convolution fusion | flops 1217789952 | bytes 27144192 | tf_op jit(solution)/shard_map/rstj,ij->rsti/dot_general | solution.py:165
  (59 shorter events, 1.3 us)
Async XLA Ops:
  1.7 22.1 %collective-permute-start = (bf16[2,66,4,384]{3,2,1,0:T(4,128)(2,1)S(1)}, bf16[2,66,4,384]{3,2,1,0:T(4,128)(2,1)S(1)}, u32[]{:S(2)}, u32[]{:S(2)}) collective-permute-start(bf16[2,66,4,384]{3,2,1,0:T(4,128)(2,1)S(1)} %get-tuple-element.13), channel_id=1, source_target_pairs={{0,4},{4,8},{8,12},{1,5},{5,9},{9,13},{2,6},{6,10},{10,14},{3,7},{... | collective-permute-start | bytes 1216520 | tf_op jit(solution)/shard_map/ppermute | solution.py:19
  4.9 18.9 %collective-permute-start.1 = (bf16[2,66,4,384]{3,2,1,0:T(4,128)(2,1)S(1)}, bf16[2,66,4,384]{3,2,1,0:T(4,128)(2,1)S(1)}, u32[]{:S(2)}, u32[]{:S(2)}) collective-permute-start(bf16[2,66,4,384]{3,2,1,0:T(4,128)(2,1)S(1)} %get-tuple-element.14), channel_id=1, source_target_pairs={{4,0},{8,4},{12,8},{5,1},{9,5},{13,9},{6,2},{10,6},{14,10},{7,3},{... | collective-permute-start | bytes 1216520 | tf_op jit(solution)/shard_map/ppermute | solution.py:21
  7.0 38.6 %collective-permute-start.6 = (bf16[1,384,1536]{2,1,0:T(8,128)(2,1)}, bf16[1,384,1536]{2,1,0:T(8,128)(2,1)S(1)}, u32[]{:S(2)}, u32[]{:S(2)}) collective-permute-start(bf16[1,384,1536]{2,1,0:T(8,128)(2,1)} %param.12), channel_id=1, source_target_pairs={{0,2},{1,3},{2,0},{3,1},{4,6},{5,7},{6,4},{7,5},{8,10},{9,11},{10,... | collective-permute-start | bytes 3538952 | tf_op jit(solution)/shard_map/ppermute | solution.py:117
  36.8 56.5 %collective-permute-start.2 = (bf16[2,32,16,384]{3,2,1,0:T(8,128)(2,1)}, bf16[2,32,16,384]{3,2,1,0:T(8,128)(2,1)S(1)}, u32[]{:S(2)}, u32[]{:S(2)}) collective-permute-start(bf16[2,32,16,384]{3,2,1,0:T(8,128)(2,1)} %pad_maximum_fusion.1), channel_id=1, source_target_pairs={{0,0},{1,4},{2,8},{3,12},{4,1},{5,5},{6,9},{7,13},{8,2},{9,6},{10,... | collective-permute-start | bytes 2359304 | tf_op jit(solution)/shard_map/ppermute | solution.py:154
  41.3 55.0 %collective-permute-start.3 = (bf16[2,32,16,384]{3,2,1,0:T(8,128)(2,1)}, bf16[2,32,16,384]{3,2,1,0:T(8,128)(2,1)S(1)}, u32[]{:S(2)}, u32[]{:S(2)}) collective-permute-start(bf16[2,32,16,384]{3,2,1,0:T(8,128)(2,1)} %pad_maximum_fusion.2), channel_id=1, source_target_pairs={{0,4},{1,8},{2,12},{3,0},{4,5},{5,9},{6,13},{7,1},{8,6},{9,10},{10... | collective-permute-start | bytes 2359304 | tf_op jit(solution)/shard_map/ppermute | solution.py:154
  43.3 2.3 %copy-start.2 = (bf16[1,384,1536]{2,1,0:T(8,128)(2,1)S(1)}, bf16[1,384,1536]{2,1,0:T(8,128)(2,1)}, u32[]{:S(2)}) copy-start(bf16[1,384,1536]{2,1,0:T(8,128)(2,1)} %param.12) | copy-start | bytes 3538948
  45.4 3.3 %copy-start.6 = (f32[32]{0:T(128)S(1)}, f32[32]{0:T(128)}, u32[]{:S(2)}) copy-start(f32[32]{0:T(128)} %get-tuple-element.23) | copy-start | bytes 388
  45.4 3.3 %copy-start.7 = (f32[32]{0:T(128)S(1)}, f32[32]{0:T(128)}, u32[]{:S(2)}) copy-start(f32[32]{0:T(128)} %get-tuple-element.24) | copy-start | bytes 388
  45.5 3.3 %copy-start.8 = (f32[32]{0:T(128)S(1)}, f32[32]{0:T(128)}, u32[]{:S(2)}) copy-start(f32[32]{0:T(128)} %get-tuple-element.25) | copy-start | bytes 388
  45.5 3.3 %copy-start.9 = (f32[32]{0:T(128)S(1)}, f32[32]{0:T(128)}, u32[]{:S(2)}) copy-start(f32[32]{0:T(128)} %get-tuple-element.26) | copy-start | bytes 388
  45.5 3.3 %copy-start.10 = (f32[32]{0:T(128)S(1)}, f32[32]{0:T(128)}, u32[]{:S(2)}) copy-start(f32[32]{0:T(128)} %get-tuple-element.27) | copy-start | bytes 388
  45.5 3.3 %copy-start.11 = (f32[32]{0:T(128)S(1)}, f32[32]{0:T(128)}, u32[]{:S(2)}) copy-start(f32[32]{0:T(128)} %get-tuple-element.28) | copy-start | bytes 388
  45.5 3.3 %copy-start.12 = (f32[32]{0:T(128)S(1)}, f32[32]{0:T(128)}, u32[]{:S(2)}) copy-start(f32[32]{0:T(128)} %get-tuple-element.29) | copy-start | bytes 388
  45.5 3.3 %copy-start.13 = (f32[32]{0:T(128)S(1)}, f32[32]{0:T(128)}, u32[]{:S(2)}) copy-start(f32[32]{0:T(128)} %get-tuple-element.30) | copy-start | bytes 388
  45.5 3.3 %copy-start.14 = (f32[32]{0:T(128)S(1)}, f32[32]{0:T(128)}, u32[]{:S(2)}) copy-start(f32[32]{0:T(128)} %get-tuple-element.31) | copy-start | bytes 388
  45.5 3.3 %copy-start.15 = (f32[32]{0:T(128)S(1)}, f32[32]{0:T(128)}, u32[]{:S(2)}) copy-start(f32[32]{0:T(128)} %get-tuple-element.32) | copy-start | bytes 388
  45.5 3.3 %copy-start.16 = (f32[32]{0:T(128)S(1)}, f32[32]{0:T(128)}, u32[]{:S(2)}) copy-start(f32[32]{0:T(128)} %get-tuple-element.33) | copy-start | bytes 388
  45.5 3.3 %copy-start.17 = (f32[32]{0:T(128)S(1)}, f32[32]{0:T(128)}, u32[]{:S(2)}) copy-start(f32[32]{0:T(128)} %get-tuple-element.34) | copy-start | bytes 388
  45.6 3.3 %copy-start.18 = (f32[32]{0:T(128)S(1)}, f32[32]{0:T(128)}, u32[]{:S(2)}) copy-start(f32[32]{0:T(128)} %get-tuple-element.35) | copy-start | bytes 388
  45.6 3.3 %copy-start.19 = (f32[32]{0:T(128)S(1)}, f32[32]{0:T(128)}, u32[]{:S(2)}) copy-start(f32[32]{0:T(128)} %get-tuple-element.36) | copy-start | bytes 388
  47.3 73.4 %collective-permute-start.7 = (bf16[2,384,1536]{2,1,0:T(8,128)(2,1)}, bf16[2,384,1536]{2,1,0:T(8,128)(2,1)}, u32[]{:S(2)}, u32[]{:S(2)}) collective-permute-start(bf16[2,384,1536]{2,1,0:T(8,128)(2,1)} %pad_maximum_fusion), channel_id=1, source_target_pairs={{0,1},{1,0},{2,3},{3,2},{4,5},{5,4},{6,7},{7,6},{8,9},{9,8},{10,11... | collective-permute-start | bytes 7077896 | tf_op jit(solution)/shard_map/ppermute | solution.py:117
  54.1 65.6 %collective-permute-start.5 = (bf16[2,32,16,384]{3,2,1,0:T(8,128)(2,1)}, bf16[2,32,16,384]{3,2,1,0:T(8,128)(2,1)S(1)}, u32[]{:S(2)}, u32[]{:S(2)}) collective-permute-start(bf16[2,32,16,384]{3,2,1,0:T(8,128)(2,1)} %pad_maximum_fusion.4), channel_id=1, source_target_pairs={{0,12},{1,0},{2,4},{3,8},{4,13},{5,1},{6,5},{7,9},{8,14},{9,2},{10... | collective-permute-start | bytes 2359304 | tf_op jit(solution)/shard_map/ppermute | solution.py:154
  58.1 59.4 %collective-permute-start.4 = (bf16[2,32,16,384]{3,2,1,0:T(8,128)(2,1)}, bf16[2,32,16,384]{3,2,1,0:T(8,128)(2,1)}, u32[]{:S(2)}, u32[]{:S(2)}) collective-permute-start(bf16[2,32,16,384]{3,2,1,0:T(8,128)(2,1)} %pad_maximum_fusion.3), channel_id=1, source_target_pairs={{0,8},{1,12},{2,0},{3,4},{4,9},{5,13},{6,1},{7,5},{8,10},{9,14},{1... | collective-permute-start | bytes 2359304 | tf_op jit(solution)/shard_map/ppermute | solution.py:154
  93.3 26.4 %copy-start.4 = (bf16[2,32,16,384]{3,2,1,0:T(8,128)(2,1)}, bf16[2,32,16,384]{3,2,1,0:T(8,128)(2,1)S(1)}, u32[]{:S(2)}) copy-start(bf16[2,32,16,384]{3,2,1,0:T(8,128)(2,1)S(1)} %collective-permute-done.2) | copy-start | bytes 2359300
  95.3 25.4 %copy-start.1 = (bf16[4,384,1536]{2,1,0:T(8,128)(2,1)S(1)}, bf16[4,384,1536]{2,1,0:T(8,128)(2,1)}, u32[]{:S(2)}) copy-start(bf16[4,384,1536]{2,1,0:T(8,128)(2,1)} %constant_dynamic-update-slice_fusion.1) | copy-start | bytes 14155780
  119.6 21.2 %copy-start.3 = (bf16[2,32,16,384]{3,2,1,0:T(8,128)(2,1)}, bf16[2,32,16,384]{3,2,1,0:T(8,128)(2,1)S(1)}, u32[]{:S(2)}) copy-start(bf16[2,32,16,384]{3,2,1,0:T(8,128)(2,1)S(1)} %collective-permute-done.5) | copy-start | bytes 2359300
  140.9 5.4 %copy-start = (bf16[1536,1536]{1,0:T(8,128)(2,1)}, bf16[1536,1536]{1,0:T(8,128)(2,1)S(1)}, u32[]{:S(2)}) copy-start(bf16[1536,1536]{1,0:T(8,128)(2,1)S(1)} %fusion.6) | copy-start | bytes 14155780
  144.4 1.9 %copy-start.5 = (bf16[2,32,16,384]{3,2,1,0:T(8,128)(2,1)S(1)}, bf16[2,32,16,384]{3,2,1,0:T(8,128)(2,1)}, u32[]{:S(2)}) copy-start(bf16[2,32,16,384]{3,2,1,0:T(8,128)(2,1)} %copy-done.4) | copy-start | bytes 2359300

commit v6 on v5

--- a/solution.py
+++ b/solution.py
@@ -1,3 +1,5 @@
+import functools
+
 import jax
 import jax.numpy as jnp
 from jax import lax
@@ -23,6 +25,10 @@
             axis=dim,
         )
     return cells
+
+
+def in_order(blocks, order):
+    return jnp.concatenate([blocks[m] for m in order], axis=0)
 
 
 def masked_taps(fringe_taps, tap_windows):
@@ -122,13 +128,11 @@
             codes = codes + [x ^ step for x in codes]
             step //= 2
         where = {code: m for m, code in enumerate(codes)}
-        rows = []
-        for k in range(nf):
-            pick = sum(
-                jnp.where((k ^ b) == code, m, 0) for code, m in where.items()
-            )
-            rows.append(lax.dynamic_index_in_dim(blocks, pick, 0, keepdims=False))
-        panel = jnp.concatenate(rows, axis=0)
+        branches = [
+            functools.partial(in_order, order=[where[k ^ own] for k in range(nf)])
+            for own in range(nf)
+        ]
+        panel = lax.switch(b, branches, blocks)
     else:
         panel = lax.all_gather(filter_panels[0], "freq", axis=0, tiled=True)
     if q == 1:
@@ -139,19 +143,33 @@
     c_own = a
     u_src = (a % q) * nf + b
     fit = None
+    local = jnp.pad(visibilities, ((0, 0), (0, SLOTS), (0, 0), (0, 0)))
+    inner = t_in - 2 * REACH
     for r in range(nt):
         c_send = (u_src + r) % nt
         start = class_starts[c_send]
-        rows = lax.optimization_barrier(lax.dynamic_slice_in_dim(padded, start, SLOTS, axis=1))
         taps = lax.dynamic_index_in_dim(taps_kept, c_send, axis=1, keepdims=False)
-        chunk = convolve_class(rows, taps, class_counts[c_send], t_in)
+        count = class_counts[c_send]
         perm = []
         for sa in range(nt):
             for sb in range(nf):
                 u = (sa % q) * nf + sb
                 dc = (u + r) % nt
                 perm.append((sa * nf + sb, dc * nf + sa // q))
+        if inner > 0:
+            own = lax.optimization_barrier(lax.dynamic_slice_in_dim(local, start, SLOTS, axis=1))
+            middle = convolve_class(own, taps, count, inner)
+            got_mid = lax.ppermute(middle, ("tm", "freq"), perm)
+        rows = lax.optimization_barrier(lax.dynamic_slice_in_dim(padded, start, SLOTS, axis=1))
+        if inner > 0:
+            head = convolve_class(rows[:, :, : 3 * REACH], taps, count, REACH)
+            tail = convolve_class(rows[:, :, t_in - REACH :], taps, count, REACH)
+            chunk = jnp.concatenate([head, tail], axis=2)
+        else:
+            chunk = convolve_class(rows, taps, count, t_in)
         got = lax.ppermute(chunk, ("tm", "freq"), perm)
+        if inner > 0:
+            got = jnp.concatenate([got[:, :, :REACH], got_mid, got[:, :, REACH:]], axis=2)
         u_dst = (c_own - r) % nt
         t_sub = u_dst // nf
         b_src = u_dst % nf

time: 155 us -> 154 us (level)
  the two profiles are of different devices: /device:TPU:17 before, /device:TPU:14 now
where the time goes in v6:
time: 154 us; the launch traced here: 151 us
  waiting for transfers between devices  56.6 us (37%)
  other arithmetic  39 us (25%)
  starting transfers between devices  17.2 us (11%)
  matrix products  14.8 us (10%)
  local copies, waits for them, and re-layouts  13.4 us (9%)
  between operations  9.99 us (6%)
    ppermute x4, waiting for transfers between devices, shards(): got = lax.ppermute(chunk, ('tm', 'freq'), perm)  51.8 us
    another operation x25, other arithmetic  16.7 us
    dot_general x4, matrix products, shards(): jnp.einsum('rstj,ij->rsti', weighted, cols, preferred_element_type=jnp.fl...  14.8 us
    ppermute x4, starting transfers between devices, shards(): got = lax.ppermute(chunk, ('tm', 'freq'), perm)  5.39 us
    ppermute x4, waiting for transfers between devices, shards(): got_mid = lax.ppermute(middle, ('tm', 'freq'), perm)  4.73 us
    ppermute x4, starting transfers between devices, shards(): got_mid = lax.ppermute(middle, ('tm', 'freq'), perm)  4.58 us
    concatenate x1, other arithmetic, shards(): panel = jnp.concatenate([panel, panel], axis=1)  4.15 us
    dynamic_update_slice x4, other arithmetic, shards(): lax.dynamic_update_slice_in_dim(slotted, got, b_src * f_blk, axis=3)  4.07 us
  transfers between devices with their start and end apart: 12, of which 5 were waited for; matrix products, arithmetic and copies ran while one was open for 28% of the time, Pallas kernels for 0%

profile of v6, /device:TPU:14, one launch (start us, length us, event | category | flops | bytes accessed | tf_op | source)
XLA Modules:
  0.0 151.0 jit_solution(16782366848258336306)
XLA Ops:
  0.0 0.6 collective-permute-start.10
  0.6 1.8 %copy.8 = bf16[2,66,16,384]{3,1,2,0:T(8,128)(2,1)S(1)} copy(bf16[2,66,16,384]{3,2,1,0:T(8,128)(2,1)} %param.11) | data formatting | bytes 3244032 | tf_op args[0]
  2.4 1.0 fusion.458
  3.4 3.5 %collective-permute-start = (bf16[2,66,4,384]{3,1,2,0:T(8,128)(2,1)}, bf16[2,66,4,384]{3,1,2,0:T(8,128)(2,1)}, u32[]{:S(2)}, u32[]{:S(2)}) collective-permute-start(bf16[2,66,4,384]{3,1,2,0:T(8,128)(2,1)} %get-tuple-element.58), channel_id=1, source_target_pairs={{0,4},{4,8},{8,12},{1,5},{5,9},{9,13},{2,6},{6,10},{10,14},{3,7},{... | collective-permute-start | bytes 1216520 | tf_op jit(solution)/shard_map/ppermute | solution.py:21
  6.9 3.1 %collective-permute-start.1 = (bf16[2,66,4,384]{3,1,2,0:T(8,128)(2,1)}, bf16[2,66,4,384]{3,1,2,0:T(8,128)(2,1)}, u32[]{:S(2)}, u32[]{:S(2)}) collective-permute-start(bf16[2,66,4,384]{3,1,2,0:T(8,128)(2,1)} %get-tuple-element.59), channel_id=1, source_target_pairs={{4,0},{8,4},{12,8},{5,1},{9,5},{13,9},{6,2},{10,6},{14,10},{7,3},{... | collective-permute-start | bytes 1216520 | tf_op jit(solution)/shard_map/ppermute | solution.py:23
  10.3 0.7 fusion.463
  16.2 0.6 constant_dynamic-slice_fusion.1
  16.8 0.7 compare_convert_fusion.3
  20.3 2.7 %pad_dynamic-slice_fusion.2 = (bf16[2,32,16,384]{3,2,1,0:T(8,128)(2,1)S(1)}, bf16[2,32,16,384]{3,2,1,0:T(8,128)(2,1)S(1)}, bf16[2,32,16,384]{3,2,1,0:T(8,128)(2,1)S(1)}, bf16[2,32,16,384]{3,2,1,0:T(8,128)(2,1)S(1)}) fusion(s32[]{:T(128)S(6)} %select_n.133, bf16[2,66,16,384]{3,2,1,0:T(8,128)(2,1)} %param.11, s32[]{:T(128)S(6)} %select_n.121, ...), kind=kLoop, calls=%fused_computation.23 | loop fusion | bytes 4767760 | tf_op jit(solution)/shard_map/dynamic_slice | solution.py:160
  23.0 1.1 fusion.161
  24.2 1.1 fusion.160
  25.4 0.8 pad_maximum_fusion.9
  26.1 2.2 %collective-permute-start.3 = (bf16[2,32,8,384]{3,2,1,0:T(8,128)(2,1)}, bf16[2,32,8,384]{3,2,1,0:T(8,128)(2,1)}, u32[]{:S(2)}, u32[]{:S(2)}) collective-permute-start(bf16[2,32,8,384]{3,2,1,0:T(8,128)(2,1)} %pad_maximum_fusion.9), channel_id=1, source_target_pairs={{0,0},{1,4},{2,8},{3,12},{4,1},{5,5},{6,9},{7,13},{8,2},{9,6},{10,... | collective-permute-start | bytes 1179656 | tf_op jit(solution)/shard_map/ppermute | solution.py:162
  28.4 0.6 compare_convert_fusion.1
  29.3 1.1 fusion.157
  30.4 1.1 fusion.156
  31.7 0.8 pad_maximum_fusion.11
  32.5 2.4 %collective-permute-start.7 = (bf16[2,32,8,384]{3,2,1,0:T(8,128)(2,1)}, bf16[2,32,8,384]{3,2,1,0:T(8,128)(2,1)}, u32[]{:S(2)}, u32[]{:S(2)}) collective-permute-start(bf16[2,32,8,384]{3,2,1,0:T(8,128)(2,1)} %pad_maximum_fusion.11), channel_id=1, source_target_pairs={{0,8},{1,12},{2,0},{3,4},{4,9},{5,13},{6,1},{7,5},{8,10},{9,14},{1... | collective-permute-start | bytes 1179656 | tf_op jit(solution)/shard_map/ppermute | solution.py:162
  34.9 0.7 compare_convert_fusion.2
  35.8 1.1 fusion.159
  37.1 1.8 %fusion.158 = bf16[1,32,8,384]{3,2,1,0:T(8,128)(2,1)} fusion(f32[32]{0:T(128)S(1)} %get-tuple-element.95, f32[32]{0:T(128)S(1)} %get-tuple-element.96, f32[32]{0:T(128)S(1)} %get-tuple-element.97, f32[32]{0:T(128)S(1)} %get-tuple-element.98, f32[32]{0:T(128)S(1)} %get-tuple-element.99, f32[32]{0:T(128)S(1)} %get-tuple-element.100, ...), kind=kLoop, calls=%fused_computation.339 | loop fusion | flops 5308416 | bytes 3737856 | tf_op jit(solution)/shard_map/convert.13
  38.9 0.7 compare_convert_fusion
  39.6 0.7 broadcast_multiply_fusion
  40.4 1.0 pad_maximum_fusion.10
  41.4 0.8 dynamic-slice_convert_fusion
  42.2 1.1 fusion.155
  43.3 1.1 fusion.154
  44.5 1.5 fusion.5
  46.2 3.0 %constant_dynamic-slice_fusion = (bf16[2,32,24,384]{3,1,2,0:T(8,128)(2,1)S(1)}, bf16[2,32,24,384]{3,1,2,0:T(8,128)(2,1)S(1)}, bf16[2,32,24,384]{3,1,2,0:T(8,128)(2,1)S(1)}, bf16[2,32,24,384]{3,1,2,0:T(8,128)(2,1)S(1)}) fusion(bf16[2,98,24,384]{3,1,2,0:T(8,128)(2,1)S(1)} %fusion.5, s32[]{:T(128)S(6)} %select_n.133, s32[]{:T(128)S(6)} %select_n.127, ...), kind=kLoop, calls=%fused_computation.931 | loop fusion | bytes 9437200 | tf_op jit(solution)/shard_map/dynamic_slice | solution.py:163
  53.4 3.0 %collective-permute-start.2 = (bf16[2,32,8,384]{3,1,2,0:T(8,128)(2,1)S(1)}, bf16[2,32,8,384]{3,1,2,0:T(8,128)(2,1)S(1)}, u32[]{:S(2)}, u32[]{:S(2)}) collective-permute-start(bf16[2,32,8,384]{3,1,2,0:T(8,128)(2,1)S(1)} %maximum_maximum_fusion), channel_id=1, source_target_pairs={{0,0},{1,4},{2,8},{3,12},{4,1},{5,5},{6,9},{7,13},{8,2},{9,6},{10,... | collective-permute-start | bytes 1179656 | tf_op jit(solution)/shard_map/ppermute | solution.py:170
  56.4 2.4 %collective-permute-start.4 = (bf16[2,32,8,384]{3,1,2,0:T(8,128)(2,1)S(1)}, bf16[2,32,8,384]{3,1,2,0:T(8,128)(2,1)S(1)}, u32[]{:S(2)}, u32[]{:S(2)}) collective-permute-start(bf16[2,32,8,384]{3,1,2,0:T(8,128)(2,1)S(1)} %maximum_maximum_fusion.1), channel_id=1, source_target_pairs={{0,4},{1,8},{2,12},{3,0},{4,5},{5,9},{6,13},{7,1},{8,6},{9,10},{10... | collective-permute-start | bytes 1179656 | tf_op jit(solution)/shard_map/ppermute | solution.py:170
  61.2 1.5 pad_maximum_fusion.4
  64.2 15.3 %collective-permute-done.2 = bf16[2,32,8,384]{3,1,2,0:T(8,128)(2,1)S(1)} collective-permute-done((bf16[2,32,8,384]{3,1,2,0:T(8,128)(2,1)S(1)}, bf16[2,32,8,384]{3,1,2,0:T(8,128)(2,1)S(1)}, u32[]{:S(2)}, u32[]{:S(2)}) %collective-permute-start.2) | collective-permute-done | bytes 393248 | tf_op jit(solution)/shard_map/ppermute | solution.py:170
  79.6 7.9 %collective-permute-done.4 = bf16[2,32,8,384]{3,1,2,0:T(8,128)(2,1)S(1)} collective-permute-done((bf16[2,32,8,384]{3,1,2,0:T(8,128)(2,1)S(1)}, bf16[2,32,8,384]{3,1,2,0:T(8,128)(2,1)S(1)}, u32[]{:S(2)}, u32[]{:S(2)}) %collective-permute-start.4) | collective-permute-done | bytes 393248 | tf_op jit(solution)/shard_map/ppermute | solution.py:170
  87.6 9.2 %collective-permute-done.8 = bf16[2,32,8,384]{3,1,2,0:T(8,128)(2,1)S(1)} collective-permute-done((bf16[2,32,8,384]{3,1,2,0:T(8,128)(2,1)S(1)}, bf16[2,32,8,384]{3,1,2,0:T(8,128)(2,1)S(1)}, u32[]{:S(2)}, u32[]{:S(2)}) %collective-permute-start.8) | collective-permute-done | bytes 393248 | tf_op jit(solution)/shard_map/ppermute | solution.py:170
  97.5 19.4 %collective-permute-done.6 = bf16[2,32,8,384]{3,1,2,0:T(8,128)(2,1)S(1)} collective-permute-done((bf16[2,32,8,384]{3,1,2,0:T(8,128)(2,1)S(1)}, bf16[2,32,8,384]{3,1,2,0:T(8,128)(2,1)S(1)}, u32[]{:S(2)}, u32[]{:S(2)}) %collective-permute-start.6) | collective-permute-done | bytes 393248 | tf_op jit(solution)/shard_map/ppermute | solution.py:170
  117.6 1.5 %fusion.165 = bf16[2,32,16,1536]{3,2,1,0:T(8,128)(2,1)S(1)} fusion(bf16[2,32,16,1536]{3,2,1,0:T(8,128)(2,1)S(1)} %broadcast_in_dim.4, s32[]{:T(128)S(6)} %select_n.118, bf16[2,32,4,384]{3,2,1,0:T(4,128)(2,1)S(1)} %copy.12, bf16[2,32,8,384]{3,2,1,0:T(8,128)(2,1)} %collective-permute-done.3, bf16[2,32,4,384]{3,2,1,0:T(4,128)(2,1)S(1)} %copy.11), kind=kLoop, calls=%fused_computation.346 | loop fusion | flops 2359296 | bytes 1572868 | tf_op jit(solution)/shard_map/dynamic_update_slice | solution.py:188
  119.1 0.5 fusion.164
  119.6 1.5 %fusion.163 = bf16[2,32,16,1536]{3,2,1,0:T(8,128)(2,1)S(1)} fusion(bf16[2,32,16,1536]{3,2,1,0:T(8,128)(2,1)S(1)} %fusion.164, s32[]{:T(128)S(6)} %select_n.130, bf16[2,32,4,384]{3,2,1,0:T(4,128)(2,1)S(1)} %copy.16, bf16[2,32,8,384]{3,2,1,0:T(8,128)(2,1)} %collective-permute-done.7, bf16[2,32,4,384]{3,2,1,0:T(4,128)(2,1)S(1)} %copy.15), kind=kLoop, calls=%fused_computation.344 | loop fusion | flops 2359296 | bytes 1572868 | tf_op jit(solution)/shard_map/dynamic_update_slice | solution.py:188
  121.2 4.7 %collective-permute-done.9 = bf16[2,32,8,384]{3,2,1,0:T(8,128)(2,1)S(1)} collective-permute-done((bf16[2,32,8,384]{3,2,1,0:T(8,128)(2,1)S(1)}, bf16[2,32,8,384]{3,2,1,0:T(8,128)(2,1)S(1)}, u32[]{:S(2)}, u32[]{:S(2)}) %collective-permute-start.9) | collective-permute-done | bytes 393248 | tf_op jit(solution)/shard_map/ppermute | solution.py:162
  126.7 1.4 copy-done.2
  128.1 3.9 %conditional.1 = (bf16[1536,1536]{1,0:T(8,128)(2,1)}) conditional(s32[]{:T(128)} %clamp.3, (bf16[1,384,1536]{2,1,0:T(8,128)(2,1)S(1)}, bf16[2,384,1536]{2,1,0:T(8,128)(2,1)S(1)}, bf16[1,384,1536]{2,1,0:T(8,128)(2,1)}) %tuple.124, (bf16[2,384,1536]{2,1,0:T(8,128)(2,1)S(1)}, bf16[1,384,1536]{2,1,0:T(8,128)(2,1)S(1)}, ...), branch_computations={%region_1.2_spmd, %region_2.3_spmd, %region_3.4_spmd, %region_4.5_... | conditional | flops 18874368 | bytes 14155784 | solution.py:135
  128.2 3.7 %pad_maximum_fusion.2 = bf16[1536,1536]{1,0:T(8,128)(2,1)} fusion(bf16[384,1536]{1,0:T(8,128)(2,1)S(1)} %get-tuple-element.51, bf16[384,1536]{1,0:T(8,128)(2,1)S(1)} %bitcast.212, bf16[384,1536]{1,0:T(8,128)(2,1)S(1)} %get-tuple-element.50, bf16[384,1536]{1,0:T(8,128)(2,1)} %bitcast.8), kind=kLoop, calls=%fused_computation.6 | loop fusion | flops 18874368 | bytes 9437184 | tf_op jit(solution)/shard_map/cond/branch_2_fun/concatenate | solution.py:31
  132.0 4.1 %fusion.3 = bf16[1536,1536]{1,0:T(8,128)(2,1)S(1)} fusion(s32[]{:T(128)S(6)} %select_n.138, bf16[1536,1536]{1,0:T(8,128)(2,1)} %get-tuple-element.164), kind=kLoop, calls=%fused_computation.19 | loop fusion | flops 9437184 | bytes 9437188 | tf_op jit(solution)/shard_map/concatenate | solution.py:140
  136.1 3.1 %fusion.7 = f32[2,32,16,1536]{3,2,1,0:T(8,128)S(1)} fusion(bf16[1536,1536]{1,0:T(8,128)(2,1)S(1)} %fusion.3, bf16[16,384]{1,0:T(8,128)(2,1)S(1)} %get-tuple-element.75, bf16[2,32,4,384]{3,2,1,0:T(4,128)(2,1)S(1)} %copy.16, bf16[2,32,8,384]{3,2,1,0:T(8,128)(2,1)} %collective-permute-done.7, bf16[2,32,4,384]{3,2,1,0:T(4,128)(2,1)S(1)} %copy.15), kind=kOutput, calls=%fused_computation.30 | convolution fusion | flops 1211105280 | bytes 8269824 | tf_op jit(solution)/shard_map/rstj,ij->rsti/dot_general | solution.py:183
  139.3 1.8 %fusion.8 = f32[2,32,16,1536]{3,2,1,0:T(8,128)S(1)} fusion(bf16[1536,1536]{1,0:T(8,128)(2,1)S(1)} %fusion.3, bf16[16,384]{1,0:T(8,128)(2,1)S(1)} %get-tuple-element.73, bf16[2,32,4,384]{3,2,1,0:T(4,128)(2,1)S(1)} %copy.14, bf16[2,32,8,384]{3,2,1,0:T(8,128)(2,1)S(1)} %collective-permute-done.5, bf16[2,32,4,384]{3,2,1,0:T(4,128)(2,1)S(1)} %copy.13), kind=kOutput, calls=%fused_computation.32 | convolution fusion | flops 1211105280 | bytes 8269824 | tf_op jit(solution)/shard_map/rstj,ij->rsti/dot_general | solution.py:183
  141.1 3.2 %fusion.9 = f32[2,32,16,1536]{3,2,1,0:T(8,128)S(1)} fusion(bf16[1536,1536]{1,0:T(8,128)(2,1)} %copy-done.1, bf16[16,384]{1,0:T(8,128)(2,1)S(1)} %get-tuple-element.74, bf16[2,32,4,384]{3,2,1,0:T(4,128)(2,1)S(1)} %copy-done.6, bf16[2,32,8,384]{3,2,1,0:T(8,128)(2,1)} %collective-permute-done.3, bf16[2,32,4,384]{3,2,1,0:T(4,128)(2,1)S(1)} %copy-done.4), kind=kOutput, calls=%fused_computation.34 | convolution fusion | flops 1211105280 | bytes 8269824 | tf_op jit(solution)/shard_map/rstj,ij->rsti/dot_general | solution.py:183
  144.4 6.6 %fusion.6 = bf16[2,1,32,16,1536]{4,3,2,1,0:T(8,128)(2,1)} fusion(f32[2,32,16,1536]{3,2,1,0:T(8,128)S(1)} %fusion.7, f32[2,32,16,1536]{3,2,1,0:T(8,128)S(1)} %fusion.9, f32[2,32,16,1536]{3,2,1,0:T(8,128)S(1)} %fusion.8, bf16[2,32,16,1536]{3,2,1,0:T(8,128)(2,1)} %copy-done.2, bf16[1536,1536]{1,0:T(8,128)(2,1)} %copy-done.1, ...), kind=kOutput, calls=%fused_computation.22 | convolution fusion | flops 1220542464 | bytes 27144192 | tf_op jit(solution)/shard_map/rstj,ij->rsti/dot_general | solution.py:183
  (282 shorter events, 10.5 us)
Async XLA Ops:
  0.0 10.1 %copy-start.108 = (s32[4]{0:T(128)S(1)}, s32[4]{0:T(128)}, u32[]{:S(2)}) copy-start(s32[4]{0:T(128)} %param.12) | copy-start | bytes 52
  0.0 16.1 %copy-start.110 = (s32[4]{0:T(128)S(1)}, s32[4]{0:T(128)}, u32[]{:S(2)}) copy-start(s32[4]{0:T(128)} %param.13) | copy-start | bytes 52
  0.0 16.2 %copy-start.109 = (f32[2,4,9]{2,1,0:T(4,128)S(1)}, f32[2,4,9]{2,1,0:T(4,128)}, u32[]{:S(2)}) copy-start(f32[2,4,9]{2,1,0:T(4,128)} %param.14) | copy-start | bytes 868
  0.0 61.2 %collective-permute-start.10 = (bf16[1,384,1536]{2,1,0:T(8,128)(2,1)}, bf16[1,384,1536]{2,1,0:T(8,128)(2,1)}, u32[]{:S(2)}, u32[]{:S(2)}) collective-permute-start(bf16[1,384,1536]{2,1,0:T(8,128)(2,1)} %param.16), channel_id=1, source_target_pairs={{0,2},{1,3},{2,0},{3,1},{4,6},{5,7},{6,4},{7,5},{8,10},{9,11},{10,... | collective-permute-start | bytes 3538952 | tf_op jit(solution)/shard_map/ppermute | solution.py:123
  3.4 41.1 %collective-permute-start = (bf16[2,66,4,384]{3,1,2,0:T(8,128)(2,1)}, bf16[2,66,4,384]{3,1,2,0:T(8,128)(2,1)}, u32[]{:S(2)}, u32[]{:S(2)}) collective-permute-start(bf16[2,66,4,384]{3,1,2,0:T(8,128)(2,1)} %get-tuple-element.58), channel_id=1, source_target_pairs={{0,4},{4,8},{8,12},{1,5},{5,9},{9,13},{2,6},{6,10},{10,14},{3,7},{... | collective-permute-start | bytes 1216520 | tf_op jit(solution)/shard_map/ppermute | solution.py:21
  6.9 37.6 %collective-permute-start.1 = (bf16[2,66,4,384]{3,1,2,0:T(8,128)(2,1)}, bf16[2,66,4,384]{3,1,2,0:T(8,128)(2,1)}, u32[]{:S(2)}, u32[]{:S(2)}) collective-permute-start(bf16[2,66,4,384]{3,1,2,0:T(8,128)(2,1)} %get-tuple-element.59), channel_id=1, source_target_pairs={{4,0},{8,4},{12,8},{5,1},{9,5},{13,9},{6,2},{10,6},{14,10},{7,3},{... | collective-permute-start | bytes 1216520 | tf_op jit(solution)/shard_map/ppermute | solution.py:23
  17.6 6.5 %copy-start.8 = (f32[32]{0:T(128)}, f32[32]{0:T(128)S(1)}, u32[]{:S(2)}) copy-start(f32[32]{0:T(128)S(1)} %get-tuple-element.116) | copy-start | bytes 388
  17.6 6.5 %copy-start.10 = (f32[32]{0:T(128)}, f32[32]{0:T(128)S(1)}, u32[]{:S(2)}) copy-start(f32[32]{0:T(128)S(1)} %get-tuple-element.117) | copy-start | bytes 388
  17.6 6.5 %copy-start.12 = (f32[32]{0:T(128)}, f32[32]{0:T(128)S(1)}, u32[]{:S(2)}) copy-start(f32[32]{0:T(128)S(1)} %get-tuple-element.118) | copy-start | bytes 388
  17.6 6.5 %copy-start.14 = (f32[32]{0:T(128)}, f32[32]{0:T(128)S(1)}, u32[]{:S(2)}) copy-start(f32[32]{0:T(128)S(1)} %get-tuple-element.119) | copy-start | bytes 388
  17.6 6.5 %copy-start.16 = (f32[32]{0:T(128)}, f32[32]{0:T(128)S(1)}, u32[]{:S(2)}) copy-start(f32[32]{0:T(128)S(1)} %get-tuple-element.120) | copy-start | bytes 388
  17.6 6.5 %copy-start.18 = (f32[32]{0:T(128)}, f32[32]{0:T(128)S(1)}, u32[]{:S(2)}) copy-start(f32[32]{0:T(128)S(1)} %get-tuple-element.121) | copy-start | bytes 388
  17.6 6.5 %copy-start.20 = (f32[32]{0:T(128)}, f32[32]{0:T(128)S(1)}, u32[]{:S(2)}) copy-start(f32[32]{0:T(128)S(1)} %get-tuple-element.122) | copy-start | bytes 388
  17.6 6.5 %copy-start.22 = (f32[32]{0:T(128)}, f32[32]{0:T(128)S(1)}, u32[]{:S(2)}) copy-start(f32[32]{0:T(128)S(1)} %get-tuple-element.123) | copy-start | bytes 388
  17.6 6.5 %copy-start.24 = (f32[32]{0:T(128)}, f32[32]{0:T(128)S(1)}, u32[]{:S(2)}) copy-start(f32[32]{0:T(128)S(1)} %get-tuple-element.124) | copy-start | bytes 388
  17.7 6.5 %copy-start.26 = (f32[32]{0:T(128)}, f32[32]{0:T(128)S(1)}, u32[]{:S(2)}) copy-start(f32[32]{0:T(128)S(1)} %get-tuple-element.125) | copy-start | bytes 388
  17.7 6.5 %copy-start.28 = (f32[32]{0:T(128)}, f32[32]{0:T(128)S(1)}, u32[]{:S(2)}) copy-start(f32[32]{0:T(128)S(1)} %get-tuple-element.126) | copy-start | bytes 388
  17.7 6.5 %copy-start.30 = (f32[32]{0:T(128)}, f32[32]{0:T(128)S(1)}, u32[]{:S(2)}) copy-start(f32[32]{0:T(128)S(1)} %get-tuple-element.127) | copy-start | bytes 388
  17.7 6.5 %copy-start.32 = (f32[32]{0:T(128)}, f32[32]{0:T(128)S(1)}, u32[]{:S(2)}) copy-start(f32[32]{0:T(128)S(1)} %get-tuple-element.128) | copy-start | bytes 388
  26.1 91.0 %collective-permute-start.3 = (bf16[2,32,8,384]{3,2,1,0:T(8,128)(2,1)}, bf16[2,32,8,384]{3,2,1,0:T(8,128)(2,1)}, u32[]{:S(2)}, u32[]{:S(2)}) collective-permute-start(bf16[2,32,8,384]{3,2,1,0:T(8,128)(2,1)} %pad_maximum_fusion.9), channel_id=1, source_target_pairs={{0,0},{1,4},{2,8},{3,12},{4,1},{5,5},{6,9},{7,13},{8,2},{9,6},{10,... | collective-permute-start | bytes 1179656 | tf_op jit(solution)/shard_map/ppermute | solution.py:162
  32.5 87.1 %collective-permute-start.7 = (bf16[2,32,8,384]{3,2,1,0:T(8,128)(2,1)}, bf16[2,32,8,384]{3,2,1,0:T(8,128)(2,1)}, u32[]{:S(2)}, u32[]{:S(2)}) collective-permute-start(bf16[2,32,8,384]{3,2,1,0:T(8,128)(2,1)} %pad_maximum_fusion.11), channel_id=1, source_target_pairs={{0,8},{1,12},{2,0},{3,4},{4,9},{5,13},{6,1},{7,5},{8,10},{9,14},{1... | collective-permute-start | bytes 1179656 | tf_op jit(solution)/shard_map/ppermute | solution.py:162
  52.3 6.6 %copy-start.37 = (f32[32]{0:T(128)S(1)}, f32[32]{0:T(128)}, u32[]{:S(2)}) copy-start(f32[32]{0:T(128)} %copy-done.36) | copy-start | bytes 388
  52.3 6.6 %copy-start.39 = (f32[32]{0:T(128)S(1)}, f32[32]{0:T(128)}, u32[]{:S(2)}) copy-start(f32[32]{0:T(128)} %copy-done.38) | copy-start | bytes 388
  52.3 6.6 %copy-start.41 = (f32[32]{0:T(128)S(1)}, f32[32]{0:T(128)}, u32[]{:S(2)}) copy-start(f32[32]{0:T(128)} %copy-done.40) | copy-start | bytes 388
  52.3 6.6 %copy-start.43 = (f32[32]{0:T(128)S(1)}, f32[32]{0:T(128)}, u32[]{:S(2)}) copy-start(f32[32]{0:T(128)} %copy-done.42) | copy-start | bytes 388
  52.3 6.6 %copy-start.45 = (f32[32]{0:T(128)S(1)}, f32[32]{0:T(128)}, u32[]{:S(2)}) copy-start(f32[32]{0:T(128)} %copy-done.44) | copy-start | bytes 388
  52.3 6.6 %copy-start.47 = (f32[32]{0:T(128)S(1)}, f32[32]{0:T(128)}, u32[]{:S(2)}) copy-start(f32[32]{0:T(128)} %copy-done.46) | copy-start | bytes 388
  52.3 6.6 %copy-start.49 = (f32[32]{0:T(128)S(1)}, f32[32]{0:T(128)}, u32[]{:S(2)}) copy-start(f32[32]{0:T(128)} %copy-done.48) | copy-start | bytes 388
  52.3 6.6 %copy-start.51 = (f32[32]{0:T(128)S(1)}, f32[32]{0:T(128)}, u32[]{:S(2)}) copy-start(f32[32]{0:T(128)} %copy-done.50) | copy-start | bytes 388
  52.3 6.6 %copy-start.53 = (f32[32]{0:T(128)S(1)}, f32[32]{0:T(128)}, u32[]{:S(2)}) copy-start(f32[32]{0:T(128)} %copy-done.52) | copy-start | bytes 388
  52.4 6.6 %copy-start.55 = (f32[32]{0:T(128)S(1)}, f32[32]{0:T(128)}, u32[]{:S(2)}) copy-start(f32[32]{0:T(128)} %copy-done.54) | copy-start | bytes 388
  52.4 6.6 %copy-start.57 = (f32[32]{0:T(128)S(1)}, f32[32]{0:T(128)}, u32[]{:S(2)}) copy-start(f32[32]{0:T(128)} %copy-done.56) | copy-start | bytes 388
  52.4 6.6 %copy-start.59 = (f32[32]{0:T(128)S(1)}, f32[32]{0:T(128)}, u32[]{:S(2)}) copy-start(f32[32]{0:T(128)} %copy-done.58) | copy-start | bytes 388
  52.4 6.6 %copy-start.61 = (f32[32]{0:T(128)S(1)}, f32[32]{0:T(128)}, u32[]{:S(2)}) copy-start(f32[32]{0:T(128)} %copy-done.60) | copy-start | bytes 388
  52.4 6.6 %copy-start.63 = (f32[32]{0:T(128)S(1)}, f32[32]{0:T(128)}, u32[]{:S(2)}) copy-start(f32[32]{0:T(128)} %copy-done.62) | copy-start | bytes 388
  52.4 6.6 %copy-start.65 = (f32[32]{0:T(128)S(1)}, f32[32]{0:T(128)}, u32[]{:S(2)}) copy-start(f32[32]{0:T(128)} %copy-done.64) | copy-start | bytes 388
  52.4 6.6 %copy-start.67 = (f32[32]{0:T(128)S(1)}, f32[32]{0:T(128)}, u32[]{:S(2)}) copy-start(f32[32]{0:T(128)} %copy-done.66) | copy-start | bytes 388
  52.4 6.6 %copy-start.69 = (f32[32]{0:T(128)S(1)}, f32[32]{0:T(128)}, u32[]{:S(2)}) copy-start(f32[32]{0:T(128)} %copy-done.68) | copy-start | bytes 388
  52.4 6.6 %copy-start.71 = (f32[32]{0:T(128)S(1)}, f32[32]{0:T(128)}, u32[]{:S(2)}) copy-start(f32[32]{0:T(128)} %copy-done.70) | copy-start | bytes 388
  53.4 26.2 %collective-permute-start.2 = (bf16[2,32,8,384]{3,1,2,0:T(8,128)(2,1)S(1)}, bf16[2,32,8,384]{3,1,2,0:T(8,128)(2,1)S(1)}, u32[]{:S(2)}, u32[]{:S(2)}) collective-permute-start(bf16[2,32,8,384]{3,1,2,0:T(8,128)(2,1)S(1)} %maximum_maximum_fusion), channel_id=1, source_target_pairs={{0,0},{1,4},{2,8},{3,12},{4,1},{5,5},{6,9},{7,13},{8,2},{9,6},{10,... | collective-permute-start | bytes 1179656 | tf_op jit(solution)/shard_map/ppermute | solution.py:170
  56.4 31.1 %collective-permute-start.4 = (bf16[2,32,8,384]{3,1,2,0:T(8,128)(2,1)S(1)}, bf16[2,32,8,384]{3,1,2,0:T(8,128)(2,1)S(1)}, u32[]{:S(2)}, u32[]{:S(2)}) collective-permute-start(bf16[2,32,8,384]{3,1,2,0:T(8,128)(2,1)S(1)} %maximum_maximum_fusion.1), channel_id=1, source_target_pairs={{0,4},{1,8},{2,12},{3,0},{4,5},{5,9},{6,13},{7,1},{8,6},{9,10},{10... | collective-permute-start | bytes 1179656 | tf_op jit(solution)/shard_map/ppermute | solution.py:170
  62.7 63.7 %collective-permute-start.11 = (bf16[2,384,1536]{2,1,0:T(8,128)(2,1)S(1)}, bf16[2,384,1536]{2,1,0:T(8,128)(2,1)S(1)}, u32[]{:S(2)}, u32[]{:S(2)}) collective-permute-start(bf16[2,384,1536]{2,1,0:T(8,128)(2,1)S(1)} %pad_maximum_fusion.4), channel_id=1, source_target_pairs={{0,1},{1,0},{2,3},{3,2},{4,5},{5,4},{6,7},{7,6},{8,9},{9,8},{10,11... | collective-permute-start | bytes 7077896 | tf_op jit(solution)/shard_map/ppermute | solution.py:123
  79.6 17.2 %collective-permute-start.8 = (bf16[2,32,8,384]{3,1,2,0:T(8,128)(2,1)S(1)}, bf16[2,32,8,384]{3,1,2,0:T(8,128)(2,1)S(1)}, u32[]{:S(2)}, u32[]{:S(2)}) collective-permute-start(bf16[2,32,8,384]{3,1,2,0:T(8,128)(2,1)S(1)} %maximum_maximum_fusion.3), channel_id=1, source_target_pairs={{0,12},{1,0},{2,4},{3,8},{4,13},{5,1},{6,5},{7,9},{8,14},{9,2},{10... | collective-permute-start | bytes 1179656 | tf_op jit(solution)/shard_map/ppermute | solution.py:170
  87.6 29.3 %collective-permute-start.6 = (bf16[2,32,8,384]{3,1,2,0:T(8,128)(2,1)S(1)}, bf16[2,32,8,384]{3,1,2,0:T(8,128)(2,1)S(1)}, u32[]{:S(2)}, u32[]{:S(2)}) collective-permute-start(bf16[2,32,8,384]{3,1,2,0:T(8,128)(2,1)S(1)} %maximum_maximum_fusion.2), channel_id=1, source_target_pairs={{0,8},{1,12},{2,0},{3,4},{4,9},{5,13},{6,1},{7,5},{8,10},{9,14},{1... | collective-permute-start | bytes 1179656 | tf_op jit(solution)/shard_map/ppermute | solution.py:170
  96.8 22.3 %collective-permute-start.5 = (bf16[2,32,8,384]{3,2,1,0:T(8,128)(2,1)S(1)}, bf16[2,32,8,384]{3,2,1,0:T(8,128)(2,1)S(1)}, u32[]{:S(2)}, u32[]{:S(2)}) collective-permute-start(bf16[2,32,8,384]{3,2,1,0:T(8,128)(2,1)S(1)} %pad_maximum_fusion.10), channel_id=1, source_target_pairs={{0,4},{1,8},{2,12},{3,0},{4,5},{5,9},{6,13},{7,1},{8,6},{9,10},{10... | collective-permute-start | bytes 1179656 | tf_op jit(solution)/shard_map/ppermute | solution.py:162
  96.9 20.6 %copy-start.3 = (bf16[2,32,4,384]{3,2,1,0:T(4,128)(2,1)}, bf16[2,32,4,384]{3,2,1,0:T(4,128)(2,1)S(1)}, u32[]{:S(2)}) copy-start(bf16[2,32,4,384]{3,2,1,0:T(4,128)(2,1)S(1)} %copy.11) | copy-start | bytes 589828
  97.1 20.5 %copy-start.5 = (bf16[2,32,4,384]{3,2,1,0:T(4,128)(2,1)}, bf16[2,32,4,384]{3,2,1,0:T(4,128)(2,1)S(1)}, u32[]{:S(2)}) copy-start(bf16[2,32,4,384]{3,2,1,0:T(4,128)(2,1)S(1)} %copy.12) | copy-start | bytes 589828
  116.9 9.0 %collective-permute-start.9 = (bf16[2,32,8,384]{3,2,1,0:T(8,128)(2,1)S(1)}, bf16[2,32,8,384]{3,2,1,0:T(8,128)(2,1)S(1)}, u32[]{:S(2)}, u32[]{:S(2)}) collective-permute-start(bf16[2,32,8,384]{3,2,1,0:T(8,128)(2,1)S(1)} %pad_maximum_fusion.12), channel_id=1, source_target_pairs={{0,12},{1,0},{2,4},{3,8},{4,13},{5,1},{6,5},{7,9},{8,14},{9,2},{10... | collective-permute-start | bytes 1179656 | tf_op jit(solution)/shard_map/ppermute | solution.py:162
  (75 other events, 162.4 us)

commit v7 on v6

--- a/solution.py
+++ b/solution.py
@@ -49,11 +49,6 @@
     return jnp.stack([real_part, imag_part]).astype(jnp.bfloat16)
 
 
-def convolve_class(rows, taps, count, length):
-    live = (jnp.arange(rows.shape[1], dtype=jnp.int32) < count).astype(jnp.float32)
-    return convolve(rows, taps[:, None, :] * live[None, :, None], length)
-
-
 def to_slots(per_baseline, class_counts):
     class_starts = jnp.cumsum(class_counts) - class_counts
     slot_positions = jnp.arange(SLOTS, dtype=jnp.int32)
@@ -101,7 +96,6 @@
             visibilities, class_ids, class_counts, tap_windows, fringe_taps, flag_mask,
             filter_panels,
         )
-    q = nt // nf
     a = lax.axis_index("tm")
     b = lax.axis_index("freq")
     t_in = visibilities.shape[2]
@@ -115,7 +109,7 @@
     padded = extended(visibilities, (("tm", 2),), REACH)
     padded = jnp.pad(padded, ((0, 0), (0, SLOTS), (0, 0), (0, 0)))
 
-    if q == 1 and nf & (nf - 1) == 0:
+    if nf & (nf - 1) == 0:
         blocks = filter_panels[0][None]
         step = nf // 2
         while step >= 1:
@@ -135,63 +129,36 @@
         panel = lax.switch(b, branches, blocks)
     else:
         panel = lax.all_gather(filter_panels[0], "freq", axis=0, tiled=True)
-    if q == 1:
-        shift = ((a + 1) % nf) * f_blk
-        panel = jnp.concatenate([panel, panel], axis=1)
-        panel = lax.dynamic_slice_in_dim(panel, shift, channels, axis=1)
+    shift = lax.rem(a + 1, nf) * f_blk
+    panel = jnp.concatenate([panel, panel], axis=1)
+    panel = lax.dynamic_slice_in_dim(panel, shift, channels, axis=1)
 
-    c_own = a
-    u_src = (a % q) * nf + b
+    rounds = jnp.arange(nt, dtype=jnp.int32)
+    c_all = lax.rem(b + rounds, nt)
+    start_all = jnp.take(class_starts, c_all)
+    count_all = jnp.take(class_counts, c_all)
+    live_all = (jnp.arange(SLOTS, dtype=jnp.int32)[None, :] < count_all[:, None]).astype(jnp.float32)
+    taps_all = jnp.take(taps_kept, c_all, axis=1)[:, :, None, :] * live_all[None, :, :, None]
+    offset_all = lax.rem(a + nt - rounds, nt) * f_blk
     fit = None
-    local = jnp.pad(visibilities, ((0, 0), (0, SLOTS), (0, 0), (0, 0)))
-    inner = t_in - 2 * REACH
+    slotted = jnp.zeros((2, SLOTS, t_out, channels), jnp.bfloat16)
     for r in range(nt):
-        c_send = (u_src + r) % nt
-        start = class_starts[c_send]
-        taps = lax.dynamic_index_in_dim(taps_kept, c_send, axis=1, keepdims=False)
-        count = class_counts[c_send]
+        rows = lax.optimization_barrier(
+            lax.dynamic_slice_in_dim(padded, start_all[r], SLOTS, axis=1)
+        )
+        chunk = convolve(rows, taps_all[:, r], t_in)
         perm = []
         for sa in range(nt):
             for sb in range(nf):
-                u = (sa % q) * nf + sb
-                dc = (u + r) % nt
-                perm.append((sa * nf + sb, dc * nf + sa // q))
-        if inner > 0:
-            own = lax.optimization_barrier(lax.dynamic_slice_in_dim(local, start, SLOTS, axis=1))
-            middle = convolve_class(own, taps, count, inner)
-            got_mid = lax.ppermute(middle, ("tm", "freq"), perm)
-        rows = lax.optimization_barrier(lax.dynamic_slice_in_dim(padded, start, SLOTS, axis=1))
-        if inner > 0:
-            head = convolve_class(rows[:, :, : 3 * REACH], taps, count, REACH)
-            tail = convolve_class(rows[:, :, t_in - REACH :], taps, count, REACH)
-            chunk = jnp.concatenate([head, tail], axis=2)
-        else:
-            chunk = convolve_class(rows, taps, count, t_in)
+                perm.append((sa * nf + sb, ((sb + r) % nt) * nf + sa))
         got = lax.ppermute(chunk, ("tm", "freq"), perm)
-        if inner > 0:
-            got = jnp.concatenate([got[:, :, :REACH], got_mid, got[:, :, REACH:]], axis=2)
-        u_dst = (c_own - r) % nt
-        t_sub = u_dst // nf
-        b_src = u_dst % nf
-        if q == 1:
-            gate = lax.dynamic_slice_in_dim(flag_mask, b_src * f_blk, f_blk, axis=1)
-            cols = lax.slice_in_dim(panel, (nf - 1 - r) * f_blk, (nf - r) * f_blk, axis=1)
-        else:
-            gate = lax.dynamic_slice(flag_mask, (t_sub * t_in, b_src * f_blk), (t_in, f_blk))
-            cols = lax.dynamic_slice_in_dim(panel, b_src * f_blk, f_blk, axis=1)
+        b_off = offset_all[r]
+        gate = lax.dynamic_slice_in_dim(flag_mask, b_off, f_blk, axis=1)
+        cols = lax.slice_in_dim(panel, (nf - 1 - r) * f_blk, (nf - r) * f_blk, axis=1)
         weighted = got * gate.astype(jnp.bfloat16)
         part = jnp.einsum("rstj,ij->rsti", weighted, cols, preferred_element_type=jnp.float32)
-        if fit is None:
-            slotted = jnp.zeros((2, SLOTS, t_out, channels), jnp.bfloat16)
-        if q == 1:
-            fit = part if fit is None else fit + part
-            slotted = lax.dynamic_update_slice_in_dim(slotted, got, b_src * f_blk, axis=3)
-        else:
-            if fit is None:
-                fit = jnp.zeros((2, SLOTS, t_out, channels), jnp.float32)
-            prev = lax.dynamic_slice_in_dim(fit, t_sub * t_in, t_in, axis=2)
-            fit = lax.dynamic_update_slice_in_dim(fit, prev + part, t_sub * t_in, axis=2)
-            slotted = lax.dynamic_update_slice(slotted, got, (0, 0, t_sub * t_in, b_src * f_blk))
+        fit = part if fit is None else fit + part
+        slotted = lax.dynamic_update_slice_in_dim(slotted, got, b_off, axis=3)
     cleaned = (slotted.astype(jnp.float32) - fit).astype(jnp.bfloat16)
     return cleaned[:, None]
 

time: 154 us -> 166 us (1.078)
  local copies, waits for them, and re-layouts: 13.4 us -> 43.6 us
  waiting for transfers between devices: 56.6 us -> 30.9 us
  between operations: 9.99 us -> 15.6 us
  matrix products: 14.8 us -> 16.5 us
    dynamic_update_slice x0 -> x4, local copies, waits for them, and re-layouts: none -> 34.4 us  [shards(): slotted = lax.dynamic_update_slice_in_dim(slotted, got, b_off, axis=3)]
    ppermute x4, waiting for transfers between devices: 51.8 us -> 30.9 us  [shards(): got = lax.ppermute(chunk, ('tm', 'freq'), perm)]
    dynamic_slice x4 -> x1, local copies, waits for them, and re-layouts: 6.96 us -> 0.71 us  [shards(): lax.dynamic_slice_in_dim(padded, start_all[r], SLOTS, axis=1)]
    ppermute x4, starting transfers between devices: 5.39 us -> 10.3 us  [shards(): got = lax.ppermute(chunk, ('tm', 'freq'), perm)]
    ppermute x4 -> x0, waiting for transfers between devices: 4.73 us -> none  [shards(): got_mid = lax.ppermute(middle, ('tm', 'freq'), perm)]
    ppermute x4 -> x0, starting transfers between devices: 4.58 us -> none  [shards(): got_mid = lax.ppermute(middle, ('tm', 'freq'), perm)]
    dynamic_update_slice x4 -> x0, other arithmetic: 4.07 us -> none  [shards(): lax.dynamic_update_slice_in_dim(slotted, got, b_src * f_blk, axis=3)]
    unnamed x224 -> x40, local copies, waits for them, and re-layouts: 3.91 us -> 0.09 us
  transfers between devices with their start and end apart: 12 -> 8, of which waited for: 5 -> 3; matrix products, arithmetic and copies ran while one was open for 28% -> 45% of each run, Pallas kernels for 0% -> 0%
where the time goes in v7:
time: 166 us; the launch traced here: 164 us
  local copies, waits for them, and re-layouts  43.6 us (26%)
  other arithmetic  39.1 us (24%)
  waiting for transfers between devices  30.9 us (19%)
  starting transfers between devices  17.9 us (11%)
  matrix products  16.5 us (10%)
  between operations  15.6 us (9%)
    dynamic_update_slice x4, local copies, waits for them, and re-layouts, shards(): slotted = lax.dynamic_update_slice_in_dim(slotted, got, b_off, axis=3)  34.4 us
    ppermute x4, waiting for transfers between devices, shards(): got = lax.ppermute(chunk, ('tm', 'freq'), perm)  30.9 us
    another operation x9, other arithmetic  17.6 us
    dot_general x4, matrix products, shards(): jnp.einsum('rstj,ij->rsti', weighted, cols, preferred_element_type=jnp.fl...  16.5 us
    ppermute x4, starting transfers between devices, shards(): got = lax.ppermute(chunk, ('tm', 'freq'), perm)  10.3 us
    concatenate x1, other arithmetic, shards(): panel = jnp.concatenate([panel, panel], axis=1)  4.16 us
    another operation x4, other arithmetic, convolve(): return jnp.stack([real_part, imag_part]).astype(jnp.bfloat16)  3.88 us
    concatenate x1, other arithmetic, in_order(): return jnp.concatenate([blocks[m] for m in order], axis=0)  3.73 us
  transfers between devices with their start and end apart: 8, of which 3 were waited for; matrix products, arithmetic and copies ran while one was open for 45% of the time, Pallas kernels for 0%

profile of v7, /device:TPU:14, one launch (start us, length us, event | category | flops | bytes accessed | tf_op | source)
XLA Modules:
  0.0 163.6 jit_solution(15113053305763798150)
XLA Ops:
  0.0 1.7 %fusion.169 = (bf16[2,66,4,384]{3,2,1,0:T(4,128)(2,1)S(1)}, bf16[2,66,4,384]{3,2,1,0:T(4,128)(2,1)S(1)}) fusion(bf16[2,66,16,384]{3,2,1,0:T(8,128)(2,1)} %param.13), kind=kLoop, calls=%fused_computation.445 | loop fusion | bytes 1622016 | tf_op jit(solution)/shard_map/slice | solution.py:18
  1.7 3.5 %collective-permute-start = (bf16[2,66,4,384]{3,2,1,0:T(4,128)(2,1)S(1)}, bf16[2,66,4,384]{3,2,1,0:T(4,128)(2,1)S(1)}, u32[]{:S(2)}, u32[]{:S(2)}) collective-permute-start(bf16[2,66,4,384]{3,2,1,0:T(4,128)(2,1)S(1)} %get-tuple-element.59), channel_id=1, source_target_pairs={{0,4},{4,8},{8,12},{1,5},{5,9},{9,13},{2,6},{6,10},{10,14},{3,7},{... | collective-permute-start | bytes 1216520 | tf_op jit(solution)/shard_map/ppermute | solution.py:21
  5.2 2.4 %collective-permute-start.1 = (bf16[2,66,4,384]{3,2,1,0:T(4,128)(2,1)S(1)}, bf16[2,66,4,384]{3,2,1,0:T(4,128)(2,1)S(1)}, u32[]{:S(2)}, u32[]{:S(2)}) collective-permute-start(bf16[2,66,4,384]{3,2,1,0:T(4,128)(2,1)S(1)} %get-tuple-element.60), channel_id=1, source_target_pairs={{4,0},{8,4},{12,8},{5,1},{9,5},{13,9},{6,2},{10,6},{14,10},{7,3},{... | collective-permute-start | bytes 1216520 | tf_op jit(solution)/shard_map/ppermute | solution.py:23
  8.2 0.8 reduce-window.9
  9.1 0.7 bitcast_subtract_fusion
  9.7 1.3 gather_fusion.1
  11.0 0.6 gather_fusion.2
  11.7 0.7 fusion.171
  17.7 0.7 compare_convert_fusion
  18.4 0.7 copy_multiply_fusion
  19.8 0.6 slice_bitcast_fusion.39
  23.1 2.9 %fusion.5 = bf16[2,98,24,384]{3,2,1,0:T(8,128)(2,1)S(1)} fusion(bf16[2,66,4,384]{3,2,1,0:T(4,128)(2,1)S(1)} %collective-permute-done.1, bf16[2,66,16,384]{3,2,1,0:T(8,128)(2,1)} %param.13, bf16[2,66,4,384]{3,2,1,0:T(4,128)(2,1)S(1)} %collective-permute-done), kind=kLoop, calls=%fused_computation.24 | loop fusion | flops 18063360 | bytes 6045696 | tf_op jit(solution)/shard_map/concatenate | solution.py:19
  26.0 0.7 constant_dynamic-slice_fusion
  26.7 2.1 %fusion.154 = bf16[1,32,16,384]{3,2,1,0:T(8,128)(2,1)S(1)} fusion(f32[32]{0:T(128)S(1)} %get-tuple-element.124, f32[32]{0:T(128)S(1)} %get-tuple-element.125, f32[32]{0:T(128)S(1)} %get-tuple-element.126, f32[32]{0:T(128)S(1)} %get-tuple-element.127, f32[32]{0:T(128)S(1)} %get-tuple-element.128, f32[32]{0:T(128)S(1)} %get-tuple-element.129, ...), kind=kLoop, calls=%fused_computation.326 | loop fusion | flops 10616832 | bytes 7473408 | tf_op jit(solution)/shard_map/convert.2
  28.8 2.1 %fusion.153 = bf16[1,32,16,384]{3,2,1,0:T(8,128)(2,1)S(1)} fusion(f32[32]{0:T(128)S(1)} %get-tuple-element.124, f32[32]{0:T(128)S(1)} %get-tuple-element.125, f32[32]{0:T(128)S(1)} %get-tuple-element.126, f32[32]{0:T(128)S(1)} %get-tuple-element.127, f32[32]{0:T(128)S(1)} %get-tuple-element.128, f32[32]{0:T(128)S(1)} %get-tuple-element.129, ...), kind=kLoop, calls=%fused_computation.325 | loop fusion | flops 10616832 | bytes 7473408 | tf_op jit(solution)/shard_map/convert.3
  30.9 2.1 %fusion.158 = bf16[1,32,16,384]{3,2,1,0:T(8,128)(2,1)S(1)} fusion(f32[32]{0:T(128)S(1)} %get-tuple-element.106, f32[32]{0:T(128)S(1)} %get-tuple-element.107, f32[32]{0:T(128)S(1)} %get-tuple-element.108, f32[32]{0:T(128)S(1)} %get-tuple-element.109, f32[32]{0:T(128)S(1)} %get-tuple-element.110, f32[32]{0:T(128)S(1)} %get-tuple-element.111, ...), kind=kLoop, calls=%fused_computation.330 | loop fusion | flops 10616832 | bytes 7473408 | tf_op jit(solution)/shard_map/convert.6
  33.0 2.1 %fusion.157 = bf16[1,32,16,384]{3,2,1,0:T(8,128)(2,1)S(1)} fusion(f32[32]{0:T(128)S(1)} %get-tuple-element.106, f32[32]{0:T(128)S(1)} %get-tuple-element.107, f32[32]{0:T(128)S(1)} %get-tuple-element.108, f32[32]{0:T(128)S(1)} %get-tuple-element.109, f32[32]{0:T(128)S(1)} %get-tuple-element.110, f32[32]{0:T(128)S(1)} %get-tuple-element.111, ...), kind=kLoop, calls=%fused_computation.329 | loop fusion | flops 10616832 | bytes 7473408 | tf_op jit(solution)/shard_map/convert.7
  35.2 1.0 pad_maximum_fusion.5
  36.1 3.0 %collective-permute-start.2 = (bf16[2,32,16,384]{3,2,1,0:T(8,128)(2,1)}, bf16[2,32,16,384]{3,2,1,0:T(8,128)(2,1)}, u32[]{:S(2)}, u32[]{:S(2)}) collective-permute-start(bf16[2,32,16,384]{3,2,1,0:T(8,128)(2,1)} %pad_maximum_fusion.5), channel_id=1, source_target_pairs={{0,0},{1,4},{2,8},{3,12},{4,1},{5,5},{6,9},{7,13},{8,2},{9,6},{10,... | collective-permute-start | bytes 2359304 | tf_op jit(solution)/shard_map/ppermute | solution.py:154
  39.1 2.1 %fusion.156 = bf16[1,32,16,384]{3,2,1,0:T(8,128)(2,1)S(1)} fusion(f32[32]{0:T(128)S(1)} %get-tuple-element.88, f32[32]{0:T(128)S(1)} %get-tuple-element.89, f32[32]{0:T(128)S(1)} %get-tuple-element.90, f32[32]{0:T(128)S(1)} %get-tuple-element.91, f32[32]{0:T(128)S(1)} %get-tuple-element.92, f32[32]{0:T(128)S(1)} %get-tuple-element.93, ...), kind=kLoop, calls=%fused_computation.328 | loop fusion | flops 10616832 | bytes 7473408 | tf_op jit(solution)/shard_map/convert.4
  41.2 2.1 %fusion.155 = bf16[1,32,16,384]{3,2,1,0:T(8,128)(2,1)S(1)} fusion(f32[32]{0:T(128)S(1)} %get-tuple-element.88, f32[32]{0:T(128)S(1)} %get-tuple-element.89, f32[32]{0:T(128)S(1)} %get-tuple-element.90, f32[32]{0:T(128)S(1)} %get-tuple-element.91, f32[32]{0:T(128)S(1)} %get-tuple-element.92, f32[32]{0:T(128)S(1)} %get-tuple-element.93, ...), kind=kLoop, calls=%fused_computation.327 | loop fusion | flops 10616832 | bytes 7473408 | tf_op jit(solution)/shard_map/convert.5
  43.5 2.9 %pad_maximum_fusion.4 = bf16[2,384,1536]{2,1,0:T(8,128)(2,1)} fusion(bf16[1,384,1536]{2,1,0:T(8,128)(2,1)} %collective-permute-done.6, bf16[1,384,1536]{2,1,0:T(8,128)(2,1)S(1)} %copy-done), kind=kLoop, calls=%fused_computation.26 | loop fusion | flops 1179648 | bytes 4718592 | tf_op jit(solution)/shard_map/concatenate | solution.py:117
  46.4 1.1 collective-permute-start.7
  47.6 1.0 pad_maximum_fusion.6
  48.6 1.4 collective-permute-start.3
  50.0 1.0 pad_maximum_fusion.7
  50.9 2.3 %collective-permute-start.4 = (bf16[2,32,16,384]{3,2,1,0:T(8,128)(2,1)}, bf16[2,32,16,384]{3,2,1,0:T(8,128)(2,1)}, u32[]{:S(2)}, u32[]{:S(2)}) collective-permute-start(bf16[2,32,16,384]{3,2,1,0:T(8,128)(2,1)} %pad_maximum_fusion.7), channel_id=1, source_target_pairs={{0,8},{1,12},{2,0},{3,4},{4,9},{5,13},{6,1},{7,5},{8,10},{9,14},{1... | collective-permute-start | bytes 2359304 | tf_op jit(solution)/shard_map/ppermute | solution.py:154
  53.3 2.1 %fusion.152 = bf16[1,32,16,384]{3,2,1,0:T(8,128)(2,1)S(1)} fusion(f32[32]{0:T(128)S(1)} %get-tuple-element.70, f32[32]{0:T(128)S(1)} %get-tuple-element.71, f32[32]{0:T(128)S(1)} %copy-done.5, f32[32]{0:T(128)S(1)} %copy-done.6, f32[32]{0:T(128)S(1)} %copy-done.7, f32[32]{0:T(128)S(1)} %copy-done.8, f32[32]{0:T(128)S(1)} %copy-done.9, f32[32]{0:T(128)S(1)} %copy-done.10, ...), kind=kLoop, calls=%fused_computation.324 | loop fusion | flops 10616832 | bytes 7473408 | tf_op jit(solution)/shard_map/convert
  55.4 2.1 %fusion.151 = bf16[1,32,16,384]{3,2,1,0:T(8,128)(2,1)S(1)} fusion(f32[32]{0:T(128)S(1)} %get-tuple-element.70, f32[32]{0:T(128)S(1)} %get-tuple-element.71, f32[32]{0:T(128)S(1)} %copy-done.5, f32[32]{0:T(128)S(1)} %copy-done.6, f32[32]{0:T(128)S(1)} %copy-done.7, f32[32]{0:T(128)S(1)} %copy-done.8, f32[32]{0:T(128)S(1)} %copy-done.9, f32[32]{0:T(128)S(1)} %copy-done.10, ...), kind=kLoop, calls=%fused_computation.323 | loop fusion | flops 10616832 | bytes 7473408 | tf_op jit(solution)/shard_map/convert.1
  57.5 1.0 pad_maximum_fusion.8
  58.5 3.6 %collective-permute-start.5 = (bf16[2,32,16,384]{3,2,1,0:T(8,128)(2,1)}, bf16[2,32,16,384]{3,2,1,0:T(8,128)(2,1)}, u32[]{:S(2)}, u32[]{:S(2)}) collective-permute-start(bf16[2,32,16,384]{3,2,1,0:T(8,128)(2,1)} %pad_maximum_fusion.8), channel_id=1, source_target_pairs={{0,12},{1,0},{2,4},{3,8},{4,13},{5,1},{6,5},{7,9},{8,14},{9,2},{10... | collective-permute-start | bytes 2359304 | tf_op jit(solution)/shard_map/ppermute | solution.py:154
  62.1 0.6 fusion.170
  70.0 1.6 dynamic-slice_convert_fusion
  71.6 20.7 %collective-permute-done.2 = bf16[2,32,16,384]{3,2,1,0:T(8,128)(2,1)} collective-permute-done((bf16[2,32,16,384]{3,2,1,0:T(8,128)(2,1)}, bf16[2,32,16,384]{3,2,1,0:T(8,128)(2,1)}, u32[]{:S(2)}, u32[]{:S(2)}) %collective-permute-start.2) | collective-permute-done | bytes 786464 | tf_op jit(solution)/shard_map/ppermute | solution.py:154
  92.3 2.0 %broadcast_in_dim.17 = bf16[2,32,16,1536]{3,2,1,0:T(8,128)(2,1)} broadcast(bf16[]{:T(256)} %constant.30.clone.1), dimensions={} | broadcast | bytes 3145730 | tf_op jit(solution)/shard_map/broadcast_in_dim | solution.py:144
  94.3 8.7 %dynamic_update_slice.12 = bf16[2,32,16,1536]{3,2,1,0:T(8,128)(2,1)} dynamic-update-slice(bf16[2,32,16,1536]{3,2,1,0:T(8,128)(2,1)} %broadcast_in_dim.17, bf16[2,32,16,384]{3,2,1,0:T(8,128)(2,1)} %collective-permute-done.2, s32[]{:T(128)} %constant.32.clone.1, s32[]{:T(128)} %constant.32.clone.1, s32[]{:T(128)} %constant.32.clone.1, s32[]{:T(128)S(6)} %select_n.65) | dynamic-update-slice | bytes 1572868 | tf_op jit(solution)/shard_map/dynamic_update_slice | solution.py:161
  103.0 6.1 %collective-permute-done.3 = bf16[2,32,16,384]{3,2,1,0:T(8,128)(2,1)} collective-permute-done((bf16[2,32,16,384]{3,2,1,0:T(8,128)(2,1)}, bf16[2,32,16,384]{3,2,1,0:T(8,128)(2,1)}, u32[]{:S(2)}, u32[]{:S(2)}) %collective-permute-start.3) | collective-permute-done | bytes 786464 | tf_op jit(solution)/shard_map/ppermute | solution.py:154
  109.1 8.7 %dynamic_update_slice.13 = bf16[2,32,16,1536]{3,2,1,0:T(8,128)(2,1)} dynamic-update-slice(bf16[2,32,16,1536]{3,2,1,0:T(8,128)(2,1)} %dynamic_update_slice.12, bf16[2,32,16,384]{3,2,1,0:T(8,128)(2,1)} %collective-permute-done.3, s32[]{:T(128)} %constant.32.clone.1, s32[]{:T(128)} %constant.32.clone.1, s32[]{:T(128)} %constant.32.clone.1, s32[]{:T(128)S(6)} %select_n.67) | dynamic-update-slice | bytes 1572868 | tf_op jit(solution)/shard_map/dynamic_update_slice | solution.py:161
  117.9 4.2 %collective-permute-done.4 = bf16[2,32,16,384]{3,2,1,0:T(8,128)(2,1)} collective-permute-done((bf16[2,32,16,384]{3,2,1,0:T(8,128)(2,1)}, bf16[2,32,16,384]{3,2,1,0:T(8,128)(2,1)}, u32[]{:S(2)}, u32[]{:S(2)}) %collective-permute-start.4) | collective-permute-done | bytes 786464 | tf_op jit(solution)/shard_map/ppermute | solution.py:154
  122.0 8.1 %dynamic_update_slice.14 = bf16[2,32,16,1536]{3,2,1,0:T(8,128)(2,1)} dynamic-update-slice(bf16[2,32,16,1536]{3,2,1,0:T(8,128)(2,1)} %dynamic_update_slice.13, bf16[2,32,16,384]{3,2,1,0:T(8,128)(2,1)} %collective-permute-done.4, s32[]{:T(128)} %constant.32.clone.1, s32[]{:T(128)} %constant.32.clone.1, s32[]{:T(128)} %constant.32.clone.1, s32[]{:T(128)S(6)} %select_n.69) | dynamic-update-slice | bytes 1572868 | tf_op jit(solution)/shard_map/dynamic_update_slice | solution.py:161
  130.2 8.8 %dynamic_update_slice.15 = bf16[2,32,16,1536]{3,2,1,0:T(8,128)(2,1)} dynamic-update-slice(bf16[2,32,16,1536]{3,2,1,0:T(8,128)(2,1)} %dynamic_update_slice.14, bf16[2,32,16,384]{3,2,1,0:T(8,128)(2,1)} %collective-permute-done.5, s32[]{:T(128)} %constant.32.clone.1, s32[]{:T(128)} %constant.32.clone.1, s32[]{:T(128)} %constant.32.clone.1, s32[]{:T(128)S(6)} %select_n.71) | dynamic-update-slice | bytes 1572868 | tf_op jit(solution)/shard_map/dynamic_update_slice | solution.py:161
  138.9 3.9 %conditional.1 = (bf16[1536,1536]{1,0:T(8,128)(2,1)}) conditional(s32[]{:T(128)} %clamp.3, (bf16[1,384,1536]{2,1,0:T(8,128)(2,1)S(1)}, bf16[2,384,1536]{2,1,0:T(8,128)(2,1)S(1)}, bf16[1,384,1536]{2,1,0:T(8,128)(2,1)}) %tuple.115, (bf16[2,384,1536]{2,1,0:T(8,128)(2,1)S(1)}, bf16[1,384,1536]{2,1,0:T(8,128)(2,1)S(1)}, ...), branch_computations={%region_1.3_spmd, %region_2.4_spmd, %region_3.5_spmd, %region_4.6_... | conditional | flops 18874368 | bytes 14155784 | solution.py:129
  139.1 3.7 %pad_maximum_fusion.2 = bf16[1536,1536]{1,0:T(8,128)(2,1)} fusion(bf16[384,1536]{1,0:T(8,128)(2,1)S(1)} %get-tuple-element.52, bf16[384,1536]{1,0:T(8,128)(2,1)S(1)} %bitcast.220, bf16[384,1536]{1,0:T(8,128)(2,1)S(1)} %get-tuple-element.51, bf16[384,1536]{1,0:T(8,128)(2,1)} %bitcast.8), kind=kLoop, calls=%fused_computation.9 | loop fusion | flops 18874368 | bytes 9437184 | tf_op jit(solution)/shard_map/cond/branch_2_fun/concatenate | solution.py:31
  142.8 4.2 %fusion.3 = bf16[1536,1536]{1,0:T(8,128)(2,1)S(1)} fusion(s32[]{:T(128)S(6)} %select_n.72, bf16[1536,1536]{1,0:T(8,128)(2,1)} %get-tuple-element.151), kind=kLoop, calls=%fused_computation.22 | loop fusion | flops 9437184 | bytes 9437188 | tf_op jit(solution)/shard_map/concatenate | solution.py:133
  147.0 3.6 %fusion.8 = f32[2,32,16,1536]{3,2,1,0:T(8,128)S(1)} fusion(bf16[1536,1536]{1,0:T(8,128)(2,1)S(1)} %fusion.3, bf16[2,32,16,384]{3,2,1,0:T(8,128)(2,1)} %collective-permute-done.4, bf16[16,384]{1,0:T(8,128)(2,1)S(1)} %copy-done.3), kind=kOutput, calls=%fused_computation.30 | convolution fusion | flops 1208352768 | bytes 8269824 | tf_op jit(solution)/shard_map/rstj,ij->rsti/dot_general | solution.py:159
  150.6 3.0 %fusion.9 = f32[2,32,16,1536]{3,2,1,0:T(8,128)S(1)} fusion(bf16[1536,1536]{1,0:T(8,128)(2,1)S(1)} %fusion.3, bf16[2,32,16,384]{3,2,1,0:T(8,128)(2,1)} %collective-permute-done.3, bf16[16,384]{1,0:T(8,128)(2,1)S(1)} %copy-done.2), kind=kOutput, calls=%fused_computation.32 | convolution fusion | flops 1208352768 | bytes 8269824 | tf_op jit(solution)/shard_map/rstj,ij->rsti/dot_general | solution.py:159
  153.6 3.3 %fusion.10 = f32[2,32,16,1536]{3,2,1,0:T(8,128)S(1)} fusion(bf16[1536,1536]{1,0:T(8,128)(2,1)} %copy-done.1, bf16[2,32,16,384]{3,2,1,0:T(8,128)(2,1)} %collective-permute-done.2, bf16[16,384]{1,0:T(8,128)(2,1)S(1)} %get-tuple-element.63), kind=kOutput, calls=%fused_computation.34 | convolution fusion | flops 1208352768 | bytes 8269824 | tf_op jit(solution)/shard_map/rstj,ij->rsti/dot_general | solution.py:159
  156.9 6.7 %fusion.6 = bf16[2,1,32,16,1536]{4,3,2,1,0:T(8,128)(2,1)} fusion(f32[2,32,16,1536]{3,2,1,0:T(8,128)S(1)} %fusion.8, f32[2,32,16,1536]{3,2,1,0:T(8,128)S(1)} %fusion.10, f32[2,32,16,1536]{3,2,1,0:T(8,128)S(1)} %fusion.9, bf16[2,32,16,1536]{3,2,1,0:T(8,128)(2,1)} %dynamic_update_slice.15, bf16[1536,1536]{1,0:T(8,128)(2,1)} %copy-done.1, ...), kind=kOutput, calls=%fused_computation.25 | convolution fusion | flops 1217789952 | bytes 27144192 | tf_op jit(solution)/shard_map/rstj,ij->rsti/dot_general | solution.py:159
  (63 shorter events, 1.8 us)
Async XLA Ops:
  1.7 21.4 %collective-permute-start = (bf16[2,66,4,384]{3,2,1,0:T(4,128)(2,1)S(1)}, bf16[2,66,4,384]{3,2,1,0:T(4,128)(2,1)S(1)}, u32[]{:S(2)}, u32[]{:S(2)}) collective-permute-start(bf16[2,66,4,384]{3,2,1,0:T(4,128)(2,1)S(1)} %get-tuple-element.59), channel_id=1, source_target_pairs={{0,4},{4,8},{8,12},{1,5},{5,9},{9,13},{2,6},{6,10},{10,14},{3,7},{... | collective-permute-start | bytes 1216520 | tf_op jit(solution)/shard_map/ppermute | solution.py:21
  5.2 17.9 %collective-permute-start.1 = (bf16[2,66,4,384]{3,2,1,0:T(4,128)(2,1)S(1)}, bf16[2,66,4,384]{3,2,1,0:T(4,128)(2,1)S(1)}, u32[]{:S(2)}, u32[]{:S(2)}) collective-permute-start(bf16[2,66,4,384]{3,2,1,0:T(4,128)(2,1)S(1)} %get-tuple-element.60), channel_id=1, source_target_pairs={{4,0},{8,4},{12,8},{5,1},{9,5},{13,9},{6,2},{10,6},{14,10},{7,3},{... | collective-permute-start | bytes 1216520 | tf_op jit(solution)/shard_map/ppermute | solution.py:23
  7.6 35.9 %collective-permute-start.6 = (bf16[1,384,1536]{2,1,0:T(8,128)(2,1)}, bf16[1,384,1536]{2,1,0:T(8,128)(2,1)}, u32[]{:S(2)}, u32[]{:S(2)}) collective-permute-start(bf16[1,384,1536]{2,1,0:T(8,128)(2,1)} %param.18), channel_id=1, source_target_pairs={{0,2},{1,3},{2,0},{3,1},{4,6},{5,7},{6,4},{7,5},{8,10},{9,11},{10,... | collective-permute-start | bytes 3538952 | tf_op jit(solution)/shard_map/ppermute | solution.py:117
  36.1 56.1 %collective-permute-start.2 = (bf16[2,32,16,384]{3,2,1,0:T(8,128)(2,1)}, bf16[2,32,16,384]{3,2,1,0:T(8,128)(2,1)}, u32[]{:S(2)}, u32[]{:S(2)}) collective-permute-start(bf16[2,32,16,384]{3,2,1,0:T(8,128)(2,1)} %pad_maximum_fusion.5), channel_id=1, source_target_pairs={{0,0},{1,4},{2,8},{3,12},{4,1},{5,5},{6,9},{7,13},{8,2},{9,6},{10,... | collective-permute-start | bytes 2359304 | tf_op jit(solution)/shard_map/ppermute | solution.py:154
  41.2 2.3 %copy-start = (bf16[1,384,1536]{2,1,0:T(8,128)(2,1)S(1)}, bf16[1,384,1536]{2,1,0:T(8,128)(2,1)}, u32[]{:S(2)}) copy-start(bf16[1,384,1536]{2,1,0:T(8,128)(2,1)} %param.18) | copy-start | bytes 3538948
  43.3 9.9 %copy-start.5 = (f32[32]{0:T(128)S(1)}, f32[32]{0:T(128)}, u32[]{:S(2)}) copy-start(f32[32]{0:T(128)} %get-tuple-element.72) | copy-start | bytes 388
  43.3 9.9 %copy-start.6 = (f32[32]{0:T(128)S(1)}, f32[32]{0:T(128)}, u32[]{:S(2)}) copy-start(f32[32]{0:T(128)} %get-tuple-element.73) | copy-start | bytes 388
  43.3 9.9 %copy-start.7 = (f32[32]{0:T(128)S(1)}, f32[32]{0:T(128)}, u32[]{:S(2)}) copy-start(f32[32]{0:T(128)} %get-tuple-element.74) | copy-start | bytes 388
  43.4 9.8 %copy-start.8 = (f32[32]{0:T(128)S(1)}, f32[32]{0:T(128)}, u32[]{:S(2)}) copy-start(f32[32]{0:T(128)} %get-tuple-element.75) | copy-start | bytes 388
  43.4 9.8 %copy-start.9 = (f32[32]{0:T(128)S(1)}, f32[32]{0:T(128)}, u32[]{:S(2)}) copy-start(f32[32]{0:T(128)} %get-tuple-element.76) | copy-start | bytes 388
  43.4 9.8 %copy-start.10 = (f32[32]{0:T(128)S(1)}, f32[32]{0:T(128)}, u32[]{:S(2)}) copy-start(f32[32]{0:T(128)} %get-tuple-element.77) | copy-start | bytes 388
  43.4 9.8 %copy-start.11 = (f32[32]{0:T(128)S(1)}, f32[32]{0:T(128)}, u32[]{:S(2)}) copy-start(f32[32]{0:T(128)} %get-tuple-element.78) | copy-start | bytes 388
  43.4 9.8 %copy-start.12 = (f32[32]{0:T(128)S(1)}, f32[32]{0:T(128)}, u32[]{:S(2)}) copy-start(f32[32]{0:T(128)} %get-tuple-element.79) | copy-start | bytes 388
  43.4 9.8 %copy-start.13 = (f32[32]{0:T(128)S(1)}, f32[32]{0:T(128)}, u32[]{:S(2)}) copy-start(f32[32]{0:T(128)} %get-tuple-element.80) | copy-start | bytes 388
  43.4 9.8 %copy-start.14 = (f32[32]{0:T(128)S(1)}, f32[32]{0:T(128)}, u32[]{:S(2)}) copy-start(f32[32]{0:T(128)} %get-tuple-element.81) | copy-start | bytes 388
  43.4 9.8 %copy-start.15 = (f32[32]{0:T(128)S(1)}, f32[32]{0:T(128)}, u32[]{:S(2)}) copy-start(f32[32]{0:T(128)} %get-tuple-element.82) | copy-start | bytes 388
  43.4 9.8 %copy-start.16 = (f32[32]{0:T(128)S(1)}, f32[32]{0:T(128)}, u32[]{:S(2)}) copy-start(f32[32]{0:T(128)} %get-tuple-element.83) | copy-start | bytes 388
  43.4 9.8 %copy-start.17 = (f32[32]{0:T(128)S(1)}, f32[32]{0:T(128)}, u32[]{:S(2)}) copy-start(f32[32]{0:T(128)} %get-tuple-element.84) | copy-start | bytes 388
  43.5 9.8 %copy-start.18 = (f32[32]{0:T(128)S(1)}, f32[32]{0:T(128)}, u32[]{:S(2)}) copy-start(f32[32]{0:T(128)} %get-tuple-element.85) | copy-start | bytes 388
  43.5 9.8 %copy-start.19 = (f32[32]{0:T(128)S(1)}, f32[32]{0:T(128)}, u32[]{:S(2)}) copy-start(f32[32]{0:T(128)} %get-tuple-element.86) | copy-start | bytes 388
  46.4 92.5 %collective-permute-start.7 = (bf16[2,384,1536]{2,1,0:T(8,128)(2,1)}, bf16[2,384,1536]{2,1,0:T(8,128)(2,1)S(1)}, u32[]{:S(2)}, u32[]{:S(2)}) collective-permute-start(bf16[2,384,1536]{2,1,0:T(8,128)(2,1)} %pad_maximum_fusion.4), channel_id=1, source_target_pairs={{0,1},{1,0},{2,3},{3,2},{4,5},{5,4},{6,7},{7,6},{8,9},{9,8},{10,11... | collective-permute-start | bytes 7077896 | tf_op jit(solution)/shard_map/ppermute | solution.py:117
  48.6 60.6 %collective-permute-start.3 = (bf16[2,32,16,384]{3,2,1,0:T(8,128)(2,1)}, bf16[2,32,16,384]{3,2,1,0:T(8,128)(2,1)}, u32[]{:S(2)}, u32[]{:S(2)}) collective-permute-start(bf16[2,32,16,384]{3,2,1,0:T(8,128)(2,1)} %pad_maximum_fusion.6), channel_id=1, source_target_pairs={{0,4},{1,8},{2,12},{3,0},{4,5},{5,9},{6,13},{7,1},{8,6},{9,10},{10... | collective-permute-start | bytes 2359304 | tf_op jit(solution)/shard_map/ppermute | solution.py:154
  50.9 71.1 %collective-permute-start.4 = (bf16[2,32,16,384]{3,2,1,0:T(8,128)(2,1)}, bf16[2,32,16,384]{3,2,1,0:T(8,128)(2,1)}, u32[]{:S(2)}, u32[]{:S(2)}) collective-permute-start(bf16[2,32,16,384]{3,2,1,0:T(8,128)(2,1)} %pad_maximum_fusion.7), channel_id=1, source_target_pairs={{0,8},{1,12},{2,0},{3,4},{4,9},{5,13},{6,1},{7,5},{8,10},{9,14},{1... | collective-permute-start | bytes 2359304 | tf_op jit(solution)/shard_map/ppermute | solution.py:154
  58.5 71.7 %collective-permute-start.5 = (bf16[2,32,16,384]{3,2,1,0:T(8,128)(2,1)}, bf16[2,32,16,384]{3,2,1,0:T(8,128)(2,1)}, u32[]{:S(2)}, u32[]{:S(2)}) collective-permute-start(bf16[2,32,16,384]{3,2,1,0:T(8,128)(2,1)} %pad_maximum_fusion.8), channel_id=1, source_target_pairs={{0,12},{1,0},{2,4},{3,8},{4,13},{5,1},{6,5},{7,9},{8,14},{9,2},{10... | collective-permute-start | bytes 2359304 | tf_op jit(solution)/shard_map/ppermute | solution.py:154
  142.8 4.2 %copy-start.3 = (bf16[16,384]{1,0:T(8,128)(2,1)S(1)}, bf16[16,384]{1,0:T(8,128)(2,1)}, u32[]{:S(2)}) copy-start(bf16[16,384]{1,0:T(8,128)(2,1)} %get-tuple-element.64) | copy-start | bytes 36868
  147.0 6.6 %copy-start.1 = (bf16[1536,1536]{1,0:T(8,128)(2,1)}, bf16[1536,1536]{1,0:T(8,128)(2,1)S(1)}, u32[]{:S(2)}) copy-start(bf16[1536,1536]{1,0:T(8,128)(2,1)S(1)} %fusion.3) | copy-start | bytes 14155780
  147.0 3.6 %copy-start.2 = (bf16[16,384]{1,0:T(8,128)(2,1)S(1)}, bf16[16,384]{1,0:T(8,128)(2,1)}, u32[]{:S(2)}) copy-start(bf16[16,384]{1,0:T(8,128)(2,1)} %get-tuple-element.62) | copy-start | bytes 36868
  153.6 3.4 %copy-start.4 = (bf16[16,384]{1,0:T(8,128)(2,1)S(1)}, bf16[16,384]{1,0:T(8,128)(2,1)}, u32[]{:S(2)}) copy-start(bf16[16,384]{1,0:T(8,128)(2,1)} %get-tuple-element.61) | copy-start | bytes 36868

commit v8 on v6

--- a/solution.py
+++ b/solution.py
@@ -112,8 +112,14 @@
     taps_kept = masked_taps(fringe_taps, tap_windows)
     class_starts = jnp.cumsum(class_counts) - class_counts
 
+    pad_b = ((0, 0), (0, SLOTS), (0, 0), (0, 0))
+    local = jnp.pad(visibilities, pad_b)
     padded = extended(visibilities, (("tm", 2),), REACH)
-    padded = jnp.pad(padded, ((0, 0), (0, SLOTS), (0, 0), (0, 0)))
+    inner = t_in - 2 * REACH
+    if inner > 0:
+        head_src = jnp.pad(lax.slice_in_dim(padded, 0, 3 * REACH, axis=2), pad_b)
+        tail_src = jnp.pad(lax.slice_in_dim(padded, t_in - REACH, t_in + 2 * REACH, axis=2), pad_b)
+    padded = jnp.pad(padded, pad_b)
 
     if q == 1 and nf & (nf - 1) == 0:
         blocks = filter_panels[0][None]
@@ -143,8 +149,6 @@
     c_own = a
     u_src = (a % q) * nf + b
     fit = None
-    local = jnp.pad(visibilities, ((0, 0), (0, SLOTS), (0, 0), (0, 0)))
-    inner = t_in - 2 * REACH
     for r in range(nt):
         c_send = (u_src + r) % nt
         start = class_starts[c_send]
@@ -156,20 +160,18 @@
                 u = (sa % q) * nf + sb
                 dc = (u + r) % nt
                 perm.append((sa * nf + sb, dc * nf + sa // q))
-        if inner > 0:
+        if r == 0 and inner > 0:
             own = lax.optimization_barrier(lax.dynamic_slice_in_dim(local, start, SLOTS, axis=1))
             middle = convolve_class(own, taps, count, inner)
             got_mid = lax.ppermute(middle, ("tm", "freq"), perm)
-        rows = lax.optimization_barrier(lax.dynamic_slice_in_dim(padded, start, SLOTS, axis=1))
-        if inner > 0:
-            head = convolve_class(rows[:, :, : 3 * REACH], taps, count, REACH)
-            tail = convolve_class(rows[:, :, t_in - REACH :], taps, count, REACH)
-            chunk = jnp.concatenate([head, tail], axis=2)
+            head = convolve_class(lax.dynamic_slice_in_dim(head_src, start, SLOTS, axis=1), taps, count, REACH)
+            tail = convolve_class(lax.dynamic_slice_in_dim(tail_src, start, SLOTS, axis=1), taps, count, REACH)
+            got = lax.ppermute(jnp.concatenate([head, tail], axis=2), ("tm", "freq"), perm)
+            got = jnp.concatenate([got[:, :, :REACH], got_mid, got[:, :, REACH:]], axis=2)
         else:
+            rows = lax.optimization_barrier(lax.dynamic_slice_in_dim(padded, start, SLOTS, axis=1))
             chunk = convolve_class(rows, taps, count, t_in)
-        got = lax.ppermute(chunk, ("tm", "freq"), perm)
-        if inner > 0:
-            got = jnp.concatenate([got[:, :, :REACH], got_mid, got[:, :, REACH:]], axis=2)
+            got = lax.ppermute(chunk, ("tm", "freq"), perm)
         u_dst = (c_own - r) % nt
         t_sub = u_dst // nf
         b_src = u_dst % nf

time: 154 us -> 171 us (1.11); the launches traced: 151 us -> 170 us
  waiting for transfers between devices: 56.6 us -> 66.8 us
  local copies, waits for them, and re-layouts: 13.4 us -> 18.3 us
  other arithmetic: 39 us -> 42.8 us
    ppermute x1, waiting for transfers between devices: 0.01 us -> 8.28 us  [extended(): lax.ppermute(tail, axis, [(i, (i + 1) % count) for i in range(ends)])]
    ppermute x4 -> x3, waiting for transfers between devices: 51.8 us -> 58.5 us  [shards(): got = lax.ppermute(chunk, ('tm', 'freq'), perm)]
    ppermute x4 -> x1, waiting for transfers between devices: 4.73 us -> 0.01 us  [shards(): got_mid = lax.ppermute(middle, ('tm', 'freq'), perm)]
    dynamic_update_slice x0 -> x3, local copies, waits for them, and re-layouts: none -> 3.9 us  [shards(): lax.dynamic_update_slice_in_dim(slotted, got, b_src * f_blk, axis=3)]
    concatenate x1 -> x2, other arithmetic: 1.5 us -> 4.04 us  [extended(): jnp.concatenate([lax.ppermute(tail, axis, [(i, (i + 1) % count) for i in...]
    dynamic_slice x1, local copies, waits for them, and re-layouts: 2.99 us -> 0.46 us  [shards(): lax.dynamic_slice_in_dim(padded, start, SLOTS, axis=1)]
    dynamic_update_slice x4 -> x1, other arithmetic: 4.07 us -> 1.61 us  [shards(): lax.dynamic_update_slice_in_dim(slotted, got, b_src * f_blk, axis=3)]
    ppermute x0 -> x1, starting transfers between devices: none -> 2.29 us  [shards(): lax.ppermute(jnp.concatenate([head, tail], axis=2), ('tm', 'freq'), perm)]
  transfers between devices with their start and end apart: 12 -> 9, of which waited for: 5 -> 3; matrix products, arithmetic and copies ran while one was open for 28% -> 24% of each run, Pallas kernels for 0% -> 0%
where the time goes in v8:
time: 171 us; the launch traced here: 170 us
  waiting for transfers between devices  66.8 us (39%)
  other arithmetic  42.8 us (25%)
  local copies, waits for them, and re-layouts  18.3 us (11%)
  starting transfers between devices  16.9 us (10%)
  matrix products  16.5 us (10%)
  between operations  8.64 us (5%)
    ppermute x3, waiting for transfers between devices, shards(): got = lax.ppermute(chunk, ('tm', 'freq'), perm)  58.5 us
    another operation x13, other arithmetic  18.8 us
    dot_general x4, matrix products, shards(): jnp.einsum('rstj,ij->rsti', weighted, cols, preferred_element_type=jnp.fl...  16.5 us
    ppermute x1, waiting for transfers between devices, extended(): lax.ppermute(tail, axis, [(i, (i + 1) % count) for i in range(ends)])  8.28 us
    unnamed x126, local copies, waits for them, and re-layouts  5.27 us
    ppermute x1, starting transfers between devices, extended(): lax.ppermute(tail, axis, [(i, (i + 1) % count) for i in range(ends)])  4.97 us
    ppermute x3, starting transfers between devices, shards(): got = lax.ppermute(chunk, ('tm', 'freq'), perm)  4.35 us
    concatenate x1, other arithmetic, shards(): panel = jnp.concatenate([panel, panel], axis=1)  4.16 us
  transfers between devices with their start and end apart: 9, of which 3 were waited for; matrix products, arithmetic and copies ran while one was open for 24% of the time, Pallas kernels for 0%

profile of v8, /device:TPU:14, one launch (start us, length us, event | category | flops | bytes accessed | tf_op | source)
XLA Modules:
  0.0 169.9 jit_solution(11951629686820216674)
XLA Ops:
  0.0 0.8 reduce-window.9
  2.9 1.5 fusion.245
  7.2 1.3 pad_dynamic-slice_fusion.2
  8.6 1.1 fusion.168
  9.7 1.1 fusion.167
  11.0 0.8 pad_maximum_fusion.9
  11.8 2.9 %collective-permute-start.3 = (bf16[2,32,8,384]{3,2,1,0:T(8,128)(2,1)}, bf16[2,32,8,384]{3,2,1,0:T(8,128)(2,1)}, u32[]{:S(2)}, u32[]{:S(2)}) collective-permute-start(bf16[2,32,8,384]{3,2,1,0:T(8,128)(2,1)} %pad_maximum_fusion.9), channel_id=1, source_target_pairs={{0,0},{1,4},{2,8},{3,12},{4,1},{5,5},{6,9},{7,13},{8,2},{9,6},{10,... | collective-permute-start | bytes 1179656 | tf_op jit(solution)/shard_map/ppermute | solution.py:166
  14.8 1.6 copy.8
  16.3 2.0 %fusion.243 = (bf16[2,66,4,384]{3,1,2,0:T(8,128)(2,1)}, bf16[2,66,4,384]{3,1,2,0:T(8,128)(2,1)S(1)}) fusion(bf16[2,66,16,384]{3,1,2,0:T(8,128)(2,1)} %copy.8), kind=kLoop, calls=%fused_computation.590 | loop fusion | bytes 1622016 | tf_op jit(solution)/shard_map/slice | solution.py:18
  18.4 5.0 %collective-permute-start = (bf16[2,66,4,384]{3,1,2,0:T(8,128)(2,1)}, bf16[2,66,4,384]{3,1,2,0:T(8,128)(2,1)S(1)}, u32[]{:S(2)}, u32[]{:S(2)}) collective-permute-start(bf16[2,66,4,384]{3,1,2,0:T(8,128)(2,1)} %get-tuple-element.59), channel_id=1, source_target_pairs={{0,4},{4,8},{8,12},{1,5},{5,9},{9,13},{2,6},{6,10},{10,14},{3,7},{... | collective-permute-start | bytes 1216520 | tf_op jit(solution)/shard_map/ppermute | solution.py:21
  23.3 1.9 %collective-permute-start.1 = (bf16[2,66,4,384]{3,1,2,0:T(8,128)(2,1)S(1)}, bf16[2,66,4,384]{3,1,2,0:T(8,128)(2,1)}, u32[]{:S(2)}, u32[]{:S(2)}) collective-permute-start(bf16[2,66,4,384]{3,1,2,0:T(8,128)(2,1)S(1)} %get-tuple-element.60), channel_id=1, source_target_pairs={{4,0},{8,4},{12,8},{5,1},{9,5},{13,9},{6,2},{10,6},{14,10},{7,3},{... | collective-permute-start | bytes 1216520 | tf_op jit(solution)/shard_map/ppermute | solution.py:23
  33.7 8.3 %collective-permute-done = bf16[2,66,4,384]{3,1,2,0:T(8,128)(2,1)S(1)} collective-permute-done((bf16[2,66,4,384]{3,1,2,0:T(8,128)(2,1)}, bf16[2,66,4,384]{3,1,2,0:T(8,128)(2,1)S(1)}, u32[]{:S(2)}, u32[]{:S(2)}) %collective-permute-start) | collective-permute-done | bytes 405536 | tf_op jit(solution)/shard_map/ppermute | solution.py:21
  41.9 0.8 copy-done.7
  42.7 2.4 %fusion.127 = (bf16[2,32,12,384]{3,1,2,0:T(8,128)(2,1)S(1)}, bf16[2,32,12,384]{3,1,2,0:T(8,128)(2,1)S(1)}) fusion(s32[]{:T(128)S(6)} %select_n.113, bf16[2,66,4,384]{3,1,2,0:T(8,128)(2,1)} %copy-done.7, bf16[2,66,16,384]{3,1,2,0:T(8,128)(2,1)} %copy.8, bf16[2,66,4,384]{3,1,2,0:T(8,128)(2,1)} %collective-permute-done.1), kind=kLoop, calls=%fused_computation.266 | loop fusion | flops 4128768 | bytes 3613696 | tf_op jit(solution)/shard_map/concatenate | solution.py:19
  45.1 1.1 fusion.240
  46.3 1.2 fusion.241
  48.7 1.2 copy.15
  49.8 1.7 fusion.5
  52.0 2.1 %fusion.124 = bf16[1,32,16,384]{3,2,1,0:T(8,128)(2,1)S(1)} fusion(f32[32]{0:T(128)S(1)} %get-tuple-element.122, f32[32]{0:T(128)S(1)} %get-tuple-element.123, f32[32]{0:T(128)S(1)} %get-tuple-element.124, f32[32]{0:T(128)S(1)} %get-tuple-element.125, f32[32]{0:T(128)S(1)} %get-tuple-element.126, f32[32]{0:T(128)S(1)} %get-tuple-element.127, ...), kind=kLoop, calls=%fused_computation.263 | loop fusion | flops 10616832 | bytes 7473408 | tf_op jit(solution)/shard_map/convert.2
  54.2 2.1 %fusion.123 = bf16[1,32,16,384]{3,2,1,0:T(8,128)(2,1)S(1)} fusion(f32[32]{0:T(128)S(1)} %get-tuple-element.122, f32[32]{0:T(128)S(1)} %get-tuple-element.123, f32[32]{0:T(128)S(1)} %get-tuple-element.124, f32[32]{0:T(128)S(1)} %get-tuple-element.125, f32[32]{0:T(128)S(1)} %get-tuple-element.126, f32[32]{0:T(128)S(1)} %get-tuple-element.127, ...), kind=kLoop, calls=%fused_computation.262 | loop fusion | flops 10616832 | bytes 7473408 | tf_op jit(solution)/shard_map/convert.3
  56.4 2.3 %collective-permute-start.2 = (bf16[2,32,8,384]{3,1,2,0:T(8,128)(2,1)S(1)}, bf16[2,32,8,384]{3,1,2,0:T(8,128)(2,1)}, u32[]{:S(2)}, u32[]{:S(2)}) collective-permute-start(bf16[2,32,8,384]{3,1,2,0:T(8,128)(2,1)S(1)} %maximum_maximum_fusion), channel_id=1, source_target_pairs={{0,0},{1,4},{2,8},{3,12},{4,1},{5,5},{6,9},{7,13},{8,2},{9,6},{10,... | collective-permute-start | bytes 1179656 | tf_op jit(solution)/shard_map/ppermute | solution.py:169
  58.9 2.1 %fusion.122 = bf16[1,32,16,384]{3,2,1,0:T(8,128)(2,1)S(1)} fusion(f32[32]{0:T(128)S(1)} %copy-done.45, f32[32]{0:T(128)S(1)} %copy-done.46, f32[32]{0:T(128)S(1)} %copy-done.47, f32[32]{0:T(128)S(1)} %copy-done.48, f32[32]{0:T(128)S(1)} %copy-done.49, f32[32]{0:T(128)S(1)} %copy-done.50, f32[32]{0:T(128)S(1)} %copy-done.51, f32[32]{0:T(128)S(1)} %copy-done.52, ...), kind=kLoop, calls=%fused_computation.261 | loop fusion | flops 10616832 | bytes 7473408 | tf_op jit(solution)/shard_map/convert
  61.0 2.1 %fusion.121 = bf16[1,32,16,384]{3,2,1,0:T(8,128)(2,1)S(1)} fusion(f32[32]{0:T(128)S(1)} %copy-done.45, f32[32]{0:T(128)S(1)} %copy-done.46, f32[32]{0:T(128)S(1)} %copy-done.47, f32[32]{0:T(128)S(1)} %copy-done.48, f32[32]{0:T(128)S(1)} %copy-done.49, f32[32]{0:T(128)S(1)} %copy-done.50, f32[32]{0:T(128)S(1)} %copy-done.51, f32[32]{0:T(128)S(1)} %copy-done.52, ...), kind=kLoop, calls=%fused_computation.260 | loop fusion | flops 10616832 | bytes 7473408 | tf_op jit(solution)/shard_map/convert.1
  63.1 1.0 copy-done.1
  64.1 1.6 pad_maximum_fusion.4
  66.2 2.1 %fusion.126 = bf16[1,32,16,384]{3,2,1,0:T(8,128)(2,1)S(1)} fusion(f32[32]{0:T(128)S(1)} %get-tuple-element.86, f32[32]{0:T(128)S(1)} %get-tuple-element.87, f32[32]{0:T(128)S(1)} %get-tuple-element.88, f32[32]{0:T(128)S(1)} %get-tuple-element.89, f32[32]{0:T(128)S(1)} %get-tuple-element.90, f32[32]{0:T(128)S(1)} %get-tuple-element.91, ...), kind=kLoop, calls=%fused_computation.265 | loop fusion | flops 10616832 | bytes 7473408 | tf_op jit(solution)/shard_map/convert.4
  68.2 2.1 %fusion.125 = bf16[1,32,16,384]{3,2,1,0:T(8,128)(2,1)S(1)} fusion(f32[32]{0:T(128)S(1)} %get-tuple-element.86, f32[32]{0:T(128)S(1)} %get-tuple-element.87, f32[32]{0:T(128)S(1)} %get-tuple-element.88, f32[32]{0:T(128)S(1)} %get-tuple-element.89, f32[32]{0:T(128)S(1)} %get-tuple-element.90, f32[32]{0:T(128)S(1)} %get-tuple-element.91, ...), kind=kLoop, calls=%fused_computation.264 | loop fusion | flops 10616832 | bytes 7473408 | tf_op jit(solution)/shard_map/convert.5
  70.3 1.0 pad_maximum_fusion.6
  71.3 3.1 %collective-permute-start.4 = (bf16[2,32,16,384]{3,2,1,0:T(8,128)(2,1)}, bf16[2,32,16,384]{3,2,1,0:T(8,128)(2,1)}, u32[]{:S(2)}, u32[]{:S(2)}) collective-permute-start(bf16[2,32,16,384]{3,2,1,0:T(8,128)(2,1)} %pad_maximum_fusion.6), channel_id=1, source_target_pairs={{0,4},{1,8},{2,12},{3,0},{4,5},{5,9},{6,13},{7,1},{8,6},{9,10},{10... | collective-permute-start | bytes 2359304 | tf_op jit(solution)/shard_map/ppermute | solution.py:174
  74.5 1.0 pad_maximum_fusion.7
  75.9 1.0 pad_maximum_fusion.8
  76.9 0.8 collective-permute-start.6
  77.7 1.4 dynamic-slice_convert_fusion
  79.1 1.1 fusion.244
  80.8 1.6 fusion.169
  82.4 22.7 %collective-permute-done.4 = bf16[2,32,16,384]{3,2,1,0:T(8,128)(2,1)} collective-permute-done((bf16[2,32,16,384]{3,2,1,0:T(8,128)(2,1)}, bf16[2,32,16,384]{3,2,1,0:T(8,128)(2,1)}, u32[]{:S(2)}, u32[]{:S(2)}) %collective-permute-start.4) | collective-permute-done | bytes 786464 | tf_op jit(solution)/shard_map/ppermute | solution.py:174
  105.2 1.3 constant_dynamic-update-slice_fusion.2
  106.5 35.7 %collective-permute-done.5 = bf16[2,32,16,384]{3,2,1,0:T(8,128)(2,1)} collective-permute-done((bf16[2,32,16,384]{3,2,1,0:T(8,128)(2,1)}, bf16[2,32,16,384]{3,2,1,0:T(8,128)(2,1)}, u32[]{:S(2)}, u32[]{:S(2)}) %collective-permute-start.5) | collective-permute-done | bytes 786464 | tf_op jit(solution)/shard_map/ppermute | solution.py:174
  142.2 1.3 constant_dynamic-update-slice_fusion.1
  143.5 1.3 constant_dynamic-update-slice_fusion
  144.9 1.6 copy-done.6
  146.5 2.6 %conditional.1 = (bf16[1536,1536]{1,0:T(8,128)(2,1)}) conditional(s32[]{:T(128)} %clamp.3, (bf16[1,384,1536]{2,1,0:T(8,128)(2,1)S(1)}, bf16[2,384,1536]{2,1,0:T(8,128)(2,1)S(1)}, bf16[1,384,1536]{2,1,0:T(8,128)(2,1)S(1)}) %tuple.122, (bf16[2,384,1536]{2,1,0:T(8,128)(2,1)S(1)}, bf16[1,384,1536]{2,1,0:T(8,128)(2,1)S(1)}, ...), branch_computations={%region_1.2_spmd, %region_2.3_spmd, %region_3.4_spmd, %region_4.5_... | conditional | flops 18874368 | bytes 14155784 | solution.py:141
  146.7 2.4 %pad_maximum_fusion.2 = bf16[1536,1536]{1,0:T(8,128)(2,1)} fusion(bf16[384,1536]{1,0:T(8,128)(2,1)S(1)} %get-tuple-element.51, bf16[384,1536]{1,0:T(8,128)(2,1)S(1)} %bitcast.214, bf16[384,1536]{1,0:T(8,128)(2,1)S(1)} %get-tuple-element.50, bf16[384,1536]{1,0:T(8,128)(2,1)S(1)} %bitcast.218), kind=kLoop, calls=%fused_computation.6 | loop fusion | flops 18874368 | bytes 9437184 | tf_op jit(solution)/shard_map/cond/branch_2_fun/concatenate | solution.py:31
  149.1 4.2 %fusion.3 = bf16[1536,1536]{1,0:T(8,128)(2,1)S(1)} fusion(s32[]{:T(128)S(6)} %select_n.136, bf16[1536,1536]{1,0:T(8,128)(2,1)} %get-tuple-element.155), kind=kLoop, calls=%fused_computation.19 | loop fusion | flops 9437184 | bytes 9437188 | tf_op jit(solution)/shard_map/concatenate | solution.py:146
  153.3 3.6 %fusion.8 = f32[2,32,16,1536]{3,2,1,0:T(8,128)S(1)} fusion(bf16[1536,1536]{1,0:T(8,128)(2,1)S(1)} %fusion.3, bf16[2,32,16,384]{3,2,1,0:T(8,128)(2,1)} %collective-permute-done.5, bf16[16,384]{1,0:T(8,128)(2,1)S(1)} %copy-done.14), kind=kOutput, calls=%fused_computation.32 | convolution fusion | flops 1208352768 | bytes 8269824 | tf_op jit(solution)/shard_map/rstj,ij->rsti/dot_general | solution.py:185
  156.9 3.0 %fusion.9 = f32[2,32,16,1536]{3,2,1,0:T(8,128)S(1)} fusion(bf16[1536,1536]{1,0:T(8,128)(2,1)S(1)} %fusion.3, bf16[2,32,16,384]{3,2,1,0:T(8,128)(2,1)} %collective-permute-done.4, bf16[16,384]{1,0:T(8,128)(2,1)S(1)} %copy-done.13), kind=kOutput, calls=%fused_computation.34 | convolution fusion | flops 1208352768 | bytes 8269824 | tf_op jit(solution)/shard_map/rstj,ij->rsti/dot_general | solution.py:185
  160.0 3.2 %fusion.10 = f32[2,32,16,1536]{3,2,1,0:T(8,128)S(1)} fusion(bf16[1536,1536]{1,0:T(8,128)(2,1)} %copy-done.3, bf16[16,384]{1,0:T(8,128)(2,1)S(1)} %get-tuple-element.65, bf16[2,32,4,384]{3,2,1,0:T(4,128)(2,1)S(1)} %copy-done.12, bf16[2,32,8,384]{3,2,1,0:T(8,128)(2,1)} %collective-permute-done.3, bf16[2,32,4,384]{3,2,1,0:T(4,128)(2,1)S(1)} %copy-done.10), kind=kOutput, calls=%fused_computation.36 | convolution fusion | flops 1211105280 | bytes 8269824 | tf_op jit(solution)/shard_map/rstj,ij->rsti/dot_general | solution.py:185
  163.3 6.7 %fusion.6 = bf16[2,1,32,16,1536]{4,3,2,1,0:T(8,128)(2,1)} fusion(f32[2,32,16,1536]{3,2,1,0:T(8,128)S(1)} %fusion.8, f32[2,32,16,1536]{3,2,1,0:T(8,128)S(1)} %fusion.10, f32[2,32,16,1536]{3,2,1,0:T(8,128)S(1)} %fusion.9, bf16[2,32,16,1536]{3,2,1,0:T(8,128)(2,1)} %copy-done.6, bf16[1536,1536]{1,0:T(8,128)(2,1)} %copy-done.3, ...), kind=kOutput, calls=%fused_computation.22 | convolution fusion | flops 1217789952 | bytes 27144192 | tf_op jit(solution)/shard_map/rstj,ij->rsti/dot_general | solution.py:185
  (157 shorter events, 9.1 us)
Async XLA Ops:
  6.4 4.4 %copy-start.16 = (f32[32]{0:T(128)}, f32[32]{0:T(128)S(1)}, u32[]{:S(2)}) copy-start(f32[32]{0:T(128)S(1)} %get-tuple-element.107) | copy-start | bytes 388
  9.7 5.0 %copy-start = (bf16[1,384,1536]{2,1,0:T(8,128)(2,1)S(1)}, bf16[1,384,1536]{2,1,0:T(8,128)(2,1)}, u32[]{:S(2)}) copy-start(bf16[1,384,1536]{2,1,0:T(8,128)(2,1)} %param.16) | copy-start | bytes 3538948
  9.7 5.1 %copy-start.4 = (bf16[2,66,16,384]{3,2,1,0:T(8,128)(2,1)S(1)}, bf16[2,66,16,384]{3,2,1,0:T(8,128)(2,1)}, u32[]{:S(2)}) copy-start(bf16[2,66,16,384]{3,2,1,0:T(8,128)(2,1)} %param.11) | copy-start | bytes 4866052
  11.8 68.6 %collective-permute-start.3 = (bf16[2,32,8,384]{3,2,1,0:T(8,128)(2,1)}, bf16[2,32,8,384]{3,2,1,0:T(8,128)(2,1)}, u32[]{:S(2)}, u32[]{:S(2)}) collective-permute-start(bf16[2,32,8,384]{3,2,1,0:T(8,128)(2,1)} %pad_maximum_fusion.9), channel_id=1, source_target_pairs={{0,0},{1,4},{2,8},{3,12},{4,1},{5,5},{6,9},{7,13},{8,2},{9,6},{10,... | collective-permute-start | bytes 1179656 | tf_op jit(solution)/shard_map/ppermute | solution.py:166
  14.7 48.4 %collective-permute-start.7 = (bf16[1,384,1536]{2,1,0:T(8,128)(2,1)S(1)}, bf16[1,384,1536]{2,1,0:T(8,128)(2,1)S(1)}, u32[]{:S(2)}, u32[]{:S(2)}) collective-permute-start(bf16[1,384,1536]{2,1,0:T(8,128)(2,1)S(1)} %copy-done), channel_id=1, source_target_pairs={{0,2},{1,3},{2,0},{3,1},{4,6},{5,7},{6,4},{7,5},{8,10},{9,11},{10,... | collective-permute-start | bytes 3538952 | tf_op jit(solution)/shard_map/ppermute | solution.py:129
  18.4 23.6 %collective-permute-start = (bf16[2,66,4,384]{3,1,2,0:T(8,128)(2,1)}, bf16[2,66,4,384]{3,1,2,0:T(8,128)(2,1)S(1)}, u32[]{:S(2)}, u32[]{:S(2)}) collective-permute-start(bf16[2,66,4,384]{3,1,2,0:T(8,128)(2,1)} %get-tuple-element.59), channel_id=1, source_target_pairs={{0,4},{4,8},{8,12},{1,5},{5,9},{9,13},{2,6},{6,10},{10,14},{3,7},{... | collective-permute-start | bytes 1216520 | tf_op jit(solution)/shard_map/ppermute | solution.py:21
  23.3 19.4 %collective-permute-start.1 = (bf16[2,66,4,384]{3,1,2,0:T(8,128)(2,1)S(1)}, bf16[2,66,4,384]{3,1,2,0:T(8,128)(2,1)}, u32[]{:S(2)}, u32[]{:S(2)}) collective-permute-start(bf16[2,66,4,384]{3,1,2,0:T(8,128)(2,1)S(1)} %get-tuple-element.60), channel_id=1, source_target_pairs={{4,0},{8,4},{12,8},{5,1},{9,5},{13,9},{6,2},{10,6},{14,10},{7,3},{... | collective-permute-start | bytes 1216520 | tf_op jit(solution)/shard_map/ppermute | solution.py:23
  33.5 14.0 %copy-start.17 = (f32[32]{0:T(128)S(1)}, f32[32]{0:T(128)}, u32[]{:S(2)}) copy-start(f32[32]{0:T(128)} %copy-done.16) | copy-start | bytes 388
  33.5 14.0 %copy-start.19 = (f32[32]{0:T(128)S(1)}, f32[32]{0:T(128)}, u32[]{:S(2)}) copy-start(f32[32]{0:T(128)} %copy-done.18) | copy-start | bytes 388
  33.5 14.0 %copy-start.21 = (f32[32]{0:T(128)S(1)}, f32[32]{0:T(128)}, u32[]{:S(2)}) copy-start(f32[32]{0:T(128)} %copy-done.20) | copy-start | bytes 388
  33.5 14.0 %copy-start.23 = (f32[32]{0:T(128)S(1)}, f32[32]{0:T(128)}, u32[]{:S(2)}) copy-start(f32[32]{0:T(128)} %copy-done.22) | copy-start | bytes 388
  33.6 14.0 %copy-start.25 = (f32[32]{0:T(128)S(1)}, f32[32]{0:T(128)}, u32[]{:S(2)}) copy-start(f32[32]{0:T(128)} %copy-done.24) | copy-start | bytes 388
  33.6 14.0 %copy-start.27 = (f32[32]{0:T(128)S(1)}, f32[32]{0:T(128)}, u32[]{:S(2)}) copy-start(f32[32]{0:T(128)} %copy-done.26) | copy-start | bytes 388
  33.6 14.0 %copy-start.29 = (f32[32]{0:T(128)S(1)}, f32[32]{0:T(128)}, u32[]{:S(2)}) copy-start(f32[32]{0:T(128)} %copy-done.28) | copy-start | bytes 388
  33.6 14.0 %copy-start.31 = (f32[32]{0:T(128)S(1)}, f32[32]{0:T(128)}, u32[]{:S(2)}) copy-start(f32[32]{0:T(128)} %copy-done.30) | copy-start | bytes 388
  33.6 14.0 %copy-start.33 = (f32[32]{0:T(128)S(1)}, f32[32]{0:T(128)}, u32[]{:S(2)}) copy-start(f32[32]{0:T(128)} %copy-done.32) | copy-start | bytes 388
  33.6 14.0 %copy-start.35 = (f32[32]{0:T(128)S(1)}, f32[32]{0:T(128)}, u32[]{:S(2)}) copy-start(f32[32]{0:T(128)} %copy-done.34) | copy-start | bytes 388
  33.6 14.0 %copy-start.37 = (f32[32]{0:T(128)S(1)}, f32[32]{0:T(128)}, u32[]{:S(2)}) copy-start(f32[32]{0:T(128)} %copy-done.36) | copy-start | bytes 388
  33.6 14.0 %copy-start.39 = (f32[32]{0:T(128)S(1)}, f32[32]{0:T(128)}, u32[]{:S(2)}) copy-start(f32[32]{0:T(128)} %copy-done.38) | copy-start | bytes 388
  33.6 14.0 %copy-start.41 = (f32[32]{0:T(128)S(1)}, f32[32]{0:T(128)}, u32[]{:S(2)}) copy-start(f32[32]{0:T(128)} %copy-done.40) | copy-start | bytes 388
  33.6 14.0 %copy-start.43 = (f32[32]{0:T(128)S(1)}, f32[32]{0:T(128)}, u32[]{:S(2)}) copy-start(f32[32]{0:T(128)} %copy-done.42) | copy-start | bytes 388
  54.1 4.6 %copy-start.44 = (f32[32]{0:T(128)S(1)}, f32[32]{0:T(128)}, u32[]{:S(2)}) copy-start(f32[32]{0:T(128)} %get-tuple-element.67) | copy-start | bytes 388
  54.1 4.6 %copy-start.45 = (f32[32]{0:T(128)S(1)}, f32[32]{0:T(128)}, u32[]{:S(2)}) copy-start(f32[32]{0:T(128)} %get-tuple-element.68) | copy-start | bytes 388
  54.1 4.6 %copy-start.46 = (f32[32]{0:T(128)S(1)}, f32[32]{0:T(128)}, u32[]{:S(2)}) copy-start(f32[32]{0:T(128)} %get-tuple-element.69) | copy-start | bytes 388
  54.1 4.6 %copy-start.47 = (f32[32]{0:T(128)S(1)}, f32[32]{0:T(128)}, u32[]{:S(2)}) copy-start(f32[32]{0:T(128)} %get-tuple-element.70) | copy-start | bytes 388
  54.1 4.6 %copy-start.48 = (f32[32]{0:T(128)S(1)}, f32[32]{0:T(128)}, u32[]{:S(2)}) copy-start(f32[32]{0:T(128)} %get-tuple-element.71) | copy-start | bytes 388
  54.1 4.6 %copy-start.49 = (f32[32]{0:T(128)S(1)}, f32[32]{0:T(128)}, u32[]{:S(2)}) copy-start(f32[32]{0:T(128)} %get-tuple-element.72) | copy-start | bytes 388
  54.1 4.6 %copy-start.50 = (f32[32]{0:T(128)S(1)}, f32[32]{0:T(128)}, u32[]{:S(2)}) copy-start(f32[32]{0:T(128)} %get-tuple-element.73) | copy-start | bytes 388
  54.1 4.6 %copy-start.51 = (f32[32]{0:T(128)S(1)}, f32[32]{0:T(128)}, u32[]{:S(2)}) copy-start(f32[32]{0:T(128)} %get-tuple-element.74) | copy-start | bytes 388
  54.1 4.6 %copy-start.52 = (f32[32]{0:T(128)S(1)}, f32[32]{0:T(128)}, u32[]{:S(2)}) copy-start(f32[32]{0:T(128)} %get-tuple-element.75) | copy-start | bytes 388
  54.2 4.6 %copy-start.53 = (f32[32]{0:T(128)S(1)}, f32[32]{0:T(128)}, u32[]{:S(2)}) copy-start(f32[32]{0:T(128)} %get-tuple-element.76) | copy-start | bytes 388
  54.2 4.6 %copy-start.54 = (f32[32]{0:T(128)S(1)}, f32[32]{0:T(128)}, u32[]{:S(2)}) copy-start(f32[32]{0:T(128)} %get-tuple-element.77) | copy-start | bytes 388
  54.2 4.6 %copy-start.55 = (f32[32]{0:T(128)S(1)}, f32[32]{0:T(128)}, u32[]{:S(2)}) copy-start(f32[32]{0:T(128)} %get-tuple-element.78) | copy-start | bytes 388
  54.2 4.6 %copy-start.56 = (f32[32]{0:T(128)S(1)}, f32[32]{0:T(128)}, u32[]{:S(2)}) copy-start(f32[32]{0:T(128)} %get-tuple-element.79) | copy-start | bytes 388
  54.2 4.6 %copy-start.57 = (f32[32]{0:T(128)S(1)}, f32[32]{0:T(128)}, u32[]{:S(2)}) copy-start(f32[32]{0:T(128)} %get-tuple-element.80) | copy-start | bytes 388
  54.2 4.6 %copy-start.58 = (f32[32]{0:T(128)S(1)}, f32[32]{0:T(128)}, u32[]{:S(2)}) copy-start(f32[32]{0:T(128)} %get-tuple-element.81) | copy-start | bytes 388
  54.2 4.6 %copy-start.59 = (f32[32]{0:T(128)S(1)}, f32[32]{0:T(128)}, u32[]{:S(2)}) copy-start(f32[32]{0:T(128)} %get-tuple-element.82) | copy-start | bytes 388
  54.2 4.6 %copy-start.60 = (f32[32]{0:T(128)S(1)}, f32[32]{0:T(128)}, u32[]{:S(2)}) copy-start(f32[32]{0:T(128)} %get-tuple-element.83) | copy-start | bytes 388
  54.2 4.6 %copy-start.61 = (f32[32]{0:T(128)S(1)}, f32[32]{0:T(128)}, u32[]{:S(2)}) copy-start(f32[32]{0:T(128)} %get-tuple-element.84) | copy-start | bytes 388
  56.4 20.5 %collective-permute-start.2 = (bf16[2,32,8,384]{3,1,2,0:T(8,128)(2,1)S(1)}, bf16[2,32,8,384]{3,1,2,0:T(8,128)(2,1)}, u32[]{:S(2)}, u32[]{:S(2)}) collective-permute-start(bf16[2,32,8,384]{3,1,2,0:T(8,128)(2,1)S(1)} %maximum_maximum_fusion), channel_id=1, source_target_pairs={{0,0},{1,4},{2,8},{3,12},{4,1},{5,5},{6,9},{7,13},{8,2},{9,6},{10,... | collective-permute-start | bytes 1179656 | tf_op jit(solution)/shard_map/ppermute | solution.py:169
  65.7 79.2 %collective-permute-start.8 = (bf16[2,384,1536]{2,1,0:T(8,128)(2,1)}, bf16[2,384,1536]{2,1,0:T(8,128)(2,1)S(1)}, u32[]{:S(2)}, u32[]{:S(2)}) collective-permute-start(bf16[2,384,1536]{2,1,0:T(8,128)(2,1)} %pad_maximum_fusion.4), channel_id=1, source_target_pairs={{0,1},{1,0},{2,3},{3,2},{4,5},{5,4},{6,7},{7,6},{8,9},{9,8},{10,11... | collective-permute-start | bytes 7077896 | tf_op jit(solution)/shard_map/ppermute | solution.py:129
  71.3 33.8 %collective-permute-start.4 = (bf16[2,32,16,384]{3,2,1,0:T(8,128)(2,1)}, bf16[2,32,16,384]{3,2,1,0:T(8,128)(2,1)}, u32[]{:S(2)}, u32[]{:S(2)}) collective-permute-start(bf16[2,32,16,384]{3,2,1,0:T(8,128)(2,1)} %pad_maximum_fusion.6), channel_id=1, source_target_pairs={{0,4},{1,8},{2,12},{3,0},{4,5},{5,9},{6,13},{7,1},{8,6},{9,10},{10... | collective-permute-start | bytes 2359304 | tf_op jit(solution)/shard_map/ppermute | solution.py:174
  75.4 66.8 %collective-permute-start.5 = (bf16[2,32,16,384]{3,2,1,0:T(8,128)(2,1)}, bf16[2,32,16,384]{3,2,1,0:T(8,128)(2,1)}, u32[]{:S(2)}, u32[]{:S(2)}) collective-permute-start(bf16[2,32,16,384]{3,2,1,0:T(8,128)(2,1)} %pad_maximum_fusion.7), channel_id=1, source_target_pairs={{0,8},{1,12},{2,0},{3,4},{4,9},{5,13},{6,1},{7,5},{8,10},{9,14},{1... | collective-permute-start | bytes 2359304 | tf_op jit(solution)/shard_map/ppermute | solution.py:174
  76.9 66.6 %collective-permute-start.6 = (bf16[2,32,16,384]{3,2,1,0:T(8,128)(2,1)}, bf16[2,32,16,384]{3,2,1,0:T(8,128)(2,1)}, u32[]{:S(2)}, u32[]{:S(2)}) collective-permute-start(bf16[2,32,16,384]{3,2,1,0:T(8,128)(2,1)} %pad_maximum_fusion.8), channel_id=1, source_target_pairs={{0,12},{1,0},{2,4},{3,8},{4,13},{5,1},{6,5},{7,9},{8,14},{9,2},{10... | collective-permute-start | bytes 2359304 | tf_op jit(solution)/shard_map/ppermute | solution.py:174
  80.3 26.2 %copy-start.9 = (bf16[2,32,4,384]{3,2,1,0:T(4,128)(2,1)}, bf16[2,32,4,384]{3,2,1,0:T(4,128)(2,1)S(1)}, u32[]{:S(2)}) copy-start(bf16[2,32,4,384]{3,2,1,0:T(4,128)(2,1)S(1)} %copy.12) | copy-start | bytes 589828
  80.4 26.1 %copy-start.11 = (bf16[2,32,4,384]{3,2,1,0:T(4,128)(2,1)}, bf16[2,32,4,384]{3,2,1,0:T(4,128)(2,1)S(1)}, u32[]{:S(2)}) copy-start(bf16[2,32,4,384]{3,2,1,0:T(4,128)(2,1)S(1)} %copy.13) | copy-start | bytes 589828
  80.8 64.1 %copy-start.2 = (bf16[1,384,1536]{2,1,0:T(8,128)(2,1)S(1)}, bf16[1,384,1536]{2,1,0:T(8,128)(2,1)}, u32[]{:S(2)}) copy-start(bf16[1,384,1536]{2,1,0:T(8,128)(2,1)} %copy-done.1) | copy-start | bytes 3538948
  153.3 6.7 %copy-start.3 = (bf16[1536,1536]{1,0:T(8,128)(2,1)}, bf16[1536,1536]{1,0:T(8,128)(2,1)S(1)}, u32[]{:S(2)}) copy-start(bf16[1536,1536]{1,0:T(8,128)(2,1)S(1)} %fusion.3) | copy-start | bytes 14155780
  (23 other events, 82.3 us)

commit v9 on v5

--- a/solution.py
+++ b/solution.py
@@ -1,3 +1,5 @@
+import functools
+
 import jax
 import jax.numpy as jnp
 from jax import lax
@@ -23,6 +25,10 @@
             axis=dim,
         )
     return cells
+
+
+def in_order(blocks, order):
+    return jnp.concatenate([blocks[m] for m in order], axis=0)
 
 
 def masked_taps(fringe_taps, tap_windows):
@@ -122,24 +128,17 @@
             codes = codes + [x ^ step for x in codes]
             step //= 2
         where = {code: m for m, code in enumerate(codes)}
-        rows = []
-        for k in range(nf):
-            pick = sum(
-                jnp.where((k ^ b) == code, m, 0) for code, m in where.items()
-            )
-            rows.append(lax.dynamic_index_in_dim(blocks, pick, 0, keepdims=False))
-        panel = jnp.concatenate(rows, axis=0)
+        branches = [
+            functools.partial(in_order, order=[where[k ^ own] for k in range(nf)])
+            for own in range(nf)
+        ]
+        panel = lax.switch(b, branches, blocks)
     else:
         panel = lax.all_gather(filter_panels[0], "freq", axis=0, tiled=True)
-    if q == 1:
-        shift = ((a + 1) % nf) * f_blk
-        panel = jnp.concatenate([panel, panel], axis=1)
-        panel = lax.dynamic_slice_in_dim(panel, shift, channels, axis=1)
-
     c_own = a
     u_src = (a % q) * nf + b
     fit = None
-    for r in range(nt):
+    for r in list(range(1, nt)) + [0]:
         c_send = (u_src + r) % nt
         start = class_starts[c_send]
         rows = lax.optimization_barrier(lax.dynamic_slice_in_dim(padded, start, SLOTS, axis=1))
@@ -157,7 +156,7 @@
         b_src = u_dst % nf
         if q == 1:
             gate = lax.dynamic_slice_in_dim(flag_mask, b_src * f_blk, f_blk, axis=1)
-            cols = lax.slice_in_dim(panel, (nf - 1 - r) * f_blk, (nf - r) * f_blk, axis=1)
+            cols = lax.dynamic_slice_in_dim(panel, b_src * f_blk, f_blk, axis=1)
         else:
             gate = lax.dynamic_slice(flag_mask, (t_sub * t_in, b_src * f_blk), (t_in, f_blk))
             cols = lax.dynamic_slice_in_dim(panel, b_src * f_blk, f_blk, axis=1)

time: 155 us -> 134 us (0.86)
  the two profiles are of different devices: /device:TPU:17 before, /device:TPU:14 now
where the time goes in v9:
time: 134 us; the launch traced here: 132 us
  waiting for transfers between devices  43.4 us (32%)
  other arithmetic  35.6 us (27%)
  matrix products  16.1 us (12%)
  starting transfers between devices  15.4 us (11%)
  local copies, waits for them, and re-layouts  13.2 us (10%)
  between operations  8.72 us (7%)
    ppermute x4, waiting for transfers between devices, shards(): got = lax.ppermute(chunk, ('tm', 'freq'), perm)  43.3 us
    another operation x9, other arithmetic  18.4 us
    dot_general x4, matrix products, shards(): jnp.einsum('rstj,ij->rsti', weighted, cols, preferred_element_type=jnp.fl...  16.1 us
    ppermute x4, starting transfers between devices, shards(): got = lax.ppermute(chunk, ('tm', 'freq'), perm)  8.96 us
    dynamic_update_slice x4, local copies, waits for them, and re-layouts, shards(): lax.dynamic_update_slice_in_dim(slotted, got, b_src * f_blk, axis=3)  5.29 us
    another operation x4, other arithmetic, convolve(): return jnp.stack([real_part, imag_part]).astype(jnp.bfloat16)  4 us
    ppermute x1, starting transfers between devices, extended(): lax.ppermute(tail, axis, [(i, (i + 1) % count) for i in range(ends)])  3.48 us
    concatenate x1, other arithmetic, extended(): jnp.concatenate([lax.ppermute(tail, axis, [(i, (i + 1) % count) for i in...  2.88 us
  transfers between devices with their start and end apart: 8, of which 3 were waited for; matrix products, arithmetic and copies ran while one was open for 32% of the time, Pallas kernels for 0%

profile of v9, /device:TPU:14, one launch (start us, length us, event | category | flops | bytes accessed | tf_op | source)
XLA Modules:
  0.0 132.4 jit_solution(12836792430599596475)
XLA Ops:
  0.0 1.7 %fusion.176 = (bf16[2,66,4,384]{3,2,1,0:T(4,128)(2,1)S(1)}, bf16[2,66,4,384]{3,2,1,0:T(4,128)(2,1)S(1)}) fusion(bf16[2,66,16,384]{3,2,1,0:T(8,128)(2,1)} %param.11), kind=kLoop, calls=%fused_computation.437 | loop fusion | bytes 1622016 | tf_op jit(solution)/shard_map/slice | solution.py:18
  1.7 3.5 %collective-permute-start = (bf16[2,66,4,384]{3,2,1,0:T(4,128)(2,1)S(1)}, bf16[2,66,4,384]{3,2,1,0:T(4,128)(2,1)S(1)}, u32[]{:S(2)}, u32[]{:S(2)}) collective-permute-start(bf16[2,66,4,384]{3,2,1,0:T(4,128)(2,1)S(1)} %get-tuple-element.58), channel_id=1, source_target_pairs={{0,4},{4,8},{8,12},{1,5},{5,9},{9,13},{2,6},{6,10},{10,14},{3,7},{... | collective-permute-start | bytes 1216520 | tf_op jit(solution)/shard_map/ppermute | solution.py:21
  5.2 2.4 %collective-permute-start.1 = (bf16[2,66,4,384]{3,2,1,0:T(4,128)(2,1)S(1)}, bf16[2,66,4,384]{3,2,1,0:T(4,128)(2,1)S(1)}, u32[]{:S(2)}, u32[]{:S(2)}) collective-permute-start(bf16[2,66,4,384]{3,2,1,0:T(4,128)(2,1)S(1)} %get-tuple-element.59), channel_id=1, source_target_pairs={{4,0},{8,4},{12,8},{5,1},{9,5},{13,9},{6,2},{10,6},{14,10},{7,3},{... | collective-permute-start | bytes 1216520 | tf_op jit(solution)/shard_map/ppermute | solution.py:23
  7.6 0.6 collective-permute-start.6
  8.2 0.8 reduce-window.9
  9.0 0.7 bitcast_subtract_fusion
  9.7 1.5 %fusion.177 = (s32[1]{0:T(128)}, s32[1]{0:T(128)}, s32[1]{0:T(128)}, s32[1]{0:T(128)}, s32[1]{0:T(128)}, /*index=5*/s32[1]{0:T(128)}, s32[1]{0:T(128)}, s32[1]{0:T(128)}) fusion(s32[4]{0:T(128)S(1)} %bitcast_subtract_fusion, s32[]{:T(128)S(6)} %select_n.125, s32[]{:T(128)S(6)} %select_n.119, s32[]{:T(128)S(6)} %select_n.113, s32[]{:T(128)S(6)} %select_n.107, ...), kind=kLoop, calls=%fused_computation.438 | loop fusion | bytes 80 | tf_op jit(solution)/shard_map/dynamic_slice | solution.py:143
  16.3 0.7 compare_convert_fusion.4
  17.1 0.7 broadcast_multiply_fusion.4
  17.8 0.6 compare_convert_fusion.1
  18.4 0.6 compare_convert_fusion.3
  19.1 0.6 compare_convert_fusion.2
  19.6 0.7 compare_convert_fusion
  20.7 0.6 slice_bitcast_fusion.61
  24.1 2.9 %fusion.4 = bf16[2,98,24,384]{3,2,1,0:T(8,128)(2,1)S(1)} fusion(bf16[2,66,4,384]{3,2,1,0:T(4,128)(2,1)S(1)} %collective-permute-done.1, bf16[2,66,16,384]{3,2,1,0:T(8,128)(2,1)} %param.11, bf16[2,66,4,384]{3,2,1,0:T(4,128)(2,1)S(1)} %collective-permute-done), kind=kLoop, calls=%fused_computation.18 | loop fusion | flops 18063360 | bytes 6045696 | tf_op jit(solution)/shard_map/concatenate | solution.py:19
  27.0 0.7 constant_dynamic-slice_fusion
  27.7 2.1 %fusion.163 = bf16[1,32,16,384]{3,2,1,0:T(8,128)(2,1)S(1)} fusion(f32[32]{0:T(128)S(1)} %get-tuple-element.119, f32[32]{0:T(128)S(1)} %get-tuple-element.120, f32[32]{0:T(128)S(1)} %get-tuple-element.121, f32[32]{0:T(128)S(1)} %get-tuple-element.122, f32[32]{0:T(128)S(1)} %get-tuple-element.123, f32[32]{0:T(128)S(1)} %get-tuple-element.124, ...), kind=kLoop, calls=%fused_computation.324 | loop fusion | flops 10616832 | bytes 7473408 | tf_op jit(solution)/shard_map/convert.2
  29.8 2.1 %fusion.162 = bf16[1,32,16,384]{3,2,1,0:T(8,128)(2,1)S(1)} fusion(f32[32]{0:T(128)S(1)} %get-tuple-element.119, f32[32]{0:T(128)S(1)} %get-tuple-element.120, f32[32]{0:T(128)S(1)} %get-tuple-element.121, f32[32]{0:T(128)S(1)} %get-tuple-element.122, f32[32]{0:T(128)S(1)} %get-tuple-element.123, f32[32]{0:T(128)S(1)} %get-tuple-element.124, ...), kind=kLoop, calls=%fused_computation.323 | loop fusion | flops 10616832 | bytes 7473408 | tf_op jit(solution)/shard_map/convert.3
  31.9 2.1 %fusion.167 = bf16[1,32,16,384]{3,2,1,0:T(8,128)(2,1)S(1)} fusion(f32[32]{0:T(128)S(1)} %get-tuple-element.101, f32[32]{0:T(128)S(1)} %get-tuple-element.102, f32[32]{0:T(128)S(1)} %get-tuple-element.103, f32[32]{0:T(128)S(1)} %get-tuple-element.104, f32[32]{0:T(128)S(1)} %get-tuple-element.105, f32[32]{0:T(128)S(1)} %get-tuple-element.106, ...), kind=kLoop, calls=%fused_computation.328 | loop fusion | flops 10616832 | bytes 7473408 | tf_op jit(solution)/shard_map/convert.6
  34.0 2.1 %fusion.166 = bf16[1,32,16,384]{3,2,1,0:T(8,128)(2,1)S(1)} fusion(f32[32]{0:T(128)S(1)} %get-tuple-element.101, f32[32]{0:T(128)S(1)} %get-tuple-element.102, f32[32]{0:T(128)S(1)} %get-tuple-element.103, f32[32]{0:T(128)S(1)} %get-tuple-element.104, f32[32]{0:T(128)S(1)} %get-tuple-element.105, f32[32]{0:T(128)S(1)} %get-tuple-element.106, ...), kind=kLoop, calls=%fused_computation.327 | loop fusion | flops 10616832 | bytes 7473408 | tf_op jit(solution)/shard_map/convert.7
  36.1 1.0 pad_maximum_fusion.5
  37.1 2.1 %collective-permute-start.2 = (bf16[2,32,16,384]{3,2,1,0:T(8,128)(2,1)}, bf16[2,32,16,384]{3,2,1,0:T(8,128)(2,1)}, u32[]{:S(2)}, u32[]{:S(2)}) collective-permute-start(bf16[2,32,16,384]{3,2,1,0:T(8,128)(2,1)} %pad_maximum_fusion.5), channel_id=1, source_target_pairs={{0,4},{1,8},{2,12},{3,0},{4,5},{5,9},{6,13},{7,1},{8,6},{9,10},{10... | collective-permute-start | bytes 2359304 | tf_op jit(solution)/shard_map/ppermute | solution.py:153
  39.4 2.1 %fusion.161 = bf16[1,32,16,384]{3,2,1,0:T(8,128)(2,1)S(1)} fusion(f32[32]{0:T(128)S(1)} %get-tuple-element.65, f32[32]{0:T(128)S(1)} %get-tuple-element.66, f32[32]{0:T(128)S(1)} %get-tuple-element.67, f32[32]{0:T(128)S(1)} %get-tuple-element.68, f32[32]{0:T(128)S(1)} %get-tuple-element.69, f32[32]{0:T(128)S(1)} %get-tuple-element.70, ...), kind=kLoop, calls=%fused_computation.322 | loop fusion | flops 10616832 | bytes 7473408 | tf_op jit(solution)/shard_map/convert
  41.5 2.9 %fusion.160 = bf16[1,32,16,384]{3,2,1,0:T(8,128)(2,1)S(1)} fusion(f32[32]{0:T(128)} %copy-done.22, f32[32]{0:T(128)} %copy-done.23, f32[32]{0:T(128)} %copy-done.24, f32[32]{0:T(128)} %copy-done.25, f32[32]{0:T(128)} %copy-done.26, f32[32]{0:T(128)} %copy-done.27, f32[32]{0:T(128)} %copy-done.28, f32[32]{0:T(128)} %copy-done.29, f32[32]{0:T(128)} %copy-done.30, ...), kind=kLoop, calls=%fused_computation.321 | loop fusion | flops 10616832 | bytes 7473408 | tf_op jit(solution)/shard_map/convert.1
  44.6 1.0 copy-done.1
  45.6 1.6 %pad_maximum_fusion.4 = bf16[2,384,1536]{2,1,0:T(8,128)(2,1)} fusion(bf16[1,384,1536]{2,1,0:T(8,128)(2,1)S(1)} %collective-permute-done.6, bf16[1,384,1536]{2,1,0:T(8,128)(2,1)S(1)} %copy-done), kind=kLoop, calls=%fused_computation.20 | loop fusion | flops 1179648 | bytes 4718592 | tf_op jit(solution)/shard_map/concatenate | solution.py:123
  47.3 2.1 %fusion.165 = bf16[1,32,16,384]{3,2,1,0:T(8,128)(2,1)S(1)} fusion(f32[32]{0:T(128)S(1)} %get-tuple-element.83, f32[32]{0:T(128)S(1)} %get-tuple-element.84, f32[32]{0:T(128)S(1)} %get-tuple-element.85, f32[32]{0:T(128)S(1)} %copy-done.7, f32[32]{0:T(128)S(1)} %copy-done.8, f32[32]{0:T(128)S(1)} %copy-done.9, f32[32]{0:T(128)S(1)} %copy-done.10, ...), kind=kLoop, calls=%fused_computation.326 | loop fusion | flops 10616832 | bytes 7473408 | tf_op jit(solution)/shard_map/convert.4
  49.4 2.1 %fusion.164 = bf16[1,32,16,384]{3,2,1,0:T(8,128)(2,1)S(1)} fusion(f32[32]{0:T(128)S(1)} %get-tuple-element.83, f32[32]{0:T(128)S(1)} %get-tuple-element.84, f32[32]{0:T(128)S(1)} %get-tuple-element.85, f32[32]{0:T(128)S(1)} %copy-done.7, f32[32]{0:T(128)S(1)} %copy-done.8, f32[32]{0:T(128)S(1)} %copy-done.9, f32[32]{0:T(128)S(1)} %copy-done.10, ...), kind=kLoop, calls=%fused_computation.325 | loop fusion | flops 10616832 | bytes 7473408 | tf_op jit(solution)/shard_map/convert.5
  51.5 1.1 pad_maximum_fusion.6
  52.6 1.5 %collective-permute-start.3 = (bf16[2,32,16,384]{3,2,1,0:T(8,128)(2,1)}, bf16[2,32,16,384]{3,2,1,0:T(8,128)(2,1)}, u32[]{:S(2)}, u32[]{:S(2)}) collective-permute-start(bf16[2,32,16,384]{3,2,1,0:T(8,128)(2,1)} %pad_maximum_fusion.6), channel_id=1, source_target_pairs={{0,8},{1,12},{2,0},{3,4},{4,9},{5,13},{6,1},{7,5},{8,10},{9,14},{1... | collective-permute-start | bytes 2359304 | tf_op jit(solution)/shard_map/ppermute | solution.py:153
  54.2 1.0 pad_maximum_fusion.7
  55.4 1.0 pad_maximum_fusion.8
  56.4 5.0 %collective-permute-start.5 = (bf16[2,32,16,384]{3,2,1,0:T(8,128)(2,1)}, bf16[2,32,16,384]{3,2,1,0:T(8,128)(2,1)}, u32[]{:S(2)}, u32[]{:S(2)}) collective-permute-start(bf16[2,32,16,384]{3,2,1,0:T(8,128)(2,1)} %pad_maximum_fusion.8), channel_id=1, source_target_pairs={{0,0},{1,4},{2,8},{3,12},{4,1},{5,5},{6,9},{7,13},{8,2},{9,6},{10,... | collective-permute-start | bytes 2359304 | tf_op jit(solution)/shard_map/ppermute | solution.py:153
  61.6 1.4 %dynamic-slice_convert_fusion = (bf16[16,384]{1,0:T(8,128)(2,1)S(1)}, bf16[16,384]{1,0:T(8,128)(2,1)}, bf16[16,384]{1,0:T(8,128)(2,1)}, bf16[16,384]{1,0:T(8,128)(2,1)}) fusion(s32[16,1536]{1,0:T(8,128)} %param.15, s32[]{:T(128)S(6)} %select_n.129, s32[]{:T(128)S(6)} %select_n.117, s32[]{:T(128)S(6)} %select_n.111, s32[]{:T(128)S(6)} %select_n.123), kind=kLoop, calls=%fused_computation.333 | loop fusion | flops 24576 | bytes 147472 | tf_op jit(solution)/shard_map/convert_element_type | solution.py:163
  63.4 1.4 %constant_dynamic-update-slice_fusion.3 = bf16[2,32,16,1536]{3,2,1,0:T(8,128)(2,1)S(1)} fusion(bf16[2,32,16,1536]{3,2,1,0:T(8,128)(2,1)S(1)} %broadcast_in_dim.4, bf16[2,32,16,384]{3,2,1,0:T(8,128)(2,1)} %collective-permute-done.2, s32[]{:T(128)S(6)} %select_n.111), kind=kLoop, calls=%fused_computation.354 | loop fusion | bytes 1572868 | tf_op jit(solution)/shard_map/dynamic_update_slice | solution.py:169
  64.8 32.6 %collective-permute-done.3 = bf16[2,32,16,384]{3,2,1,0:T(8,128)(2,1)} collective-permute-done((bf16[2,32,16,384]{3,2,1,0:T(8,128)(2,1)}, bf16[2,32,16,384]{3,2,1,0:T(8,128)(2,1)}, u32[]{:S(2)}, u32[]{:S(2)}) %collective-permute-start.3) | collective-permute-done | bytes 786464 | tf_op jit(solution)/shard_map/ppermute | solution.py:153
  97.4 1.3 constant_dynamic-update-slice_fusion.2
  98.7 8.0 %collective-permute-done.4 = bf16[2,32,16,384]{3,2,1,0:T(8,128)(2,1)} collective-permute-done((bf16[2,32,16,384]{3,2,1,0:T(8,128)(2,1)}, bf16[2,32,16,384]{3,2,1,0:T(8,128)(2,1)}, u32[]{:S(2)}, u32[]{:S(2)}) %collective-permute-start.4) | collective-permute-done | bytes 786464 | tf_op jit(solution)/shard_map/ppermute | solution.py:153
  106.7 1.3 constant_dynamic-update-slice_fusion.1
  108.0 2.8 %collective-permute-done.5 = bf16[2,32,16,384]{3,2,1,0:T(8,128)(2,1)} collective-permute-done((bf16[2,32,16,384]{3,2,1,0:T(8,128)(2,1)}, bf16[2,32,16,384]{3,2,1,0:T(8,128)(2,1)}, u32[]{:S(2)}, u32[]{:S(2)}) %collective-permute-start.5) | collective-permute-done | bytes 786464 | tf_op jit(solution)/shard_map/ppermute | solution.py:153
  110.7 1.3 constant_dynamic-update-slice_fusion
  112.1 1.6 %copy-done.4 = bf16[2,32,16,1536]{3,2,1,0:T(8,128)(2,1)} copy-done((bf16[2,32,16,1536]{3,2,1,0:T(8,128)(2,1)}, bf16[2,32,16,1536]{3,2,1,0:T(8,128)(2,1)S(1)}, u32[]{:S(2)}) %copy-start.4) | copy-done | bytes 3145752
  113.7 2.5 %conditional.1 = (bf16[1536,1536]{1,0:T(8,128)(2,1)}) conditional(s32[]{:T(128)} %clamp.3, (bf16[1,384,1536]{2,1,0:T(8,128)(2,1)S(1)}, bf16[2,384,1536]{2,1,0:T(8,128)(2,1)S(1)}, bf16[1,384,1536]{2,1,0:T(8,128)(2,1)S(1)}) %tuple.121, (bf16[2,384,1536]{2,1,0:T(8,128)(2,1)S(1)}, bf16[1,384,1536]{2,1,0:T(8,128)(2,1)S(1)}, ...), branch_computations={%region_1.2_spmd, %region_2.3_spmd, %region_3.4_spmd, %region_4.5_... | conditional | flops 18874368 | bytes 14155784 | solution.py:135
  113.9 2.4 %pad_maximum_fusion.2 = bf16[1536,1536]{1,0:T(8,128)(2,1)} fusion(bf16[384,1536]{1,0:T(8,128)(2,1)S(1)} %get-tuple-element.51, bf16[384,1536]{1,0:T(8,128)(2,1)S(1)} %bitcast.214, bf16[384,1536]{1,0:T(8,128)(2,1)S(1)} %get-tuple-element.50, bf16[384,1536]{1,0:T(8,128)(2,1)S(1)} %bitcast.218), kind=kLoop, calls=%fused_computation.6 | loop fusion | flops 18874368 | bytes 9437184 | tf_op jit(solution)/shard_map/cond/branch_2_fun/concatenate | solution.py:31
  116.2 3.5 %fusion.10 = f32[2,32,16,1536]{3,2,1,0:T(8,128)S(1)} fusion(bf16[1536,1536]{1,0:T(8,128)(2,1)} %get-tuple-element.152, s32[]{:T(128)S(6)} %select_n.123, bf16[2,32,16,384]{3,2,1,0:T(8,128)(2,1)} %collective-permute-done.4, bf16[16,384]{1,0:T(8,128)(2,1)} %get-tuple-element.63), kind=kOutput, calls=%fused_computation.23 | convolution fusion | flops 1208352768 | bytes 8269828 | tf_op jit(solution)/shard_map/rstj,ij->rsti/dot_general | solution.py:164
  119.8 3.0 %fusion.12 = f32[2,32,16,1536]{3,2,1,0:T(8,128)S(1)} fusion(bf16[1536,1536]{1,0:T(8,128)(2,1)S(1)} %copy-done.3, s32[]{:T(128)S(6)} %select_n.117, bf16[2,32,16,384]{3,2,1,0:T(8,128)(2,1)} %collective-permute-done.3, bf16[16,384]{1,0:T(8,128)(2,1)S(1)} %copy-done.6), kind=kOutput, calls=%fused_computation.25 | convolution fusion | flops 1208352768 | bytes 8269828 | tf_op jit(solution)/shard_map/rstj,ij->rsti/dot_general | solution.py:164
  122.7 3.0 %fusion.14 = f32[2,32,16,1536]{3,2,1,0:T(8,128)S(1)} fusion(bf16[1536,1536]{1,0:T(8,128)(2,1)S(1)} %copy-done.3, s32[]{:T(128)S(6)} %select_n.111, bf16[2,32,16,384]{3,2,1,0:T(8,128)(2,1)} %collective-permute-done.2, bf16[16,384]{1,0:T(8,128)(2,1)S(1)} %copy-done.5), kind=kOutput, calls=%fused_computation.27 | convolution fusion | flops 1208352768 | bytes 8269828 | tf_op jit(solution)/shard_map/rstj,ij->rsti/dot_general | solution.py:164
  125.7 6.7 %fusion.5 = bf16[2,1,32,16,1536]{4,3,2,1,0:T(8,128)(2,1)} fusion(f32[2,32,16,1536]{3,2,1,0:T(8,128)S(1)} %fusion.10, f32[2,32,16,1536]{3,2,1,0:T(8,128)S(1)} %fusion.14, f32[2,32,16,1536]{3,2,1,0:T(8,128)S(1)} %fusion.12, bf16[2,32,16,1536]{3,2,1,0:T(8,128)(2,1)} %copy-done.4, bf16[1536,1536]{1,0:T(8,128)(2,1)} %get-tuple-element.152, s32[]{:T(128)S(6)} %select_n.129, ...), kind=kOutput, calls=%fused_computation.19 | convolution fusion | flops 1217789952 | bytes 27144196 | tf_op jit(solution)/shard_map/rstj,ij->rsti/dot_general | solution.py:164
  (95 shorter events, 1.3 us)
Async XLA Ops:
  1.7 22.4 %collective-permute-start = (bf16[2,66,4,384]{3,2,1,0:T(4,128)(2,1)S(1)}, bf16[2,66,4,384]{3,2,1,0:T(4,128)(2,1)S(1)}, u32[]{:S(2)}, u32[]{:S(2)}) collective-permute-start(bf16[2,66,4,384]{3,2,1,0:T(4,128)(2,1)S(1)} %get-tuple-element.58), channel_id=1, source_target_pairs={{0,4},{4,8},{8,12},{1,5},{5,9},{9,13},{2,6},{6,10},{10,14},{3,7},{... | collective-permute-start | bytes 1216520 | tf_op jit(solution)/shard_map/ppermute | solution.py:21
  5.2 18.9 %collective-permute-start.1 = (bf16[2,66,4,384]{3,2,1,0:T(4,128)(2,1)S(1)}, bf16[2,66,4,384]{3,2,1,0:T(4,128)(2,1)S(1)}, u32[]{:S(2)}, u32[]{:S(2)}) collective-permute-start(bf16[2,66,4,384]{3,2,1,0:T(4,128)(2,1)S(1)} %get-tuple-element.59), channel_id=1, source_target_pairs={{4,0},{8,4},{12,8},{5,1},{9,5},{13,9},{6,2},{10,6},{14,10},{7,3},{... | collective-permute-start | bytes 1216520 | tf_op jit(solution)/shard_map/ppermute | solution.py:23
  7.6 37.0 %collective-permute-start.6 = (bf16[1,384,1536]{2,1,0:T(8,128)(2,1)}, bf16[1,384,1536]{2,1,0:T(8,128)(2,1)S(1)}, u32[]{:S(2)}, u32[]{:S(2)}) collective-permute-start(bf16[1,384,1536]{2,1,0:T(8,128)(2,1)} %param.16), channel_id=1, source_target_pairs={{0,2},{1,3},{2,0},{3,1},{4,6},{5,7},{6,4},{7,5},{8,10},{9,11},{10,... | collective-permute-start | bytes 3538952 | tf_op jit(solution)/shard_map/ppermute | solution.py:123
  20.4 18.8 %copy-start.21 = (f32[32]{0:T(128)}, f32[32]{0:T(128)S(1)}, u32[]{:S(2)}) copy-start(f32[32]{0:T(128)S(1)} %get-tuple-element.64) | copy-start | bytes 388
  20.4 18.8 %copy-start.22 = (f32[32]{0:T(128)}, f32[32]{0:T(128)S(1)}, u32[]{:S(2)}) copy-start(f32[32]{0:T(128)S(1)} %get-tuple-element.65) | copy-start | bytes 388
  20.4 18.8 %copy-start.23 = (f32[32]{0:T(128)}, f32[32]{0:T(128)S(1)}, u32[]{:S(2)}) copy-start(f32[32]{0:T(128)S(1)} %get-tuple-element.66) | copy-start | bytes 388
  20.4 18.8 %copy-start.24 = (f32[32]{0:T(128)}, f32[32]{0:T(128)S(1)}, u32[]{:S(2)}) copy-start(f32[32]{0:T(128)S(1)} %get-tuple-element.67) | copy-start | bytes 388
  20.5 18.8 %copy-start.25 = (f32[32]{0:T(128)}, f32[32]{0:T(128)S(1)}, u32[]{:S(2)}) copy-start(f32[32]{0:T(128)S(1)} %get-tuple-element.68) | copy-start | bytes 388
  20.5 18.8 %copy-start.26 = (f32[32]{0:T(128)}, f32[32]{0:T(128)S(1)}, u32[]{:S(2)}) copy-start(f32[32]{0:T(128)S(1)} %get-tuple-element.69) | copy-start | bytes 388
  20.5 18.8 %copy-start.27 = (f32[32]{0:T(128)}, f32[32]{0:T(128)S(1)}, u32[]{:S(2)}) copy-start(f32[32]{0:T(128)S(1)} %get-tuple-element.70) | copy-start | bytes 388
  20.5 18.8 %copy-start.28 = (f32[32]{0:T(128)}, f32[32]{0:T(128)S(1)}, u32[]{:S(2)}) copy-start(f32[32]{0:T(128)S(1)} %get-tuple-element.71) | copy-start | bytes 388
  20.5 18.8 %copy-start.29 = (f32[32]{0:T(128)}, f32[32]{0:T(128)S(1)}, u32[]{:S(2)}) copy-start(f32[32]{0:T(128)S(1)} %get-tuple-element.72) | copy-start | bytes 388
  20.5 18.8 %copy-start.30 = (f32[32]{0:T(128)}, f32[32]{0:T(128)S(1)}, u32[]{:S(2)}) copy-start(f32[32]{0:T(128)S(1)} %get-tuple-element.73) | copy-start | bytes 388
  20.5 18.8 %copy-start.31 = (f32[32]{0:T(128)}, f32[32]{0:T(128)S(1)}, u32[]{:S(2)}) copy-start(f32[32]{0:T(128)S(1)} %get-tuple-element.74) | copy-start | bytes 388
  20.5 18.8 %copy-start.32 = (f32[32]{0:T(128)}, f32[32]{0:T(128)S(1)}, u32[]{:S(2)}) copy-start(f32[32]{0:T(128)S(1)} %get-tuple-element.75) | copy-start | bytes 388
  20.5 18.8 %copy-start.33 = (f32[32]{0:T(128)}, f32[32]{0:T(128)S(1)}, u32[]{:S(2)}) copy-start(f32[32]{0:T(128)S(1)} %get-tuple-element.76) | copy-start | bytes 388
  20.5 18.8 %copy-start.34 = (f32[32]{0:T(128)}, f32[32]{0:T(128)S(1)}, u32[]{:S(2)}) copy-start(f32[32]{0:T(128)S(1)} %get-tuple-element.77) | copy-start | bytes 388
  20.6 18.8 %copy-start.35 = (f32[32]{0:T(128)}, f32[32]{0:T(128)S(1)}, u32[]{:S(2)}) copy-start(f32[32]{0:T(128)S(1)} %get-tuple-element.78) | copy-start | bytes 388
  20.6 18.8 %copy-start.36 = (f32[32]{0:T(128)}, f32[32]{0:T(128)S(1)}, u32[]{:S(2)}) copy-start(f32[32]{0:T(128)S(1)} %get-tuple-element.79) | copy-start | bytes 388
  20.6 18.8 %copy-start.37 = (f32[32]{0:T(128)}, f32[32]{0:T(128)S(1)}, u32[]{:S(2)}) copy-start(f32[32]{0:T(128)S(1)} %get-tuple-element.80) | copy-start | bytes 388
  20.6 18.8 %copy-start.38 = (f32[32]{0:T(128)}, f32[32]{0:T(128)S(1)}, u32[]{:S(2)}) copy-start(f32[32]{0:T(128)S(1)} %get-tuple-element.81) | copy-start | bytes 388
  37.1 25.9 %collective-permute-start.2 = (bf16[2,32,16,384]{3,2,1,0:T(8,128)(2,1)}, bf16[2,32,16,384]{3,2,1,0:T(8,128)(2,1)}, u32[]{:S(2)}, u32[]{:S(2)}) collective-permute-start(bf16[2,32,16,384]{3,2,1,0:T(8,128)(2,1)} %pad_maximum_fusion.5), channel_id=1, source_target_pairs={{0,4},{1,8},{2,12},{3,0},{4,5},{5,9},{6,13},{7,1},{8,6},{9,10},{10... | collective-permute-start | bytes 2359304 | tf_op jit(solution)/shard_map/ppermute | solution.py:153
  41.5 4.1 %copy-start = (bf16[1,384,1536]{2,1,0:T(8,128)(2,1)S(1)}, bf16[1,384,1536]{2,1,0:T(8,128)(2,1)}, u32[]{:S(2)}) copy-start(bf16[1,384,1536]{2,1,0:T(8,128)(2,1)} %param.16) | copy-start | bytes 3538948
  44.4 2.8 %copy-start.7 = (f32[32]{0:T(128)S(1)}, f32[32]{0:T(128)}, u32[]{:S(2)}) copy-start(f32[32]{0:T(128)} %get-tuple-element.86) | copy-start | bytes 388
  44.4 2.8 %copy-start.8 = (f32[32]{0:T(128)S(1)}, f32[32]{0:T(128)}, u32[]{:S(2)}) copy-start(f32[32]{0:T(128)} %get-tuple-element.87) | copy-start | bytes 388
  44.4 2.8 %copy-start.9 = (f32[32]{0:T(128)S(1)}, f32[32]{0:T(128)}, u32[]{:S(2)}) copy-start(f32[32]{0:T(128)} %get-tuple-element.88) | copy-start | bytes 388
  44.5 2.8 %copy-start.10 = (f32[32]{0:T(128)S(1)}, f32[32]{0:T(128)}, u32[]{:S(2)}) copy-start(f32[32]{0:T(128)} %get-tuple-element.89) | copy-start | bytes 388
  44.5 2.8 %copy-start.11 = (f32[32]{0:T(128)S(1)}, f32[32]{0:T(128)}, u32[]{:S(2)}) copy-start(f32[32]{0:T(128)} %get-tuple-element.90) | copy-start | bytes 388
  44.5 2.8 %copy-start.12 = (f32[32]{0:T(128)S(1)}, f32[32]{0:T(128)}, u32[]{:S(2)}) copy-start(f32[32]{0:T(128)} %get-tuple-element.91) | copy-start | bytes 388
  44.5 2.8 %copy-start.13 = (f32[32]{0:T(128)S(1)}, f32[32]{0:T(128)}, u32[]{:S(2)}) copy-start(f32[32]{0:T(128)} %get-tuple-element.92) | copy-start | bytes 388
  44.5 2.8 %copy-start.14 = (f32[32]{0:T(128)S(1)}, f32[32]{0:T(128)}, u32[]{:S(2)}) copy-start(f32[32]{0:T(128)} %get-tuple-element.93) | copy-start | bytes 388
  44.5 2.8 %copy-start.15 = (f32[32]{0:T(128)S(1)}, f32[32]{0:T(128)}, u32[]{:S(2)}) copy-start(f32[32]{0:T(128)} %get-tuple-element.94) | copy-start | bytes 388
  44.5 2.8 %copy-start.16 = (f32[32]{0:T(128)S(1)}, f32[32]{0:T(128)}, u32[]{:S(2)}) copy-start(f32[32]{0:T(128)} %get-tuple-element.95) | copy-start | bytes 388
  44.5 2.8 %copy-start.17 = (f32[32]{0:T(128)S(1)}, f32[32]{0:T(128)}, u32[]{:S(2)}) copy-start(f32[32]{0:T(128)} %get-tuple-element.96) | copy-start | bytes 388
  44.5 2.8 %copy-start.18 = (f32[32]{0:T(128)S(1)}, f32[32]{0:T(128)}, u32[]{:S(2)}) copy-start(f32[32]{0:T(128)} %get-tuple-element.97) | copy-start | bytes 388
  44.5 2.8 %copy-start.19 = (f32[32]{0:T(128)S(1)}, f32[32]{0:T(128)}, u32[]{:S(2)}) copy-start(f32[32]{0:T(128)} %get-tuple-element.98) | copy-start | bytes 388
  44.6 2.8 %copy-start.20 = (f32[32]{0:T(128)S(1)}, f32[32]{0:T(128)}, u32[]{:S(2)}) copy-start(f32[32]{0:T(128)} %get-tuple-element.99) | copy-start | bytes 388
  44.6 1.0 copy-start.1
  47.2 64.8 %collective-permute-start.7 = (bf16[2,384,1536]{2,1,0:T(8,128)(2,1)}, bf16[2,384,1536]{2,1,0:T(8,128)(2,1)S(1)}, u32[]{:S(2)}, u32[]{:S(2)}) collective-permute-start(bf16[2,384,1536]{2,1,0:T(8,128)(2,1)} %pad_maximum_fusion.4), channel_id=1, source_target_pairs={{0,1},{1,0},{2,3},{3,2},{4,5},{5,4},{6,7},{7,6},{8,9},{9,8},{10,11... | collective-permute-start | bytes 7077896 | tf_op jit(solution)/shard_map/ppermute | solution.py:123
  52.6 44.8 %collective-permute-start.3 = (bf16[2,32,16,384]{3,2,1,0:T(8,128)(2,1)}, bf16[2,32,16,384]{3,2,1,0:T(8,128)(2,1)}, u32[]{:S(2)}, u32[]{:S(2)}) collective-permute-start(bf16[2,32,16,384]{3,2,1,0:T(8,128)(2,1)} %pad_maximum_fusion.6), channel_id=1, source_target_pairs={{0,8},{1,12},{2,0},{3,4},{4,9},{5,13},{6,1},{7,5},{8,10},{9,14},{1... | collective-permute-start | bytes 2359304 | tf_op jit(solution)/shard_map/ppermute | solution.py:153
  55.1 51.6 %collective-permute-start.4 = (bf16[2,32,16,384]{3,2,1,0:T(8,128)(2,1)}, bf16[2,32,16,384]{3,2,1,0:T(8,128)(2,1)}, u32[]{:S(2)}, u32[]{:S(2)}) collective-permute-start(bf16[2,32,16,384]{3,2,1,0:T(8,128)(2,1)} %pad_maximum_fusion.7), channel_id=1, source_target_pairs={{0,12},{1,0},{2,4},{3,8},{4,13},{5,1},{6,5},{7,9},{8,14},{9,2},{10... | collective-permute-start | bytes 2359304 | tf_op jit(solution)/shard_map/ppermute | solution.py:153
  56.4 54.4 %collective-permute-start.5 = (bf16[2,32,16,384]{3,2,1,0:T(8,128)(2,1)}, bf16[2,32,16,384]{3,2,1,0:T(8,128)(2,1)}, u32[]{:S(2)}, u32[]{:S(2)}) collective-permute-start(bf16[2,32,16,384]{3,2,1,0:T(8,128)(2,1)} %pad_maximum_fusion.8), channel_id=1, source_target_pairs={{0,0},{1,4},{2,8},{3,12},{4,1},{5,5},{6,9},{7,13},{8,2},{9,6},{10,... | collective-permute-start | bytes 2359304 | tf_op jit(solution)/shard_map/ppermute | solution.py:153
  63.4 48.7 %copy-start.2 = (bf16[1,384,1536]{2,1,0:T(8,128)(2,1)S(1)}, bf16[1,384,1536]{2,1,0:T(8,128)(2,1)}, u32[]{:S(2)}) copy-start(bf16[1,384,1536]{2,1,0:T(8,128)(2,1)} %copy-done.1) | copy-start | bytes 3538948
  112.0 1.7 %copy-start.4 = (bf16[2,32,16,1536]{3,2,1,0:T(8,128)(2,1)}, bf16[2,32,16,1536]{3,2,1,0:T(8,128)(2,1)S(1)}, u32[]{:S(2)}) copy-start(bf16[2,32,16,1536]{3,2,1,0:T(8,128)(2,1)S(1)} %constant_dynamic-update-slice_fusion) | copy-start | bytes 9437188
  116.2 3.5 %copy-start.3 = (bf16[1536,1536]{1,0:T(8,128)(2,1)S(1)}, bf16[1536,1536]{1,0:T(8,128)(2,1)}, u32[]{:S(2)}) copy-start(bf16[1536,1536]{1,0:T(8,128)(2,1)} %get-tuple-element.152) | copy-start | bytes 14155780
  116.2 3.5 %copy-start.6 = (bf16[16,384]{1,0:T(8,128)(2,1)S(1)}, bf16[16,384]{1,0:T(8,128)(2,1)}, u32[]{:S(2)}) copy-start(bf16[16,384]{1,0:T(8,128)(2,1)} %get-tuple-element.61) | copy-start | bytes 36868
  119.8 3.0 %copy-start.5 = (bf16[16,384]{1,0:T(8,128)(2,1)S(1)}, bf16[16,384]{1,0:T(8,128)(2,1)}, u32[]{:S(2)}) copy-start(bf16[16,384]{1,0:T(8,128)(2,1)} %get-tuple-element.62) | copy-start | bytes 36868

commit v10 on v9

--- a/solution.py
+++ b/solution.py
@@ -135,13 +135,18 @@
         panel = lax.switch(b, branches, blocks)
     else:
         panel = lax.all_gather(filter_panels[0], "freq", axis=0, tiled=True)
+    if q == 1:
+        shift = ((a + 1) % nf) * f_blk
+        panel = jnp.concatenate([panel, panel], axis=1)
+        panel = lax.dynamic_slice_in_dim(panel, shift, channels, axis=1)
+
     c_own = a
     u_src = (a % q) * nf + b
     fit = None
     for r in list(range(1, nt)) + [0]:
         c_send = (u_src + r) % nt
         start = class_starts[c_send]
-        rows = lax.optimization_barrier(lax.dynamic_slice_in_dim(padded, start, SLOTS, axis=1))
+        rows = lax.dynamic_slice_in_dim(padded, start, SLOTS, axis=1)
         taps = lax.dynamic_index_in_dim(taps_kept, c_send, axis=1, keepdims=False)
         chunk = convolve_class(rows, taps, class_counts[c_send], t_in)
         perm = []
@@ -156,7 +161,7 @@
         b_src = u_dst % nf
         if q == 1:
             gate = lax.dynamic_slice_in_dim(flag_mask, b_src * f_blk, f_blk, axis=1)
-            cols = lax.dynamic_slice_in_dim(panel, b_src * f_blk, f_blk, axis=1)
+            cols = lax.slice_in_dim(panel, (nf - 1 - r) * f_blk, (nf - r) * f_blk, axis=1)
         else:
             gate = lax.dynamic_slice(flag_mask, (t_sub * t_in, b_src * f_blk), (t_in, f_blk))
             cols = lax.dynamic_slice_in_dim(panel, b_src * f_blk, f_blk, axis=1)

time: 134 us -> 140 us (1.045)
  other arithmetic: 35.6 us -> 43.1 us
    concatenate x0 -> x1, other arithmetic: none -> 4.16 us  [shards(): panel = jnp.concatenate([panel, panel], axis=1)]
    another operation x9, other arithmetic: 18.4 us -> 21.8 us
    unnamed x79 -> x73, local copies, waits for them, and re-layouts: 2.82 us -> 2.82 us
  transfers between devices with their start and end apart: 8 -> 8, of which waited for: 3 -> 3; matrix products, arithmetic and copies ran while one was open for 32% -> 31% of each run, Pallas kernels for 0% -> 0%
where the time goes in v10:
time: 140 us; the launch traced here: 139 us
  waiting for transfers between devices  43.4 us (31%)
  other arithmetic  43.1 us (31%)
  matrix products  16.5 us (12%)
  starting transfers between devices  15.4 us (11%)
  local copies, waits for them, and re-layouts  11.8 us (8%)
  between operations  8.46 us (6%)
    ppermute x4, waiting for transfers between devices, shards(): got = lax.ppermute(chunk, ('tm', 'freq'), perm)  43.4 us
    another operation x9, other arithmetic  21.8 us
    dot_general x4, matrix products, shards(): jnp.einsum('rstj,ij->rsti', weighted, cols, preferred_element_type=jnp.fl...  16.5 us
    ppermute x4, starting transfers between devices, shards(): got = lax.ppermute(chunk, ('tm', 'freq'), perm)  8.95 us
    dynamic_update_slice x4, local copies, waits for them, and re-layouts, shards(): lax.dynamic_update_slice_in_dim(slotted, got, b_src * f_blk, axis=3)  5.2 us
    concatenate x1, other arithmetic, shards(): panel = jnp.concatenate([panel, panel], axis=1)  4.16 us
    another operation x4, other arithmetic, convolve(): return jnp.stack([real_part, imag_part]).astype(jnp.bfloat16)  4.01 us
    ppermute x1, starting transfers between devices, extended(): lax.ppermute(tail, axis, [(i, (i + 1) % count) for i in range(ends)])  3.48 us
  transfers between devices with their start and end apart: 8, of which 3 were waited for; matrix products, arithmetic and copies ran while one was open for 31% of the time, Pallas kernels for 0%

profile of v10, /device:TPU:14, one launch (start us, length us, event | category | flops | bytes accessed | tf_op | source)
XLA Modules:
  0.0 138.8 jit_solution(2121271731045919508)
XLA Ops:
  0.0 1.7 %fusion.163 = (bf16[2,66,4,384]{3,2,1,0:T(4,128)(2,1)S(1)}, bf16[2,66,4,384]{3,2,1,0:T(4,128)(2,1)S(1)}) fusion(bf16[2,66,16,384]{3,2,1,0:T(8,128)(2,1)} %param.11), kind=kLoop, calls=%fused_computation.428 | loop fusion | bytes 1622016 | tf_op jit(solution)/shard_map/slice | solution.py:18
  1.7 3.5 %collective-permute-start = (bf16[2,66,4,384]{3,2,1,0:T(4,128)(2,1)S(1)}, bf16[2,66,4,384]{3,2,1,0:T(4,128)(2,1)S(1)}, u32[]{:S(2)}, u32[]{:S(2)}) collective-permute-start(bf16[2,66,4,384]{3,2,1,0:T(4,128)(2,1)S(1)} %get-tuple-element.54), channel_id=1, source_target_pairs={{0,4},{4,8},{8,12},{1,5},{5,9},{9,13},{2,6},{6,10},{10,14},{3,7},{... | collective-permute-start | bytes 1216520 | tf_op jit(solution)/shard_map/ppermute | solution.py:21
  5.2 2.4 %collective-permute-start.1 = (bf16[2,66,4,384]{3,2,1,0:T(4,128)(2,1)S(1)}, bf16[2,66,4,384]{3,2,1,0:T(4,128)(2,1)S(1)}, u32[]{:S(2)}, u32[]{:S(2)}) collective-permute-start(bf16[2,66,4,384]{3,2,1,0:T(4,128)(2,1)S(1)} %get-tuple-element.55), channel_id=1, source_target_pairs={{4,0},{8,4},{12,8},{5,1},{9,5},{13,9},{6,2},{10,6},{14,10},{7,3},{... | collective-permute-start | bytes 1216520 | tf_op jit(solution)/shard_map/ppermute | solution.py:23
  7.6 0.6 collective-permute-start.6
  8.2 0.8 reduce-window.9
  9.0 0.7 bitcast_subtract_fusion
  9.7 1.5 %fusion.164 = (s32[1]{0:T(128)}, s32[1]{0:T(128)}, s32[1]{0:T(128)}, s32[1]{0:T(128)}, s32[1]{0:T(128)}, /*index=5*/s32[1]{0:T(128)}, s32[1]{0:T(128)}, s32[1]{0:T(128)}) fusion(s32[4]{0:T(128)S(1)} %bitcast_subtract_fusion, s32[]{:T(128)S(6)} %select_n.128, s32[]{:T(128)S(6)} %select_n.122, s32[]{:T(128)S(6)} %select_n.116, s32[]{:T(128)S(6)} %select_n.110, ...), kind=kLoop, calls=%fused_computation.429 | loop fusion | bytes 80 | tf_op jit(solution)/shard_map/dynamic_slice | solution.py:148
  16.2 0.7 compare_convert_fusion.4
  16.9 0.7 broadcast_multiply_fusion.4
  17.6 0.6 compare_convert_fusion.1
  18.2 0.7 compare_convert_fusion.3
  18.9 0.7 compare_convert_fusion.2
  19.6 0.6 compare_convert_fusion
  23.2 2.9 %fusion.5 = bf16[2,98,24,384]{3,2,1,0:T(8,128)(2,1)S(1)} fusion(bf16[2,66,4,384]{3,2,1,0:T(4,128)(2,1)S(1)} %collective-permute-done.1, bf16[2,66,16,384]{3,2,1,0:T(8,128)(2,1)} %param.11, bf16[2,66,4,384]{3,2,1,0:T(4,128)(2,1)S(1)} %collective-permute-done), kind=kLoop, calls=%fused_computation.21 | loop fusion | flops 18063360 | bytes 6045696 | tf_op jit(solution)/shard_map/concatenate | solution.py:19
  26.0 2.6 %fusion.158 = bf16[1,32,16,384]{3,2,1,0:T(8,128)(2,1)S(1)} fusion(f32[32]{0:T(128)S(1)} %get-tuple-element.97, f32[32]{0:T(128)S(1)} %get-tuple-element.98, f32[32]{0:T(128)S(1)} %get-tuple-element.99, f32[32]{0:T(128)S(1)} %get-tuple-element.100, f32[32]{0:T(128)S(1)} %get-tuple-element.101, f32[32]{0:T(128)S(1)} %get-tuple-element.102, ...), kind=kLoop, calls=%fused_computation.327 | loop fusion | flops 10616832 | bytes 7473444 | tf_op jit(solution)/shard_map/convert.6
  28.7 2.6 %fusion.157 = bf16[1,32,16,384]{3,2,1,0:T(8,128)(2,1)S(1)} fusion(f32[32]{0:T(128)S(1)} %get-tuple-element.97, f32[32]{0:T(128)S(1)} %get-tuple-element.98, f32[32]{0:T(128)S(1)} %get-tuple-element.99, f32[32]{0:T(128)S(1)} %get-tuple-element.100, f32[32]{0:T(128)S(1)} %get-tuple-element.101, f32[32]{0:T(128)S(1)} %get-tuple-element.102, ...), kind=kLoop, calls=%fused_computation.326 | loop fusion | flops 10616832 | bytes 7473444 | tf_op jit(solution)/shard_map/convert.7
  31.3 1.0 pad_maximum_fusion.5
  32.3 2.1 %collective-permute-start.2 = (bf16[2,32,16,384]{3,2,1,0:T(8,128)(2,1)}, bf16[2,32,16,384]{3,2,1,0:T(8,128)(2,1)}, u32[]{:S(2)}, u32[]{:S(2)}) collective-permute-start(bf16[2,32,16,384]{3,2,1,0:T(8,128)(2,1)} %pad_maximum_fusion.5), channel_id=1, source_target_pairs={{0,4},{1,8},{2,12},{3,0},{4,5},{5,9},{6,13},{7,1},{8,6},{9,10},{10... | collective-permute-start | bytes 2359304 | tf_op jit(solution)/shard_map/ppermute | solution.py:158
  34.4 2.6 %fusion.151 = bf16[1,32,16,384]{3,2,1,0:T(8,128)(2,1)S(1)} fusion(f32[32]{0:T(128)S(1)} %get-tuple-element.61, f32[32]{0:T(128)S(1)} %get-tuple-element.62, f32[32]{0:T(128)S(1)} %get-tuple-element.63, f32[32]{0:T(128)S(1)} %get-tuple-element.64, f32[32]{0:T(128)S(1)} %get-tuple-element.65, f32[32]{0:T(128)S(1)} %get-tuple-element.66, ...), kind=kLoop, calls=%fused_computation.320 | loop fusion | flops 10616832 | bytes 7473444 | tf_op jit(solution)/shard_map/convert.1
  37.0 2.6 %fusion.152 = bf16[1,32,16,384]{3,2,1,0:T(8,128)(2,1)S(1)} fusion(f32[32]{0:T(128)S(1)} %get-tuple-element.61, f32[32]{0:T(128)S(1)} %get-tuple-element.62, f32[32]{0:T(128)S(1)} %get-tuple-element.63, f32[32]{0:T(128)S(1)} %get-tuple-element.64, f32[32]{0:T(128)S(1)} %get-tuple-element.65, f32[32]{0:T(128)S(1)} %get-tuple-element.66, ...), kind=kLoop, calls=%fused_computation.321 | loop fusion | flops 10616832 | bytes 7473444 | tf_op jit(solution)/shard_map/convert
  39.8 2.6 %fusion.156 = bf16[1,32,16,384]{3,2,1,0:T(8,128)(2,1)S(1)} fusion(f32[32]{0:T(128)S(1)} %get-tuple-element.79, f32[32]{0:T(128)S(1)} %get-tuple-element.80, f32[32]{0:T(128)S(1)} %get-tuple-element.81, f32[32]{0:T(128)S(1)} %get-tuple-element.82, f32[32]{0:T(128)S(1)} %get-tuple-element.83, f32[32]{0:T(128)S(1)} %get-tuple-element.84, ...), kind=kLoop, calls=%fused_computation.325 | loop fusion | flops 10616832 | bytes 7473444 | tf_op jit(solution)/shard_map/convert.4
  42.6 1.0 copy-done.1
  43.6 1.6 %pad_maximum_fusion.4 = bf16[2,384,1536]{2,1,0:T(8,128)(2,1)} fusion(bf16[1,384,1536]{2,1,0:T(8,128)(2,1)S(1)} %collective-permute-done.6, bf16[1,384,1536]{2,1,0:T(8,128)(2,1)S(1)} %copy-done), kind=kLoop, calls=%fused_computation.23 | loop fusion | flops 1179648 | bytes 4718592 | tf_op jit(solution)/shard_map/concatenate | solution.py:123
  45.4 2.6 %fusion.155 = bf16[1,32,16,384]{3,2,1,0:T(8,128)(2,1)S(1)} fusion(f32[32]{0:T(128)S(1)} %get-tuple-element.79, f32[32]{0:T(128)S(1)} %get-tuple-element.80, f32[32]{0:T(128)S(1)} %get-tuple-element.81, f32[32]{0:T(128)S(1)} %copy-done.9, f32[32]{0:T(128)S(1)} %copy-done.11, f32[32]{0:T(128)S(1)} %copy-done.13, f32[32]{0:T(128)S(1)} %copy-done.15, ...), kind=kLoop, calls=%fused_computation.324 | loop fusion | flops 10616832 | bytes 7473444 | tf_op jit(solution)/shard_map/convert.5
  48.0 2.6 %fusion.154 = bf16[1,32,16,384]{3,2,1,0:T(8,128)(2,1)S(1)} fusion(f32[32]{0:T(128)S(1)} %get-tuple-element.115, f32[32]{0:T(128)S(1)} %get-tuple-element.116, f32[32]{0:T(128)S(1)} %get-tuple-element.117, f32[32]{0:T(128)S(1)} %get-tuple-element.118, f32[32]{0:T(128)S(1)} %get-tuple-element.119, f32[32]{0:T(128)S(1)} %get-tuple-element.120, ...), kind=kLoop, calls=%fused_computation.323 | loop fusion | flops 10616832 | bytes 7473444 | tf_op jit(solution)/shard_map/convert.2
  50.6 2.6 %fusion.153 = bf16[1,32,16,384]{3,2,1,0:T(8,128)(2,1)S(1)} fusion(f32[32]{0:T(128)S(1)} %get-tuple-element.115, f32[32]{0:T(128)S(1)} %get-tuple-element.116, f32[32]{0:T(128)S(1)} %get-tuple-element.117, f32[32]{0:T(128)S(1)} %get-tuple-element.118, f32[32]{0:T(128)S(1)} %get-tuple-element.119, f32[32]{0:T(128)S(1)} %get-tuple-element.120, ...), kind=kLoop, calls=%fused_computation.322 | loop fusion | flops 10616832 | bytes 7473444 | tf_op jit(solution)/shard_map/convert.3
  53.2 1.1 pad_maximum_fusion.6
  54.3 1.5 %collective-permute-start.3 = (bf16[2,32,16,384]{3,2,1,0:T(8,128)(2,1)}, bf16[2,32,16,384]{3,2,1,0:T(8,128)(2,1)}, u32[]{:S(2)}, u32[]{:S(2)}) collective-permute-start(bf16[2,32,16,384]{3,2,1,0:T(8,128)(2,1)} %pad_maximum_fusion.6), channel_id=1, source_target_pairs={{0,8},{1,12},{2,0},{3,4},{4,9},{5,13},{6,1},{7,5},{8,10},{9,14},{1... | collective-permute-start | bytes 2359304 | tf_op jit(solution)/shard_map/ppermute | solution.py:158
  55.9 1.0 pad_maximum_fusion.7
  57.1 1.0 pad_maximum_fusion.8
  58.1 5.0 %collective-permute-start.5 = (bf16[2,32,16,384]{3,2,1,0:T(8,128)(2,1)}, bf16[2,32,16,384]{3,2,1,0:T(8,128)(2,1)}, u32[]{:S(2)}, u32[]{:S(2)}) collective-permute-start(bf16[2,32,16,384]{3,2,1,0:T(8,128)(2,1)} %pad_maximum_fusion.8), channel_id=1, source_target_pairs={{0,0},{1,4},{2,8},{3,12},{4,1},{5,5},{6,9},{7,13},{8,2},{9,6},{10,... | collective-permute-start | bytes 2359304 | tf_op jit(solution)/shard_map/ppermute | solution.py:158
  63.3 1.4 %dynamic-slice_convert_fusion = (bf16[16,384]{1,0:T(8,128)(2,1)}, bf16[16,384]{1,0:T(8,128)(2,1)}, bf16[16,384]{1,0:T(8,128)(2,1)S(1)}, bf16[16,384]{1,0:T(8,128)(2,1)}) fusion(s32[16,1536]{1,0:T(8,128)} %param.15, s32[]{:T(128)S(6)} %select_n.132, s32[]{:T(128)S(6)} %select_n.120, s32[]{:T(128)S(6)} %select_n.114, s32[]{:T(128)S(6)} %select_n.126), kind=kLoop, calls=%fused_computation.332 | loop fusion | flops 24576 | bytes 147472 | tf_op jit(solution)/shard_map/convert_element_type | solution.py:168
  64.7 0.4 broadcast_in_dim.4
  65.1 1.3 constant_dynamic-update-slice_fusion.3
  66.4 32.2 %collective-permute-done.3 = bf16[2,32,16,384]{3,2,1,0:T(8,128)(2,1)} collective-permute-done((bf16[2,32,16,384]{3,2,1,0:T(8,128)(2,1)}, bf16[2,32,16,384]{3,2,1,0:T(8,128)(2,1)}, u32[]{:S(2)}, u32[]{:S(2)}) %collective-permute-start.3) | collective-permute-done | bytes 786464 | tf_op jit(solution)/shard_map/ppermute | solution.py:158
  98.6 1.3 constant_dynamic-update-slice_fusion.2
  99.9 8.2 %collective-permute-done.4 = bf16[2,32,16,384]{3,2,1,0:T(8,128)(2,1)} collective-permute-done((bf16[2,32,16,384]{3,2,1,0:T(8,128)(2,1)}, bf16[2,32,16,384]{3,2,1,0:T(8,128)(2,1)}, u32[]{:S(2)}, u32[]{:S(2)}) %collective-permute-start.4) | collective-permute-done | bytes 786464 | tf_op jit(solution)/shard_map/ppermute | solution.py:158
  108.2 1.3 constant_dynamic-update-slice_fusion.1
  109.5 2.9 %collective-permute-done.5 = bf16[2,32,16,384]{3,2,1,0:T(8,128)(2,1)} collective-permute-done((bf16[2,32,16,384]{3,2,1,0:T(8,128)(2,1)}, bf16[2,32,16,384]{3,2,1,0:T(8,128)(2,1)}, u32[]{:S(2)}, u32[]{:S(2)}) %collective-permute-start.5) | collective-permute-done | bytes 786464 | tf_op jit(solution)/shard_map/ppermute | solution.py:158
  112.4 1.3 constant_dynamic-update-slice_fusion
  113.8 1.6 %copy-done.4 = bf16[2,32,16,1536]{3,2,1,0:T(8,128)(2,1)} copy-done((bf16[2,32,16,1536]{3,2,1,0:T(8,128)(2,1)}, bf16[2,32,16,1536]{3,2,1,0:T(8,128)(2,1)S(1)}, u32[]{:S(2)}) %copy-start.4) | copy-done | bytes 3145752
  115.4 2.6 %conditional.1 = (bf16[1536,1536]{1,0:T(8,128)(2,1)}) conditional(s32[]{:T(128)} %clamp.3, (bf16[1,384,1536]{2,1,0:T(8,128)(2,1)S(1)}, bf16[2,384,1536]{2,1,0:T(8,128)(2,1)S(1)}, bf16[1,384,1536]{2,1,0:T(8,128)(2,1)S(1)}) %tuple.118, (bf16[2,384,1536]{2,1,0:T(8,128)(2,1)S(1)}, bf16[1,384,1536]{2,1,0:T(8,128)(2,1)S(1)}, ...), branch_computations={%region_1.2_spmd, %region_2.3_spmd, %region_3.4_spmd, %region_4.5_... | conditional | flops 18874368 | bytes 14155784 | solution.py:135
  115.6 2.4 %pad_maximum_fusion.2 = bf16[1536,1536]{1,0:T(8,128)(2,1)} fusion(bf16[384,1536]{1,0:T(8,128)(2,1)S(1)} %get-tuple-element.51, bf16[384,1536]{1,0:T(8,128)(2,1)S(1)} %bitcast.214, bf16[384,1536]{1,0:T(8,128)(2,1)S(1)} %get-tuple-element.50, bf16[384,1536]{1,0:T(8,128)(2,1)S(1)} %bitcast.218), kind=kLoop, calls=%fused_computation.6 | loop fusion | flops 18874368 | bytes 9437184 | tf_op jit(solution)/shard_map/cond/branch_2_fun/concatenate | solution.py:31
  118.0 4.2 %fusion.3 = bf16[1536,1536]{1,0:T(8,128)(2,1)S(1)} fusion(s32[]{:T(128)S(6)} %select_n.134, bf16[1536,1536]{1,0:T(8,128)(2,1)} %get-tuple-element.148), kind=kLoop, calls=%fused_computation.19 | loop fusion | flops 9437184 | bytes 9437188 | tf_op jit(solution)/shard_map/concatenate | solution.py:140
  122.2 3.6 %fusion.8 = f32[2,32,16,1536]{3,2,1,0:T(8,128)S(1)} fusion(bf16[1536,1536]{1,0:T(8,128)(2,1)S(1)} %fusion.3, bf16[2,32,16,384]{3,2,1,0:T(8,128)(2,1)} %collective-permute-done.4, bf16[16,384]{1,0:T(8,128)(2,1)S(1)} %copy-done.6), kind=kOutput, calls=%fused_computation.27 | convolution fusion | flops 1208352768 | bytes 8269824 | tf_op jit(solution)/shard_map/rstj,ij->rsti/dot_general | solution.py:169
  125.8 3.0 %fusion.9 = f32[2,32,16,1536]{3,2,1,0:T(8,128)S(1)} fusion(bf16[1536,1536]{1,0:T(8,128)(2,1)S(1)} %fusion.3, bf16[2,32,16,384]{3,2,1,0:T(8,128)(2,1)} %collective-permute-done.3, bf16[16,384]{1,0:T(8,128)(2,1)S(1)} %copy-done.5), kind=kOutput, calls=%fused_computation.29 | convolution fusion | flops 1208352768 | bytes 8269824 | tf_op jit(solution)/shard_map/rstj,ij->rsti/dot_general | solution.py:169
  128.8 3.3 %fusion.10 = f32[2,32,16,1536]{3,2,1,0:T(8,128)S(1)} fusion(bf16[1536,1536]{1,0:T(8,128)(2,1)} %copy-done.3, bf16[2,32,16,384]{3,2,1,0:T(8,128)(2,1)} %collective-permute-done.2, bf16[16,384]{1,0:T(8,128)(2,1)S(1)} %get-tuple-element.58), kind=kOutput, calls=%fused_computation.31 | convolution fusion | flops 1208352768 | bytes 8269824 | tf_op jit(solution)/shard_map/rstj,ij->rsti/dot_general | solution.py:169
  132.1 6.7 %fusion.6 = bf16[2,1,32,16,1536]{4,3,2,1,0:T(8,128)(2,1)} fusion(f32[2,32,16,1536]{3,2,1,0:T(8,128)S(1)} %fusion.8, f32[2,32,16,1536]{3,2,1,0:T(8,128)S(1)} %fusion.10, f32[2,32,16,1536]{3,2,1,0:T(8,128)S(1)} %fusion.9, bf16[2,32,16,1536]{3,2,1,0:T(8,128)(2,1)} %copy-done.4, bf16[1536,1536]{1,0:T(8,128)(2,1)} %copy-done.3, ...), kind=kOutput, calls=%fused_computation.22 | convolution fusion | flops 1217789952 | bytes 27144192 | tf_op jit(solution)/shard_map/rstj,ij->rsti/dot_general | solution.py:169
  (89 shorter events, 0.9 us)
Async XLA Ops:
  1.7 21.4 %collective-permute-start = (bf16[2,66,4,384]{3,2,1,0:T(4,128)(2,1)S(1)}, bf16[2,66,4,384]{3,2,1,0:T(4,128)(2,1)S(1)}, u32[]{:S(2)}, u32[]{:S(2)}) collective-permute-start(bf16[2,66,4,384]{3,2,1,0:T(4,128)(2,1)S(1)} %get-tuple-element.54), channel_id=1, source_target_pairs={{0,4},{4,8},{8,12},{1,5},{5,9},{9,13},{2,6},{6,10},{10,14},{3,7},{... | collective-permute-start | bytes 1216520 | tf_op jit(solution)/shard_map/ppermute | solution.py:21
  5.2 18.0 %collective-permute-start.1 = (bf16[2,66,4,384]{3,2,1,0:T(4,128)(2,1)S(1)}, bf16[2,66,4,384]{3,2,1,0:T(4,128)(2,1)S(1)}, u32[]{:S(2)}, u32[]{:S(2)}) collective-permute-start(bf16[2,66,4,384]{3,2,1,0:T(4,128)(2,1)S(1)} %get-tuple-element.55), channel_id=1, source_target_pairs={{4,0},{8,4},{12,8},{5,1},{9,5},{13,9},{6,2},{10,6},{14,10},{7,3},{... | collective-permute-start | bytes 1216520 | tf_op jit(solution)/shard_map/ppermute | solution.py:23
  7.6 35.0 %collective-permute-start.6 = (bf16[1,384,1536]{2,1,0:T(8,128)(2,1)}, bf16[1,384,1536]{2,1,0:T(8,128)(2,1)S(1)}, u32[]{:S(2)}, u32[]{:S(2)}) collective-permute-start(bf16[1,384,1536]{2,1,0:T(8,128)(2,1)} %param.16), channel_id=1, source_target_pairs={{0,2},{1,3},{2,0},{3,1},{4,6},{5,7},{6,4},{7,5},{8,10},{9,11},{10,... | collective-permute-start | bytes 3538952 | tf_op jit(solution)/shard_map/ppermute | solution.py:123
  20.3 19.3 %copy-start.8 = (f32[32]{0:T(128)}, f32[32]{0:T(128)S(1)}, u32[]{:S(2)}) copy-start(f32[32]{0:T(128)S(1)} %get-tuple-element.82) | copy-start | bytes 388
  20.3 19.3 %copy-start.10 = (f32[32]{0:T(128)}, f32[32]{0:T(128)S(1)}, u32[]{:S(2)}) copy-start(f32[32]{0:T(128)S(1)} %get-tuple-element.83) | copy-start | bytes 388
  20.3 19.3 %copy-start.12 = (f32[32]{0:T(128)}, f32[32]{0:T(128)S(1)}, u32[]{:S(2)}) copy-start(f32[32]{0:T(128)S(1)} %get-tuple-element.84) | copy-start | bytes 388
  20.4 19.3 %copy-start.14 = (f32[32]{0:T(128)}, f32[32]{0:T(128)S(1)}, u32[]{:S(2)}) copy-start(f32[32]{0:T(128)S(1)} %get-tuple-element.85) | copy-start | bytes 388
  20.4 19.3 %copy-start.16 = (f32[32]{0:T(128)}, f32[32]{0:T(128)S(1)}, u32[]{:S(2)}) copy-start(f32[32]{0:T(128)S(1)} %get-tuple-element.86) | copy-start | bytes 388
  20.4 19.3 %copy-start.18 = (f32[32]{0:T(128)}, f32[32]{0:T(128)S(1)}, u32[]{:S(2)}) copy-start(f32[32]{0:T(128)S(1)} %get-tuple-element.87) | copy-start | bytes 388
  20.4 19.3 %copy-start.20 = (f32[32]{0:T(128)}, f32[32]{0:T(128)S(1)}, u32[]{:S(2)}) copy-start(f32[32]{0:T(128)S(1)} %get-tuple-element.88) | copy-start | bytes 388
  20.4 19.3 %copy-start.22 = (f32[32]{0:T(128)}, f32[32]{0:T(128)S(1)}, u32[]{:S(2)}) copy-start(f32[32]{0:T(128)S(1)} %get-tuple-element.89) | copy-start | bytes 388
  20.4 19.3 %copy-start.24 = (f32[32]{0:T(128)}, f32[32]{0:T(128)S(1)}, u32[]{:S(2)}) copy-start(f32[32]{0:T(128)S(1)} %get-tuple-element.90) | copy-start | bytes 388
  20.4 19.3 %copy-start.26 = (f32[32]{0:T(128)}, f32[32]{0:T(128)S(1)}, u32[]{:S(2)}) copy-start(f32[32]{0:T(128)S(1)} %get-tuple-element.91) | copy-start | bytes 388
  20.4 19.3 %copy-start.28 = (f32[32]{0:T(128)}, f32[32]{0:T(128)S(1)}, u32[]{:S(2)}) copy-start(f32[32]{0:T(128)S(1)} %get-tuple-element.92) | copy-start | bytes 388
  20.4 19.3 %copy-start.30 = (f32[32]{0:T(128)}, f32[32]{0:T(128)S(1)}, u32[]{:S(2)}) copy-start(f32[32]{0:T(128)S(1)} %get-tuple-element.93) | copy-start | bytes 388
  20.4 19.3 %copy-start.32 = (f32[32]{0:T(128)}, f32[32]{0:T(128)S(1)}, u32[]{:S(2)}) copy-start(f32[32]{0:T(128)S(1)} %get-tuple-element.94) | copy-start | bytes 388
  20.5 19.3 %copy-start.34 = (f32[32]{0:T(128)}, f32[32]{0:T(128)S(1)}, u32[]{:S(2)}) copy-start(f32[32]{0:T(128)S(1)} %get-tuple-element.95) | copy-start | bytes 388
  32.3 32.4 %collective-permute-start.2 = (bf16[2,32,16,384]{3,2,1,0:T(8,128)(2,1)}, bf16[2,32,16,384]{3,2,1,0:T(8,128)(2,1)}, u32[]{:S(2)}, u32[]{:S(2)}) collective-permute-start(bf16[2,32,16,384]{3,2,1,0:T(8,128)(2,1)} %pad_maximum_fusion.5), channel_id=1, source_target_pairs={{0,4},{1,8},{2,12},{3,0},{4,5},{5,9},{6,13},{7,1},{8,6},{9,10},{10... | collective-permute-start | bytes 2359304 | tf_op jit(solution)/shard_map/ppermute | solution.py:158
  39.6 4.0 %copy-start = (bf16[1,384,1536]{2,1,0:T(8,128)(2,1)S(1)}, bf16[1,384,1536]{2,1,0:T(8,128)(2,1)}, u32[]{:S(2)}) copy-start(bf16[1,384,1536]{2,1,0:T(8,128)(2,1)} %param.16) | copy-start | bytes 3538948
  42.4 2.8 %copy-start.9 = (f32[32]{0:T(128)S(1)}, f32[32]{0:T(128)}, u32[]{:S(2)}) copy-start(f32[32]{0:T(128)} %copy-done.8) | copy-start | bytes 388
  42.4 2.8 %copy-start.11 = (f32[32]{0:T(128)S(1)}, f32[32]{0:T(128)}, u32[]{:S(2)}) copy-start(f32[32]{0:T(128)} %copy-done.10) | copy-start | bytes 388
  42.4 2.8 %copy-start.13 = (f32[32]{0:T(128)S(1)}, f32[32]{0:T(128)}, u32[]{:S(2)}) copy-start(f32[32]{0:T(128)} %copy-done.12) | copy-start | bytes 388
  42.5 2.8 %copy-start.15 = (f32[32]{0:T(128)S(1)}, f32[32]{0:T(128)}, u32[]{:S(2)}) copy-start(f32[32]{0:T(128)} %copy-done.14) | copy-start | bytes 388
  42.5 2.8 %copy-start.17 = (f32[32]{0:T(128)S(1)}, f32[32]{0:T(128)}, u32[]{:S(2)}) copy-start(f32[32]{0:T(128)} %copy-done.16) | copy-start | bytes 388
  42.5 2.8 %copy-start.19 = (f32[32]{0:T(128)S(1)}, f32[32]{0:T(128)}, u32[]{:S(2)}) copy-start(f32[32]{0:T(128)} %copy-done.18) | copy-start | bytes 388
  42.5 2.8 %copy-start.21 = (f32[32]{0:T(128)S(1)}, f32[32]{0:T(128)}, u32[]{:S(2)}) copy-start(f32[32]{0:T(128)} %copy-done.20) | copy-start | bytes 388
  42.5 2.8 %copy-start.23 = (f32[32]{0:T(128)S(1)}, f32[32]{0:T(128)}, u32[]{:S(2)}) copy-start(f32[32]{0:T(128)} %copy-done.22) | copy-start | bytes 388
  42.5 2.8 %copy-start.25 = (f32[32]{0:T(128)S(1)}, f32[32]{0:T(128)}, u32[]{:S(2)}) copy-start(f32[32]{0:T(128)} %copy-done.24) | copy-start | bytes 388
  42.5 2.8 %copy-start.27 = (f32[32]{0:T(128)S(1)}, f32[32]{0:T(128)}, u32[]{:S(2)}) copy-start(f32[32]{0:T(128)} %copy-done.26) | copy-start | bytes 388
  42.5 2.8 %copy-start.29 = (f32[32]{0:T(128)S(1)}, f32[32]{0:T(128)}, u32[]{:S(2)}) copy-start(f32[32]{0:T(128)} %copy-done.28) | copy-start | bytes 388
  42.5 2.8 %copy-start.31 = (f32[32]{0:T(128)S(1)}, f32[32]{0:T(128)}, u32[]{:S(2)}) copy-start(f32[32]{0:T(128)} %copy-done.30) | copy-start | bytes 388
  42.5 2.8 %copy-start.33 = (f32[32]{0:T(128)S(1)}, f32[32]{0:T(128)}, u32[]{:S(2)}) copy-start(f32[32]{0:T(128)} %copy-done.32) | copy-start | bytes 388
  42.6 2.8 %copy-start.35 = (f32[32]{0:T(128)S(1)}, f32[32]{0:T(128)}, u32[]{:S(2)}) copy-start(f32[32]{0:T(128)} %copy-done.34) | copy-start | bytes 388
  42.6 1.0 copy-start.1
  45.2 68.5 %collective-permute-start.7 = (bf16[2,384,1536]{2,1,0:T(8,128)(2,1)}, bf16[2,384,1536]{2,1,0:T(8,128)(2,1)S(1)}, u32[]{:S(2)}, u32[]{:S(2)}) collective-permute-start(bf16[2,384,1536]{2,1,0:T(8,128)(2,1)} %pad_maximum_fusion.4), channel_id=1, source_target_pairs={{0,1},{1,0},{2,3},{3,2},{4,5},{5,4},{6,7},{7,6},{8,9},{9,8},{10,11... | collective-permute-start | bytes 7077896 | tf_op jit(solution)/shard_map/ppermute | solution.py:123
  54.3 44.3 %collective-permute-start.3 = (bf16[2,32,16,384]{3,2,1,0:T(8,128)(2,1)}, bf16[2,32,16,384]{3,2,1,0:T(8,128)(2,1)}, u32[]{:S(2)}, u32[]{:S(2)}) collective-permute-start(bf16[2,32,16,384]{3,2,1,0:T(8,128)(2,1)} %pad_maximum_fusion.6), channel_id=1, source_target_pairs={{0,8},{1,12},{2,0},{3,4},{4,9},{5,13},{6,1},{7,5},{8,10},{9,14},{1... | collective-permute-start | bytes 2359304 | tf_op jit(solution)/shard_map/ppermute | solution.py:158
  56.8 51.4 %collective-permute-start.4 = (bf16[2,32,16,384]{3,2,1,0:T(8,128)(2,1)}, bf16[2,32,16,384]{3,2,1,0:T(8,128)(2,1)}, u32[]{:S(2)}, u32[]{:S(2)}) collective-permute-start(bf16[2,32,16,384]{3,2,1,0:T(8,128)(2,1)} %pad_maximum_fusion.7), channel_id=1, source_target_pairs={{0,12},{1,0},{2,4},{3,8},{4,13},{5,1},{6,5},{7,9},{8,14},{9,2},{10... | collective-permute-start | bytes 2359304 | tf_op jit(solution)/shard_map/ppermute | solution.py:158
  58.1 54.4 %collective-permute-start.5 = (bf16[2,32,16,384]{3,2,1,0:T(8,128)(2,1)}, bf16[2,32,16,384]{3,2,1,0:T(8,128)(2,1)}, u32[]{:S(2)}, u32[]{:S(2)}) collective-permute-start(bf16[2,32,16,384]{3,2,1,0:T(8,128)(2,1)} %pad_maximum_fusion.8), channel_id=1, source_target_pairs={{0,0},{1,4},{2,8},{3,12},{4,1},{5,5},{6,9},{7,13},{8,2},{9,6},{10,... | collective-permute-start | bytes 2359304 | tf_op jit(solution)/shard_map/ppermute | solution.py:158
  64.7 49.1 %copy-start.2 = (bf16[1,384,1536]{2,1,0:T(8,128)(2,1)S(1)}, bf16[1,384,1536]{2,1,0:T(8,128)(2,1)}, u32[]{:S(2)}) copy-start(bf16[1,384,1536]{2,1,0:T(8,128)(2,1)} %copy-done.1) | copy-start | bytes 3538948
  113.7 1.7 %copy-start.4 = (bf16[2,32,16,1536]{3,2,1,0:T(8,128)(2,1)}, bf16[2,32,16,1536]{3,2,1,0:T(8,128)(2,1)S(1)}, u32[]{:S(2)}) copy-start(bf16[2,32,16,1536]{3,2,1,0:T(8,128)(2,1)S(1)} %constant_dynamic-update-slice_fusion) | copy-start | bytes 9437188
  118.0 4.2 %copy-start.6 = (bf16[16,384]{1,0:T(8,128)(2,1)S(1)}, bf16[16,384]{1,0:T(8,128)(2,1)}, u32[]{:S(2)}) copy-start(bf16[16,384]{1,0:T(8,128)(2,1)} %get-tuple-element.59) | copy-start | bytes 36868
  122.2 6.6 %copy-start.3 = (bf16[1536,1536]{1,0:T(8,128)(2,1)}, bf16[1536,1536]{1,0:T(8,128)(2,1)S(1)}, u32[]{:S(2)}) copy-start(bf16[1536,1536]{1,0:T(8,128)(2,1)S(1)} %fusion.3) | copy-start | bytes 14155780
  122.2 3.6 %copy-start.5 = (bf16[16,384]{1,0:T(8,128)(2,1)S(1)}, bf16[16,384]{1,0:T(8,128)(2,1)}, u32[]{:S(2)}) copy-start(bf16[16,384]{1,0:T(8,128)(2,1)} %get-tuple-element.57) | copy-start | bytes 36868
  128.8 3.4 %copy-start.7 = (bf16[16,384]{1,0:T(8,128)(2,1)S(1)}, bf16[16,384]{1,0:T(8,128)(2,1)}, u32[]{:S(2)}) copy-start(bf16[16,384]{1,0:T(8,128)(2,1)} %get-tuple-element.56) | copy-start | bytes 36868
